TPU v7x, 1024 devices: a whole 4x8x16 slice. The times are simulated.
1024 devices in a mesh: col: 32 (over y, x), af: 32 (over z, core).
Axes of the slice: x: 4, y: 8, z: 16, core: 2. Of those that a mesh axis runs over, the one named last changes fastest.
Arguments:
- inputs: bfloat16 [2, 64, 64, 8, 256], P(None, 'col', 'af'), may hold values from -6 to 6
- first_filters: bfloat16 [3, 3, 3, 256, 256], P(None, None, None, 'af'), may hold values from -0.125 to 0.125
- second_filters: bfloat16 [3, 3, 3, 256, 256], P(None, None, None, 'af'), may hold values from -0.1875 to 0.1875
Outputs:
- features: bfloat16 [2, 32, 32, 4, 256], P(None, 'col', None, None, 'af')
All inputs are finite; a program needn't handle non-finite values.
Results may differ from a plain program's by a relative error of at most 0.011.
Values may be sent and summed in bfloat16 or wider, within the bound.
No kernel may reach another device: no remote copies, remote signals or barrier semaphores. Data moves between devices by JAX's collectives and lax.ppermute only.
A program may use at most 32 MiB of HBM per device.

v0:
```python
import jax
import jax.numpy as jnp
from jax import lax
from jax.sharding import PartitionSpec as P


def extended(block, sides, width):
    for axis, dim in sides:
        count = lax.axis_size(axis)
        forward = [(i, i + 1) for i in range(count - 1)]
        backward = [(target, source) for source, target in forward]
        low = lax.ppermute(
            lax.slice_in_dim(block, block.shape[dim] - width, None, axis=dim), axis, forward
        )
        high = lax.ppermute(lax.slice_in_dim(block, 0, width, axis=dim), axis, backward)
        block = jnp.concatenate([low, block, high], axis=dim)
    return block


def passed_along(array, axis, by):
    peers = lax.axis_size(axis)
    pairs = [(i, i + by) for i in range(peers) if 0 <= i + by < peers]
    return lax.ppermute(array, axis, pairs)


def convolve(volume, kernel, stride, row_pad):
    return lax.conv_general_dilated(
        volume,
        kernel,
        (stride, stride, stride),
        ((0, 0), (row_pad, row_pad), (1, 1)),
        dimension_numbers=("NDHWC", "DHWIO", "NDHWC"),
        preferred_element_type=jnp.float32,
    )


def per_device(inputs, first_filters, second_filters):
    padded = extended(inputs, (("col", 1),), 1)
    gathered = lax.all_gather(padded, "af", axis=2, tiled=True)
    own_first = lax.all_to_all(first_filters, "af", split_axis=4, concat_axis=3, tiled=True)
    hidden = jnp.maximum(convolve(gathered, own_first, 1, 1), 0.0).astype(jnp.bfloat16)
    lower_plane = passed_along(hidden[:, -1:], "col", 1)
    stacked = jnp.concatenate([lower_plane, hidden], axis=1)
    all_channels = lax.all_gather(stacked, "af", axis=4, tiled=True)
    own_second = lax.all_to_all(second_filters, "af", split_axis=4, concat_axis=3, tiled=True)
    totals = convolve(all_channels, own_second, 2, 1)
    return jnp.maximum(totals, 0.0).astype(jnp.bfloat16)


def solution(mesh):
    placed = (
        P(None, "col", "af", None, None),
        P(None, None, None, "af", None),
        P(None, None, None, "af", None),
    )
    return jax.shard_map(
        per_device,
        mesh=mesh,
        in_specs=placed,
        out_specs=P(None, "col", None, None, "af"),
        check_vma=False,
    )
```

profile of v0, /device:TPU:9, one launch (start us, length us, event | category | flops | bytes accessed | tf_op | source)
XLA Modules:
  0.0 221.9 jit_solution(7977454261339179861)
XLA Ops:
  7.4 3.1 %collective-permute-start = (bf16[2,1,2,8,256]{4,0,3,2,1:T(2,128)(2,1)S(1)}, bf16[2,1,2,8,256]{4,0,3,2,1:T(2,128)(2,1)S(1)}, u32[]{:S(2)}, u32[]{:S(2)}) collective-permute-start(bf16[2,1,2,8,256]{4,0,3,2,1:T(2,128)(2,1)S(1)} %get-tuple-element.5), channel_id=1, source_target_pairs={{0,32},{32,64},{64,96},{96,128},{128,160},{160,192},{192,224},{224... | collective-permute-start | bytes 49160 | tf_op jit(solution)/shard_map/ppermute | solution.py:12
  10.5 4.3 %collective-permute-start.1 = (bf16[2,1,2,8,256]{4,0,3,2,1:T(2,128)(2,1)S(1)}, bf16[2,1,2,8,256]{4,0,3,2,1:T(2,128)(2,1)S(1)}, u32[]{:S(2)}, u32[]{:S(2)}) collective-permute-start(bf16[2,1,2,8,256]{4,0,3,2,1:T(2,128)(2,1)S(1)} %get-tuple-element.6), channel_id=1, source_target_pairs={{32,0},{64,32},{96,64},{128,96},{160,128},{192,160},{224,192},{256... | collective-permute-start | bytes 49160 | tf_op jit(solution)/shard_map/ppermute | solution.py:15
  14.8 0.8 collective-permute-done.1
  16.4 3.3 %copy.45 = bf16[3,3,3,8,256]{3,2,1,0,4:T(4,128)(2,1)S(1)} copy(bf16[3,3,3,8,256]{4,3,2,1,0:T(8,128)(2,1)} %param.4) | data formatting | bytes 221184 | tf_op args[1]
  19.8 1.7 reshape
  21.5 35.7 %all_to_all.36 = bf16[32,2,864]{2,1,0:T(2,128)(2,1)S(1)} all-to-all(bf16[32,2,864]{2,1,0:T(2,128)(2,1)S(1)} %reshape), channel_id=1, replica_groups=mesh['col'=32,'af'=32] {'af'}, dimensions={0} | all-to-all | bytes 221184 | tf_op jit(solution)/shard_map/all_to_all | solution.py:40
  57.2 1.6 reshape.1
  58.8 2.0 copy.61
  60.9 3.5 %all_to_all.29 = bf16[3,3,3,256,8]{3,4,2,1,0:T(8,128)(2,1)S(1)} reshape(bf16[3,3,3,32,8,8]{4,3,5,2,1,0:T(8,128)(2,1)} %bitcast.30) | data formatting | bytes 221184 | tf_op jit(solution)/shard_map/all_to_all | solution.py:40
  64.3 38.4 %all-gather.3.cloned.1.call-done = bf16[2,4,64,8,256]{4,0,3,2,1:T(2,128)(2,1)} async-done(((bf16[2,4,2,8,256]{4,0,3,2,1:T(2,128)(2,1)}), bf16[2,4,64,8,256]{4,0,3,2,1:T(2,128)(2,1)}) %all-gather.3.cloned.1.call-update) | async-done | bytes 2097168 | tf_op jit(solution)/shard_map/all_gather | solution.py:39
  102.7 13.9 %fusion = bf16[2,2,64,8,8]{4,0,3,2,1:T(2,128)(2,1)S(1)} fusion(bf16[2,4,64,8,256]{4,0,3,2,1:T(2,128)(2,1)} %all-gather.3.cloned.1.call-done, bf16[3,3,3,256,8]{3,4,2,1,0:T(8,128)(2,1)S(1)} %all_to_all.29), kind=kOutput, calls=%fused_computation.3 | convolution fusion | flops 205488128 | bytes 2240512 | tf_op jit(solution)/shard_map/conv_general_dilated | solution.py:27
  116.9 3.3 %collective-permute-start.2 = (bf16[2,1,64,8,8]{4,0,3,2,1:T(2,128)(2,1)S(1)}, bf16[2,1,64,8,8]{4,0,3,2,1:T(2,128)(2,1)S(1)}, u32[]{:S(2)}, u32[]{:S(2)}) collective-permute-start(bf16[2,1,64,8,8]{4,0,3,2,1:T(2,128)(2,1)S(1)} %slice.14), channel_id=1, source_target_pairs={{0,32},{32,64},{64,96},{96,128},{128,160},{160,192},{192,224},{224... | collective-permute-start | bytes 49160 | tf_op jit(solution)/shard_map/ppermute | solution.py:23
  120.1 8.3 %collective-permute-done.2 = bf16[2,1,64,8,8]{4,0,3,2,1:T(2,128)(2,1)S(1)} collective-permute-done((bf16[2,1,64,8,8]{4,0,3,2,1:T(2,128)(2,1)S(1)}, bf16[2,1,64,8,8]{4,0,3,2,1:T(2,128)(2,1)S(1)}, u32[]{:S(2)}, u32[]{:S(2)}) %collective-permute-start.2) | collective-permute-done | bytes 16416 | tf_op jit(solution)/shard_map/ppermute | solution.py:23
  128.4 1.2 pad_maximum_fusion
  129.7 1.8 copy.48
  131.5 1.8 copy.49
  133.3 1.8 reshape.2
  135.1 24.0 %all_to_all.37 = bf16[32,2,864]{2,1,0:T(2,128)(2,1)S(1)} all-to-all(bf16[32,2,864]{2,1,0:T(2,128)(2,1)S(1)} %reshape.2), channel_id=1, replica_groups=mesh['col'=32,'af'=32] {'af'}, dimensions={0} | all-to-all | bytes 221184 | tf_op jit(solution)/shard_map/all_to_all | solution.py:45
  159.1 1.6 reshape.3
  160.7 2.1 copy.60
  162.8 3.5 %all_to_all.33 = bf16[3,3,3,256,8]{3,4,2,1,0:T(8,128)(2,1)S(1)} reshape(bf16[3,3,3,32,8,8]{4,3,5,2,1,0:T(8,128)(2,1)} %bitcast.31) | data formatting | bytes 221184 | tf_op jit(solution)/shard_map/all_to_all | solution.py:45
  166.2 39.0 %all-gather.5.cloned.1.call-done = bf16[2,3,64,8,256]{2,3,1,0,4:T(8,128)(2,1)} async-done(((bf16[2,3,64,8,8]{2,3,1,0,4:T(8,128)(2,1)}), bf16[2,3,64,8,256]{2,3,1,0,4:T(8,128)(2,1)}) %all-gather.5.cloned.1.call-update) | async-done | bytes 1572880 | tf_op jit(solution)/shard_map/all_gather | solution.py:44
  205.2 6.2 %copy.52 = bf16[2,3,64,8,256]{4,0,3,2,1:T(2,128)(2,1)S(1)} copy(bf16[2,3,64,8,256]{2,3,1,0,4:T(8,128)(2,1)} %all-gather.5.cloned.1.call-done) | data formatting | bytes 3145728 | tf_op jit(solution)/shard_map/all_gather | solution.py:44
  211.4 2.9 %fusion.2 = bf16[2,1,32,4,8]{4,0,3,2,1:T(2,128)(2,1)S(1)} fusion(bf16[2,3,64,8,256]{4,0,3,2,1:T(2,128)(2,1)S(1)} %copy.52, bf16[3,3,3,256,8]{3,4,2,1,0:T(8,128)(2,1)S(1)} %all_to_all.33), kind=kOutput, calls=%fused_computation.8 | convolution fusion | flops 25681920 | bytes 1687552 | tf_op jit(solution)/shard_map/conv_general_dilated | solution.py:27
  (13 shorter events, 2.5 us)
Async XLA Ops:
  6.5 96.2 %all-gather.3.cloned.1.call-start = ((), (), s32[]{:S(2)}) async-start(), calls=%async_computation.2 | async-start | bytes 2162688 | tf_op jit(solution)/shard_map/all_gather | solution.py:39
  7.4 7.4 %collective-permute-start = (bf16[2,1,2,8,256]{4,0,3,2,1:T(2,128)(2,1)S(1)}, bf16[2,1,2,8,256]{4,0,3,2,1:T(2,128)(2,1)S(1)}, u32[]{:S(2)}, u32[]{:S(2)}) collective-permute-start(bf16[2,1,2,8,256]{4,0,3,2,1:T(2,128)(2,1)S(1)} %get-tuple-element.5), channel_id=1, source_target_pairs={{0,32},{32,64},{64,96},{96,128},{128,160},{160,192},{192,224},{224... | collective-permute-start | bytes 49160 | tf_op jit(solution)/shard_map/ppermute | solution.py:12
  10.5 5.1 %collective-permute-start.1 = (bf16[2,1,2,8,256]{4,0,3,2,1:T(2,128)(2,1)S(1)}, bf16[2,1,2,8,256]{4,0,3,2,1:T(2,128)(2,1)S(1)}, u32[]{:S(2)}, u32[]{:S(2)}) collective-permute-start(bf16[2,1,2,8,256]{4,0,3,2,1:T(2,128)(2,1)S(1)} %get-tuple-element.6), channel_id=1, source_target_pairs={{32,0},{64,32},{96,64},{128,96},{160,128},{192,160},{224,192},{256... | collective-permute-start | bytes 49160 | tf_op jit(solution)/shard_map/ppermute | solution.py:15
  16.4 188.8 %all-gather.5.cloned.1.call-start = ((), (), s32[]{:S(2)}) async-start(), calls=%async_computation.3 | async-start | bytes 3244032 | tf_op jit(solution)/shard_map/all_gather | solution.py:44
  116.6 14.8 %copy-start = (bf16[3,3,3,8,256]{4,3,2,1,0:T(8,128)(2,1)S(1)}, bf16[3,3,3,8,256]{4,3,2,1,0:T(8,128)(2,1)}, u32[]{:S(2)}) copy-start(bf16[3,3,3,8,256]{4,3,2,1,0:T(8,128)(2,1)} %param.5) | copy-start | bytes 331780
  116.9 11.6 %collective-permute-start.2 = (bf16[2,1,64,8,8]{4,0,3,2,1:T(2,128)(2,1)S(1)}, bf16[2,1,64,8,8]{4,0,3,2,1:T(2,128)(2,1)S(1)}, u32[]{:S(2)}, u32[]{:S(2)}) collective-permute-start(bf16[2,1,64,8,8]{4,0,3,2,1:T(2,128)(2,1)S(1)} %slice.14), channel_id=1, source_target_pairs={{0,32},{32,64},{64,96},{96,128},{128,160},{160,192},{192,224},{224... | collective-permute-start | bytes 49160 | tf_op jit(solution)/shard_map/ppermute | solution.py:23
Sparse Core Ops, SparseCore 0:
  16.5 86.1 all-gather.2
  131.6 73.5 all-gather.4
where the time goes:
time: 223 us; the launch traced here: 222 us
  waiting for transfers between devices  86.5 us (39%)
  blocking collectives  59.7 us (27%)
  local copies, waits for them, and re-layouts  32 us (14%)
  matrix products  16.8 us (8%)
  between operations  13.6 us (6%)
  starting transfers between devices  10.7 us (5%)
  other arithmetic  2.56 us (1%)
    all_gather x1, waiting for transfers between devices, per_device(): all_channels = lax.all_gather(stacked, 'af', axis=4, tiled=True)  39 us
    all_gather x1, waiting for transfers between devices, per_device(): gathered = lax.all_gather(padded, 'af', axis=2, tiled=True)  38.4 us
    all_to_all x1, blocking collectives, per_device(): lax.all_to_all(first_filters, 'af', split_axis=4, concat_axis=3, tiled=True)  35.7 us
    all_to_all x1, blocking collectives, per_device(): lax.all_to_all(second_filters, 'af', split_axis=4, concat_axis=3, tiled=T...  24 us
    conv_general_dilated x2, matrix products, convolve(): lax.conv_general_dilated(volume, kernel, (stride, stride, stride), ((0, 0...  16.8 us
    unnamed x9, local copies, waits for them, and re-layouts  12.7 us
    ppermute x1, waiting for transfers between devices, passed_along(): return lax.ppermute(array, axis, pairs)  8.28 us
    all_gather x1, local copies, waits for them, and re-layouts, per_device(): all_channels = lax.all_gather(stacked, 'af', axis=4, tiled=True)  6.22 us
  transfers between devices with their start and end apart: 5, of which 4 were waited for; matrix products, arithmetic and copies ran while one was open for 7% of the time, Pallas kernels for 0%

commit v1 on v0

--- a/solution.py
+++ b/solution.py
@@ -23,13 +23,13 @@
     return lax.ppermute(array, axis, pairs)
 
 
-def convolve(volume, kernel, stride, row_pad):
+def convolve(volume, kernel, stride, row_pad, out_spec="NDHWC"):
     return lax.conv_general_dilated(
         volume,
         kernel,
         (stride, stride, stride),
         ((0, 0), (row_pad, row_pad), (1, 1)),
-        dimension_numbers=("NDHWC", "DHWIO", "NDHWC"),
+        dimension_numbers=("NDHWC", "DHWIO", out_spec),
         preferred_element_type=jnp.float32,
     )
 
@@ -41,10 +41,9 @@
     hidden = jnp.maximum(convolve(gathered, own_first, 1, 1), 0.0).astype(jnp.bfloat16)
     lower_plane = passed_along(hidden[:, -1:], "col", 1)
     stacked = jnp.concatenate([lower_plane, hidden], axis=1)
-    all_channels = lax.all_gather(stacked, "af", axis=4, tiled=True)
-    own_second = lax.all_to_all(second_filters, "af", split_axis=4, concat_axis=3, tiled=True)
-    totals = convolve(all_channels, own_second, 2, 1)
-    return jnp.maximum(totals, 0.0).astype(jnp.bfloat16)
+    partial = convolve(stacked, second_filters, 2, 1, out_spec="CNDHW")
+    totals = lax.psum_scatter(partial, "af", scatter_dimension=0, tiled=True)
+    return jnp.maximum(jnp.transpose(totals, (1, 2, 3, 4, 0)), 0.0).astype(jnp.bfloat16)
 
 
 def solution(mesh):

time: 223 us -> 242 us (1.085)
  the two profiles are of different devices: /device:TPU:9 before, /device:TPU:32 now
where the time goes in v1:
time: 242 us
  blocking collectives  137 us (57%)
  waiting for transfers between devices  45.8 us (19%)
  matrix products  15.9 us (7%)
  local copies, waits for them, and re-layouts  15.7 us (6%)
  between operations  14.2 us (6%)
  starting transfers between devices  12.3 us (5%)
    unnamed x1, blocking collectives  102 us
    all_to_all x1, blocking collectives, per_device(): lax.all_to_all(first_filters, 'af', split_axis=4, concat_axis=3, tiled=True)  35.8 us
    all_gather x1, waiting for transfers between devices, per_device(): gathered = lax.all_gather(padded, 'af', axis=2, tiled=True)  35.7 us
    conv_general_dilated x2, matrix products, convolve(): lax.conv_general_dilated(volume, kernel, (stride, stride, stride), ((0, 0...  15.9 us
    unnamed x7, local copies, waits for them, and re-layouts  8.85 us
    ppermute x1, waiting for transfers between devices, passed_along(): return lax.ppermute(array, axis, pairs)  8.62 us
    ppermute x1, starting transfers between devices, extended(): lax.ppermute(lax.slice_in_dim(block, 0, width, axis=dim), axis, backward)  5.76 us
    all_to_all x2, local copies, waits for them, and re-layouts, per_device(): lax.all_to_all(first_filters, 'af', split_axis=4, concat_axis=3, tiled=True)  5.49 us
  transfers between devices with their start and end apart: 4, of which 3 were waited for; matrix products, arithmetic and copies ran while one was open for 4% of the time, Pallas kernels for 0%

profile of v1, /device:TPU:32, one launch (start us, length us, event | category | flops | bytes accessed | tf_op | source)
XLA Modules:
  0.0 241.8 jit_solution(3626473693193635644)
XLA Ops:
  6.5 0.0 copy-start
  6.5 0.8 copy.25
  7.4 3.4 %collective-permute-start = (bf16[2,1,2,8,256]{4,0,3,2,1:T(2,128)(2,1)S(1)}, bf16[2,1,2,8,256]{4,0,3,2,1:T(2,128)(2,1)S(1)}, u32[]{:S(2)}, u32[]{:S(2)}) collective-permute-start(bf16[2,1,2,8,256]{4,0,3,2,1:T(2,128)(2,1)S(1)} %get-tuple-element.5), channel_id=1, source_target_pairs={{0,32},{32,64},{64,96},{96,128},{128,160},{160,192},{192,224},{224... | collective-permute-start | bytes 49160 | tf_op jit(solution)/shard_map/ppermute | solution.py:12
  10.8 5.8 %collective-permute-start.1 = (bf16[2,1,2,8,256]{4,0,3,2,1:T(2,128)(2,1)S(1)}, bf16[2,1,2,8,256]{4,0,3,2,1:T(2,128)(2,1)S(1)}, u32[]{:S(2)}, u32[]{:S(2)}) collective-permute-start(bf16[2,1,2,8,256]{4,0,3,2,1:T(2,128)(2,1)S(1)} %get-tuple-element.6), channel_id=1, source_target_pairs={{32,0},{64,32},{96,64},{128,96},{160,128},{192,160},{224,192},{256... | collective-permute-start | bytes 49160 | tf_op jit(solution)/shard_map/ppermute | solution.py:15
  16.6 0.0 collective-permute-done
  16.6 1.4 collective-permute-done.1
  18.0 0.7 pad_maximum_fusion.2
  18.7 0.0 all-gather.2.cloned.1.call-update
  18.7 3.3 %copy.28 = bf16[3,3,3,8,256]{3,2,1,0,4:T(4,128)(2,1)S(1)} copy(bf16[3,3,3,8,256]{4,3,2,1,0:T(8,128)(2,1)} %param.4) | data formatting | bytes 221184 | tf_op args[1]
  22.1 1.8 reshape.1
  23.9 35.8 %all_to_all.18 = bf16[32,2,864]{2,1,0:T(2,128)(2,1)S(1)} all-to-all(bf16[32,2,864]{2,1,0:T(2,128)(2,1)S(1)} %reshape.1), channel_id=1, replica_groups=mesh['col'=32,'af'=32] {'af'}, dimensions={0} | all-to-all | bytes 221184 | tf_op jit(solution)/shard_map/all_to_all | solution.py:40
  59.7 1.6 reshape.2
  61.3 2.0 copy.36
  63.4 3.4 %all_to_all.16 = bf16[3,3,3,256,8]{3,4,2,1,0:T(8,128)(2,1)S(1)} reshape(bf16[3,3,3,32,8,8]{4,3,5,2,1,0:T(8,128)(2,1)} %bitcast.19) | data formatting | bytes 221184 | tf_op jit(solution)/shard_map/all_to_all | solution.py:40
  66.8 35.7 %all-gather.2.cloned.1.call-done = bf16[2,4,64,8,256]{4,0,3,2,1:T(2,128)(2,1)} async-done(((bf16[2,4,2,8,256]{4,0,3,2,1:T(2,128)(2,1)}), bf16[2,4,64,8,256]{4,0,3,2,1:T(2,128)(2,1)}) %all-gather.2.cloned.1.call-update) | async-done | bytes 2097168 | tf_op jit(solution)/shard_map/all_gather | solution.py:39
  102.5 13.9 %fusion = bf16[2,2,64,8,8]{4,0,3,2,1:T(2,128)(2,1)S(1)} fusion(bf16[2,4,64,8,256]{4,0,3,2,1:T(2,128)(2,1)} %all-gather.2.cloned.1.call-done, bf16[3,3,3,256,8]{3,4,2,1,0:T(8,128)(2,1)S(1)} %all_to_all.16), kind=kOutput, calls=%fused_computation.2 | convolution fusion | flops 205488128 | bytes 2240512 | tf_op jit(solution)/shard_map/conv_general_dilated | solution.py:27
  116.5 0.2 slice.14
  116.7 3.1 %collective-permute-start.2 = (bf16[2,1,64,8,8]{4,0,3,2,1:T(2,128)(2,1)S(1)}, bf16[2,1,64,8,8]{4,0,3,2,1:T(2,128)(2,1)S(1)}, u32[]{:S(2)}, u32[]{:S(2)}) collective-permute-start(bf16[2,1,64,8,8]{4,0,3,2,1:T(2,128)(2,1)S(1)} %slice.14), channel_id=1, source_target_pairs={{0,32},{32,64},{64,96},{96,128},{128,160},{160,192},{192,224},{224... | collective-permute-start | bytes 49160 | tf_op jit(solution)/shard_map/ppermute | solution.py:23
  119.8 1.3 dynamic-slice
  121.7 8.6 %collective-permute-done.2 = bf16[2,1,64,8,8]{4,0,3,2,1:T(2,128)(2,1)S(1)} collective-permute-done((bf16[2,1,64,8,8]{4,0,3,2,1:T(2,128)(2,1)S(1)}, bf16[2,1,64,8,8]{4,0,3,2,1:T(2,128)(2,1)S(1)}, u32[]{:S(2)}, u32[]{:S(2)}) %collective-permute-start.2) | collective-permute-done | bytes 16416 | tf_op jit(solution)/shard_map/ppermute | solution.py:23
  130.3 1.9 fusion.1
  132.2 0.5 copy.31
  132.8 101.5 %all-reduce.2 = bf16[256,2,1,32,4]{3,4,2,1,0:T(4,128)(2,1)S(1)} all-reduce(f32[256,2,1,32,4]{3,4,2,1,0:T(4,128)S(1)} %copy.31), channel_id=2, replica_groups=mesh['col'=32,'af'=32] {'af'}, use_global_device_ids=true, to_apply=%region_0.0.clone | all-reduce | flops 65536 | bytes 393216
  234.3 0.6 copy.32
  (4 shorter events, 0.0 us)
Async XLA Ops:
  6.5 123.8 %copy-start = (bf16[3,3,3,8,256]{4,3,2,1,0:T(8,128)(2,1)S(1)}, bf16[3,3,3,8,256]{4,3,2,1,0:T(8,128)(2,1)}, u32[]{:S(2)}) copy-start(bf16[3,3,3,8,256]{4,3,2,1,0:T(8,128)(2,1)} %param.5) | copy-start | bytes 331780
  6.5 96.0 %all-gather.2.cloned.1.call-start = ((), (), s32[]{:S(2)}) async-start(), calls=%async_computation.1 | async-start | bytes 2162688 | tf_op jit(solution)/shard_map/all_gather | solution.py:39
  7.4 9.2 %collective-permute-start = (bf16[2,1,2,8,256]{4,0,3,2,1:T(2,128)(2,1)S(1)}, bf16[2,1,2,8,256]{4,0,3,2,1:T(2,128)(2,1)S(1)}, u32[]{:S(2)}, u32[]{:S(2)}) collective-permute-start(bf16[2,1,2,8,256]{4,0,3,2,1:T(2,128)(2,1)S(1)} %get-tuple-element.5), channel_id=1, source_target_pairs={{0,32},{32,64},{64,96},{96,128},{128,160},{160,192},{192,224},{224... | collective-permute-start | bytes 49160 | tf_op jit(solution)/shard_map/ppermute | solution.py:12
  10.8 7.2 %collective-permute-start.1 = (bf16[2,1,2,8,256]{4,0,3,2,1:T(2,128)(2,1)S(1)}, bf16[2,1,2,8,256]{4,0,3,2,1:T(2,128)(2,1)S(1)}, u32[]{:S(2)}, u32[]{:S(2)}) collective-permute-start(bf16[2,1,2,8,256]{4,0,3,2,1:T(2,128)(2,1)S(1)} %get-tuple-element.6), channel_id=1, source_target_pairs={{32,0},{64,32},{96,64},{128,96},{160,128},{192,160},{224,192},{256... | collective-permute-start | bytes 49160 | tf_op jit(solution)/shard_map/ppermute | solution.py:15
  116.7 13.6 %collective-permute-start.2 = (bf16[2,1,64,8,8]{4,0,3,2,1:T(2,128)(2,1)S(1)}, bf16[2,1,64,8,8]{4,0,3,2,1:T(2,128)(2,1)S(1)}, u32[]{:S(2)}, u32[]{:S(2)}) collective-permute-start(bf16[2,1,64,8,8]{4,0,3,2,1:T(2,128)(2,1)S(1)} %slice.14), channel_id=1, source_target_pairs={{0,32},{32,64},{64,96},{96,128},{128,160},{160,192},{192,224},{224... | collective-permute-start | bytes 49160 | tf_op jit(solution)/shard_map/ppermute | solution.py:23
Sparse Core Ops, SparseCore 0:
  18.9 83.6 all-gather.1

commit v2 on v1

--- a/solution.py
+++ b/solution.py
@@ -34,6 +34,21 @@
     )
 
 
+def reduce_scattered(partial, axis):
+    peers = lax.axis_size(axis)
+    me = lax.axis_index(axis)
+    levels = peers.bit_length() - 1
+    blocks = partial.reshape((2,) * levels + (partial.shape[0] // peers,) + partial.shape[1:])
+    for bit in range(levels):
+        at = levels - 1 - bit
+        mine = (me // (1 << bit)) % 2
+        keep = lax.dynamic_index_in_dim(blocks, mine, axis=at, keepdims=False)
+        give = lax.dynamic_index_in_dim(blocks, 1 - mine, axis=at, keepdims=False)
+        pairs = [(i, i ^ (1 << bit)) for i in range(peers)]
+        blocks = keep + lax.ppermute(give, axis, pairs)
+    return blocks
+
+
 def per_device(inputs, first_filters, second_filters):
     padded = extended(inputs, (("col", 1),), 1)
     gathered = lax.all_gather(padded, "af", axis=2, tiled=True)
@@ -42,7 +57,7 @@
     lower_plane = passed_along(hidden[:, -1:], "col", 1)
     stacked = jnp.concatenate([lower_plane, hidden], axis=1)
     partial = convolve(stacked, second_filters, 2, 1, out_spec="CNDHW")
-    totals = lax.psum_scatter(partial, "af", scatter_dimension=0, tiled=True)
+    totals = reduce_scattered(partial, "af")
     return jnp.maximum(jnp.transpose(totals, (1, 2, 3, 4, 0)), 0.0).astype(jnp.bfloat16)
 
 

time: 242 us -> 193 us (0.80)
  blocking collectives: 137 us -> 36.5 us
  waiting for transfers between devices: 45.8 us -> 81.9 us
  starting transfers between devices: 12.3 us -> 29.4 us
    unnamed x1 -> x0, blocking collectives: 102 us -> none
    ppermute x0 -> x5, waiting for transfers between devices: none -> 30.1 us  [reduce_scattered(): blocks = keep + lax.ppermute(give, axis, pairs)]
    ppermute x0 -> x5, starting transfers between devices: none -> 20.8 us  [reduce_scattered(): blocks = keep + lax.ppermute(give, axis, pairs)]
    ppermute x1, waiting for transfers between devices: 0.01 us -> 7.01 us  [extended(): lax.ppermute(lax.slice_in_dim(block, block.shape[dim] - width, None, axis...]
    ppermute x1, waiting for transfers between devices: 8.62 us -> 11.5 us  [passed_along(): return lax.ppermute(array, axis, pairs)]
    all_gather x1, waiting for transfers between devices: 35.7 us -> 33.2 us  [per_device(): gathered = lax.all_gather(padded, 'af', axis=2, tiled=True)]
    unnamed x7 -> x6, local copies, waits for them, and re-layouts: 8.85 us -> 7.57 us
  transfers between devices with their start and end apart: 4 -> 9, of which waited for: 3 -> 8; matrix products, arithmetic and copies ran while one was open for 4% -> 5% of each run, Pallas kernels for 0% -> 0%
where the time goes in v2:
time: 193 us
  waiting for transfers between devices  81.9 us (42%)
  blocking collectives  36.5 us (19%)
  starting transfers between devices  29.4 us (15%)
  matrix products  15.9 us (8%)
  local copies, waits for them, and re-layouts  13.8 us (7%)
  between operations  13.8 us (7%)
    all_to_all x1, blocking collectives, per_device(): lax.all_to_all(first_filters, 'af', split_axis=4, concat_axis=3, tiled=True)  36.5 us
    all_gather x1, waiting for transfers between devices, per_device(): gathered = lax.all_gather(padded, 'af', axis=2, tiled=True)  33.2 us
    ppermute x5, waiting for transfers between devices, reduce_scattered(): blocks = keep + lax.ppermute(give, axis, pairs)  30.1 us
    ppermute x5, starting transfers between devices, reduce_scattered(): blocks = keep + lax.ppermute(give, axis, pairs)  20.8 us
    conv_general_dilated x2, matrix products, convolve(): lax.conv_general_dilated(volume, kernel, (stride, stride, stride), ((0, 0...  15.9 us
    ppermute x1, waiting for transfers between devices, passed_along(): return lax.ppermute(array, axis, pairs)  11.5 us
    unnamed x6, local copies, waits for them, and re-layouts  7.57 us
    ppermute x1, waiting for transfers between devices, extended(): lax.ppermute(lax.slice_in_dim(block, block.shape[dim] - width, None, axis...  7.01 us
  transfers between devices with their start and end apart: 9, of which 8 were waited for; matrix products, arithmetic and copies ran while one was open for 5% of the time, Pallas kernels for 0%

profile of v2, /device:TPU:32, one launch (start us, length us, event | category | flops | bytes accessed | tf_op | source)
XLA Modules:
  0.0 192.7 jit_solution(529898846591842184)
XLA Ops:
  7.4 4.6 %collective-permute-start.1 = (bf16[2,1,2,8,256]{4,0,3,2,1:T(2,128)(2,1)S(1)}, bf16[2,1,2,8,256]{4,0,3,2,1:T(2,128)(2,1)S(1)}, u32[]{:S(2)}, u32[]{:S(2)}) collective-permute-start(bf16[2,1,2,8,256]{4,0,3,2,1:T(2,128)(2,1)S(1)} %get-tuple-element.8), channel_id=1, source_target_pairs={{32,0},{64,32},{96,64},{128,96},{160,128},{192,160},{224,192},{256... | collective-permute-start | bytes 49160 | tf_op jit(solution)/shard_map/ppermute | solution.py:15
  12.0 1.9 collective-permute-start
  13.9 7.0 %collective-permute-done = bf16[2,1,2,8,256]{4,0,3,2,1:T(2,128)(2,1)S(1)} collective-permute-done((bf16[2,1,2,8,256]{4,0,3,2,1:T(2,128)(2,1)S(1)}, bf16[2,1,2,8,256]{4,0,3,2,1:T(2,128)(2,1)S(1)}, u32[]{:S(2)}, u32[]{:S(2)}) %collective-permute-start) | collective-permute-done | bytes 16416 | tf_op jit(solution)/shard_map/ppermute | solution.py:12
  21.7 3.3 %copy.35 = bf16[3,3,3,8,256]{3,2,1,0,4:T(4,128)(2,1)S(1)} copy(bf16[3,3,3,8,256]{4,3,2,1,0:T(8,128)(2,1)} %param.4) | data formatting | bytes 221184 | tf_op args[1]
  25.0 1.8 reshape.4
  26.8 36.5 %all_to_all.18 = bf16[32,2,864]{2,1,0:T(2,128)(2,1)S(1)} all-to-all(bf16[32,2,864]{2,1,0:T(2,128)(2,1)S(1)} %reshape.4), channel_id=1, replica_groups=mesh['col'=32,'af'=32] {'af'}, dimensions={0} | all-to-all | bytes 221184 | tf_op jit(solution)/shard_map/all_to_all | solution.py:55
  63.3 1.6 reshape.5
  64.9 2.0 %copy.46 = bf16[3,3,3,8,32,8]{3,4,5,2,1,0:T(8,128)(2,1)} copy(bf16[3,3,3,8,32,8]{3,2,1,0,5,4:T(4,128)(2,1)S(1)} %bitcast.44) | data formatting | bytes 221184 | tf_op jit(solution)/shard_map/all_to_all | solution.py:55
  67.0 3.4 %all_to_all.16 = bf16[3,3,3,256,8]{3,4,2,1,0:T(8,128)(2,1)S(1)} reshape(bf16[3,3,3,32,8,8]{4,3,5,2,1,0:T(8,128)(2,1)} %bitcast.46) | data formatting | bytes 221184 | tf_op jit(solution)/shard_map/all_to_all | solution.py:55
  70.4 33.2 %all-gather.2.cloned.1.call-done = bf16[2,4,64,8,256]{4,0,3,2,1:T(2,128)(2,1)} async-done(((bf16[2,4,2,8,256]{4,0,3,2,1:T(2,128)(2,1)}), bf16[2,4,64,8,256]{4,0,3,2,1:T(2,128)(2,1)}) %all-gather.2.cloned.1.call-update) | async-done | bytes 2097168 | tf_op jit(solution)/shard_map/all_gather | solution.py:54
  103.6 13.9 %fusion = bf16[2,2,64,8,8]{4,0,3,2,1:T(2,128)(2,1)S(1)} fusion(bf16[2,4,64,8,256]{4,0,3,2,1:T(2,128)(2,1)} %all-gather.2.cloned.1.call-done, bf16[3,3,3,256,8]{3,4,2,1,0:T(8,128)(2,1)S(1)} %all_to_all.16), kind=kOutput, calls=%fused_computation.2 | convolution fusion | flops 205488128 | bytes 2240512 | tf_op jit(solution)/shard_map/conv_general_dilated | solution.py:27
  117.8 2.1 %collective-permute-start.2 = (bf16[2,1,64,8,8]{4,0,3,2,1:T(2,128)(2,1)S(1)}, bf16[2,1,64,8,8]{4,0,3,2,1:T(2,128)(2,1)S(1)}, u32[]{:S(2)}, u32[]{:S(2)}) collective-permute-start(bf16[2,1,64,8,8]{4,0,3,2,1:T(2,128)(2,1)S(1)} %slice.14), channel_id=1, source_target_pairs={{0,32},{32,64},{64,96},{96,128},{128,160},{160,192},{192,224},{224... | collective-permute-start | bytes 49160 | tf_op jit(solution)/shard_map/ppermute | solution.py:23
  119.9 11.5 %collective-permute-done.2 = bf16[2,1,64,8,8]{4,0,3,2,1:T(2,128)(2,1)S(1)} collective-permute-done((bf16[2,1,64,8,8]{4,0,3,2,1:T(2,128)(2,1)S(1)}, bf16[2,1,64,8,8]{4,0,3,2,1:T(2,128)(2,1)S(1)}, u32[]{:S(2)}, u32[]{:S(2)}) %collective-permute-start.2) | collective-permute-done | bytes 16416 | tf_op jit(solution)/shard_map/ppermute | solution.py:23
  131.4 1.9 fusion.1
  133.9 1.9 collective-permute-start.3
  135.9 1.8 collective-permute-done.3
  137.8 2.4 %collective-permute-start.4 = (f32[2,2,2,8,2,1,32,4]{6,3,7,5,4,2,1,0:T(8,128)S(1)}, f32[2,2,2,8,2,1,32,4]{6,3,7,5,4,2,1,0:T(8,128)S(1)}, u32[]{:S(2)}, u32[]{:S(2)}) collective-permute-start(f32[2,2,2,8,2,1,32,4]{6,3,7,5,4,2,1,0:T(8,128)S(1)} %dynamic-slice_bitcast_fusion), channel_id=1, source_target_pairs={{0,2},{1,3},{2,0},{3,1},{4,6},{5,7},{6,4},{7,5},{8,10},{9,11},{10,... | collective-permute-start | bytes 196616 | tf_op jit(solution)/shard_map/ppermute | solution.py:48
  140.3 7.8 %collective-permute-done.4 = f32[2,2,2,8,2,1,32,4]{6,3,7,5,4,2,1,0:T(8,128)S(1)} collective-permute-done((f32[2,2,2,8,2,1,32,4]{6,3,7,5,4,2,1,0:T(8,128)S(1)}, f32[2,2,2,8,2,1,32,4]{6,3,7,5,4,2,1,0:T(8,128)S(1)}, u32[]{:S(2)}, u32[]{:S(2)}) %collective-permute-start.4) | collective-permute-done | bytes 65568 | tf_op jit(solution)/shard_map/ppermute | solution.py:48
  148.1 4.1 %collective-permute-start.5 = (f32[2,2,8,2,1,32,4]{5,2,6,3,1,0,4:T(8,128)S(1)}, f32[2,2,8,2,1,32,4]{5,2,6,3,1,0,4:T(8,128)S(1)}, u32[]{:S(2)}, u32[]{:S(2)}) collective-permute-start(f32[2,2,8,2,1,32,4]{5,2,6,3,1,0,4:T(8,128)S(1)} %dynamic-slice_bitcast_fusion.1), channel_id=1, source_target_pairs={{0,4},{1,5},{2,6},{3,7},{4,0},{5,1},{6,2},{7,3},{8,12},{9,13},{10,... | collective-permute-start | bytes 98312 | tf_op jit(solution)/shard_map/ppermute | solution.py:48
  152.3 6.1 %collective-permute-done.5 = f32[2,2,8,2,1,32,4]{5,2,6,3,1,0,4:T(8,128)S(1)} collective-permute-done((f32[2,2,8,2,1,32,4]{5,2,6,3,1,0,4:T(8,128)S(1)}, f32[2,2,8,2,1,32,4]{5,2,6,3,1,0,4:T(8,128)S(1)}, u32[]{:S(2)}, u32[]{:S(2)}) %collective-permute-start.5) | collective-permute-done | bytes 32800 | tf_op jit(solution)/shard_map/ppermute | solution.py:48
  158.4 5.0 %collective-permute-start.6 = (f32[2,8,2,1,32,4]{4,1,5,2,3,0:T(8,128)S(1)}, f32[2,8,2,1,32,4]{4,1,5,2,3,0:T(8,128)S(1)}, u32[]{:S(2)}, u32[]{:S(2)}) collective-permute-start(f32[2,8,2,1,32,4]{4,1,5,2,3,0:T(8,128)S(1)} %dynamic-slice_bitcast_fusion.2), channel_id=1, source_target_pairs={{0,8},{1,9},{2,10},{3,11},{4,12},{5,13},{6,14},{7,15},{8,0},{9,1},... | collective-permute-start | bytes 49160 | tf_op jit(solution)/shard_map/ppermute | solution.py:48
  163.5 7.2 %collective-permute-done.6 = f32[2,8,2,1,32,4]{4,1,5,2,3,0:T(8,128)S(1)} collective-permute-done((f32[2,8,2,1,32,4]{4,1,5,2,3,0:T(8,128)S(1)}, f32[2,8,2,1,32,4]{4,1,5,2,3,0:T(8,128)S(1)}, u32[]{:S(2)}, u32[]{:S(2)}) %collective-permute-start.6) | collective-permute-done | bytes 16416 | tf_op jit(solution)/shard_map/ppermute | solution.py:48
  170.7 7.3 %collective-permute-start.7 = (f32[8,2,1,32,4]{3,0,4,2,1:T(8,128)S(1)}, f32[8,2,1,32,4]{3,0,4,2,1:T(8,128)S(1)}, u32[]{:S(2)}, u32[]{:S(2)}) collective-permute-start(f32[8,2,1,32,4]{3,0,4,2,1:T(8,128)S(1)} %dynamic-slice_bitcast_fusion.3), channel_id=1, source_target_pairs={{0,16},{1,17},{2,18},{3,19},{4,20},{5,21},{6,22},{7,23},{8,24},{9,... | collective-permute-start | bytes 24584 | tf_op jit(solution)/shard_map/ppermute | solution.py:48
  178.1 7.2 %collective-permute-done.7 = f32[8,2,1,32,4]{3,0,4,2,1:T(8,128)S(1)} collective-permute-done((f32[8,2,1,32,4]{3,0,4,2,1:T(8,128)S(1)}, f32[8,2,1,32,4]{3,0,4,2,1:T(8,128)S(1)}, u32[]{:S(2)}, u32[]{:S(2)}) %collective-permute-start.7) | collective-permute-done | bytes 8224 | tf_op jit(solution)/shard_map/ppermute | solution.py:48
  (21 shorter events, 3.1 us)
Async XLA Ops:
  6.5 124.9 %copy-start = (bf16[3,3,3,8,256]{4,3,2,1,0:T(8,128)(2,1)S(1)}, bf16[3,3,3,8,256]{4,3,2,1,0:T(8,128)(2,1)}, u32[]{:S(2)}) copy-start(bf16[3,3,3,8,256]{4,3,2,1,0:T(8,128)(2,1)} %param.5) | copy-start | bytes 331780
  6.5 97.1 %all-gather.2.cloned.1.call-start = ((), (), s32[]{:S(2)}) async-start(), calls=%async_computation.1 | async-start | bytes 2162688 | tf_op jit(solution)/shard_map/all_gather | solution.py:54
  7.4 6.5 %collective-permute-start.1 = (bf16[2,1,2,8,256]{4,0,3,2,1:T(2,128)(2,1)S(1)}, bf16[2,1,2,8,256]{4,0,3,2,1:T(2,128)(2,1)S(1)}, u32[]{:S(2)}, u32[]{:S(2)}) collective-permute-start(bf16[2,1,2,8,256]{4,0,3,2,1:T(2,128)(2,1)S(1)} %get-tuple-element.8), channel_id=1, source_target_pairs={{32,0},{64,32},{96,64},{128,96},{160,128},{192,160},{224,192},{256... | collective-permute-start | bytes 49160 | tf_op jit(solution)/shard_map/ppermute | solution.py:15
  12.0 9.0 %collective-permute-start = (bf16[2,1,2,8,256]{4,0,3,2,1:T(2,128)(2,1)S(1)}, bf16[2,1,2,8,256]{4,0,3,2,1:T(2,128)(2,1)S(1)}, u32[]{:S(2)}, u32[]{:S(2)}) collective-permute-start(bf16[2,1,2,8,256]{4,0,3,2,1:T(2,128)(2,1)S(1)} %get-tuple-element.7), channel_id=1, source_target_pairs={{0,32},{32,64},{64,96},{96,128},{128,160},{160,192},{192,224},{224... | collective-permute-start | bytes 49160 | tf_op jit(solution)/shard_map/ppermute | solution.py:12
  117.8 13.6 %collective-permute-start.2 = (bf16[2,1,64,8,8]{4,0,3,2,1:T(2,128)(2,1)S(1)}, bf16[2,1,64,8,8]{4,0,3,2,1:T(2,128)(2,1)S(1)}, u32[]{:S(2)}, u32[]{:S(2)}) collective-permute-start(bf16[2,1,64,8,8]{4,0,3,2,1:T(2,128)(2,1)S(1)} %slice.14), channel_id=1, source_target_pairs={{0,32},{32,64},{64,96},{96,128},{128,160},{160,192},{192,224},{224... | collective-permute-start | bytes 49160 | tf_op jit(solution)/shard_map/ppermute | solution.py:23
  133.9 3.8 %collective-permute-start.3 = (f32[2,2,2,2,8,2,1,32,4]{7,4,8,6,5,3,2,1,0:T(8,128)S(1)}, f32[2,2,2,2,8,2,1,32,4]{7,4,8,6,5,3,2,1,0:T(8,128)S(1)}, u32[]{:S(2)}, u32[]{:S(2)}) collective-permute-start(f32[2,2,2,2,8,2,1,32,4]{7,4,8,6,5,3,2,1,0:T(8,128)S(1)} %bitcast.48), channel_id=1, source_target_pairs={{0,1},{1,0},{2,3},{3,2},{4,5},{5,4},{6,7},{7,6},{8,9},{9,8},{10,11... | collective-permute-start | bytes 393224 | tf_op jit(solution)/shard_map/ppermute | solution.py:48
  137.8 10.2 %collective-permute-start.4 = (f32[2,2,2,8,2,1,32,4]{6,3,7,5,4,2,1,0:T(8,128)S(1)}, f32[2,2,2,8,2,1,32,4]{6,3,7,5,4,2,1,0:T(8,128)S(1)}, u32[]{:S(2)}, u32[]{:S(2)}) collective-permute-start(f32[2,2,2,8,2,1,32,4]{6,3,7,5,4,2,1,0:T(8,128)S(1)} %dynamic-slice_bitcast_fusion), channel_id=1, source_target_pairs={{0,2},{1,3},{2,0},{3,1},{4,6},{5,7},{6,4},{7,5},{8,10},{9,11},{10,... | collective-permute-start | bytes 196616 | tf_op jit(solution)/shard_map/ppermute | solution.py:48
  148.1 10.2 %collective-permute-start.5 = (f32[2,2,8,2,1,32,4]{5,2,6,3,1,0,4:T(8,128)S(1)}, f32[2,2,8,2,1,32,4]{5,2,6,3,1,0,4:T(8,128)S(1)}, u32[]{:S(2)}, u32[]{:S(2)}) collective-permute-start(f32[2,2,8,2,1,32,4]{5,2,6,3,1,0,4:T(8,128)S(1)} %dynamic-slice_bitcast_fusion.1), channel_id=1, source_target_pairs={{0,4},{1,5},{2,6},{3,7},{4,0},{5,1},{6,2},{7,3},{8,12},{9,13},{10,... | collective-permute-start | bytes 98312 | tf_op jit(solution)/shard_map/ppermute | solution.py:48
  158.4 12.3 %collective-permute-start.6 = (f32[2,8,2,1,32,4]{4,1,5,2,3,0:T(8,128)S(1)}, f32[2,8,2,1,32,4]{4,1,5,2,3,0:T(8,128)S(1)}, u32[]{:S(2)}, u32[]{:S(2)}) collective-permute-start(f32[2,8,2,1,32,4]{4,1,5,2,3,0:T(8,128)S(1)} %dynamic-slice_bitcast_fusion.2), channel_id=1, source_target_pairs={{0,8},{1,9},{2,10},{3,11},{4,12},{5,13},{6,14},{7,15},{8,0},{9,1},... | collective-permute-start | bytes 49160 | tf_op jit(solution)/shard_map/ppermute | solution.py:48
  170.7 14.5 %collective-permute-start.7 = (f32[8,2,1,32,4]{3,0,4,2,1:T(8,128)S(1)}, f32[8,2,1,32,4]{3,0,4,2,1:T(8,128)S(1)}, u32[]{:S(2)}, u32[]{:S(2)}) collective-permute-start(f32[8,2,1,32,4]{3,0,4,2,1:T(8,128)S(1)} %dynamic-slice_bitcast_fusion.3), channel_id=1, source_target_pairs={{0,16},{1,17},{2,18},{3,19},{4,20},{5,21},{6,22},{7,23},{8,24},{9,... | collective-permute-start | bytes 24584 | tf_op jit(solution)/shard_map/ppermute | solution.py:48
Sparse Core Ops, SparseCore 0:
  21.8 81.8 all-gather.1

commit v3 on v1

--- a/solution.py
+++ b/solution.py
@@ -34,28 +34,39 @@
     )
 
 
+def reduce_scattered(partial):
+    chips = lax.axis_size("z")
+    mine = lax.axis_index("core")
+    blocks = partial.reshape((chips, 2, partial.shape[0] // (2 * chips)) + partial.shape[1:])
+    keep = lax.dynamic_index_in_dim(blocks, mine, axis=1, keepdims=False)
+    give = lax.dynamic_index_in_dim(blocks, 1 - mine, axis=1, keepdims=False)
+    half = keep + lax.ppermute(give, "core", [(0, 1), (1, 0)])
+    return lax.all_to_all(half, "z", 0, 0, tiled=True).sum(axis=0)
+
+
 def per_device(inputs, first_filters, second_filters):
     padded = extended(inputs, (("col", 1),), 1)
-    gathered = lax.all_gather(padded, "af", axis=2, tiled=True)
-    own_first = lax.all_to_all(first_filters, "af", split_axis=4, concat_axis=3, tiled=True)
+    gathered = lax.all_gather(lax.all_gather(padded, "core", axis=2, tiled=True), "z", axis=2, tiled=True)
+    own_first = lax.all_to_all(first_filters, ("z", "core"), split_axis=4, concat_axis=3, tiled=True)
     hidden = jnp.maximum(convolve(gathered, own_first, 1, 1), 0.0).astype(jnp.bfloat16)
     lower_plane = passed_along(hidden[:, -1:], "col", 1)
     stacked = jnp.concatenate([lower_plane, hidden], axis=1)
     partial = convolve(stacked, second_filters, 2, 1, out_spec="CNDHW")
-    totals = lax.psum_scatter(partial, "af", scatter_dimension=0, tiled=True)
+    totals = reduce_scattered(partial)
     return jnp.maximum(jnp.transpose(totals, (1, 2, 3, 4, 0)), 0.0).astype(jnp.bfloat16)
 
 
 def solution(mesh):
+    fine = jax.sharding.Mesh(mesh.devices.reshape(mesh.devices.shape[0], -1, 2), ("col", "z", "core"))
     placed = (
-        P(None, "col", "af", None, None),
-        P(None, None, None, "af", None),
-        P(None, None, None, "af", None),
+        P(None, "col", ("z", "core"), None, None),
+        P(None, None, None, ("z", "core"), None),
+        P(None, None, None, ("z", "core"), None),
     )
     return jax.shard_map(
         per_device,
-        mesh=mesh,
+        mesh=fine,
         in_specs=placed,
-        out_specs=P(None, "col", None, None, "af"),
+        out_specs=P(None, "col", None, None, ("z", "core")),
         check_vma=False,
     )

time: 242 us -> 171 us (0.71)
  blocking collectives: 137 us -> 60.5 us
  waiting for transfers between devices: 45.8 us -> 53.9 us
    unnamed x1 -> x0, blocking collectives: 102 us -> none
    all_to_all x1 -> x2, blocking collectives: 35.8 us -> 58.5 us  [the longest x1 36.6 us: per_device(): lax.all_to_all(first_filters, ('z', 'core'), split_axis=4, concat_axis=3,...]
    ppermute x1, waiting for transfers between devices: 0.01 us -> 7.01 us  [extended(): lax.ppermute(lax.slice_in_dim(block, block.shape[dim] - width, None, axis...]
    unnamed x7 -> x8, local copies, waits for them, and re-layouts: 8.85 us -> 7.99 us
    all_to_all x2 -> x3, local copies, waits for them, and re-layouts: 5.49 us -> 6.01 us  [the longest x2 5.49 us: per_device(): lax.all_to_all(first_filters, ('z', 'core'), split_axis=4, concat_axis=3,...]
  transfers between devices with their start and end apart: 4 -> 5, of which waited for: 3 -> 4; matrix products, arithmetic and copies ran while one was open for 4% -> 5% of each run, Pallas kernels for 0% -> 0%
where the time goes in v3:
time: 171 us
  blocking collectives  60.5 us (35%)
  waiting for transfers between devices  53.9 us (32%)
  matrix products  15.9 us (9%)
  local copies, waits for them, and re-layouts  14.7 us (9%)
  between operations  13.5 us (8%)
  starting transfers between devices  10.5 us (6%)
  other arithmetic  1.79 us (1%)
    all_to_all x1, blocking collectives, per_device(): lax.all_to_all(first_filters, ('z', 'core'), split_axis=4, concat_axis=3,...  36.6 us
    all_gather x1, waiting for transfers between devices, per_device(): lax.all_gather(lax.all_gather(padded, 'core', axis=2, tiled=True), 'z', a...  35.5 us
    all_to_all x1, blocking collectives, reduce_scattered(): return lax.all_to_all(half, 'z', 0, 0, tiled=True).sum(axis=0)  21.9 us
    conv_general_dilated x2, matrix products, convolve(): lax.conv_general_dilated(volume, kernel, (stride, stride, stride), ((0, 0...  15.9 us
    ppermute x1, waiting for transfers between devices, passed_along(): return lax.ppermute(array, axis, pairs)  9.47 us
    unnamed x8, local copies, waits for them, and re-layouts  7.99 us
    ppermute x1, waiting for transfers between devices, extended(): lax.ppermute(lax.slice_in_dim(block, block.shape[dim] - width, None, axis...  7.01 us
    all_to_all x2, local copies, waits for them, and re-layouts, per_device(): lax.all_to_all(first_filters, ('z', 'core'), split_axis=4, concat_axis=3,...  5.49 us
  transfers between devices with their start and end apart: 5, of which 4 were waited for; matrix products, arithmetic and copies ran while one was open for 5% of the time, Pallas kernels for 0%

profile of v3, /device:TPU:32, one launch (start us, length us, event | category | flops | bytes accessed | tf_op | source)
XLA Modules:
  0.0 170.8 jit_solution(9491735591111192867)
XLA Ops:
  6.5 0.8 copy.36
  7.4 4.6 %collective-permute-start.1 = (bf16[2,1,2,8,256]{4,0,3,2,1:T(2,128)(2,1)S(1)}, bf16[2,1,2,8,256]{4,0,3,2,1:T(2,128)(2,1)S(1)}, u32[]{:S(2)}, u32[]{:S(2)}) collective-permute-start(bf16[2,1,2,8,256]{4,0,3,2,1:T(2,128)(2,1)S(1)} %get-tuple-element.8), channel_id=1, source_target_pairs={{32,0},{64,32},{96,64},{128,96},{160,128},{192,160},{224,192},{256... | collective-permute-start | bytes 49160 | tf_op jit(solution)/shard_map/ppermute | solution.py:15
  12.0 1.9 %collective-permute-start = (bf16[2,1,2,8,256]{4,0,3,2,1:T(2,128)(2,1)S(1)}, bf16[2,1,2,8,256]{4,0,3,2,1:T(2,128)(2,1)S(1)}, u32[]{:S(2)}, u32[]{:S(2)}) collective-permute-start(bf16[2,1,2,8,256]{4,0,3,2,1:T(2,128)(2,1)S(1)} %get-tuple-element.7), channel_id=1, source_target_pairs={{0,32},{32,64},{64,96},{96,128},{128,160},{160,192},{192,224},{224... | collective-permute-start | bytes 49160 | tf_op jit(solution)/shard_map/ppermute | solution.py:12
  13.9 7.0 %collective-permute-done = bf16[2,1,2,8,256]{4,0,3,2,1:T(2,128)(2,1)S(1)} collective-permute-done((bf16[2,1,2,8,256]{4,0,3,2,1:T(2,128)(2,1)S(1)}, bf16[2,1,2,8,256]{4,0,3,2,1:T(2,128)(2,1)S(1)}, u32[]{:S(2)}, u32[]{:S(2)}) %collective-permute-start) | collective-permute-done | bytes 16416 | tf_op jit(solution)/shard_map/ppermute | solution.py:12
  21.0 2.0 %all_gather.6 = bf16[2,4,4,8,256]{4,0,3,2,1:T(2,128)(2,1)} all-gather(bf16[2,4,2,8,256]{4,0,3,2,1:T(2,128)(2,1)S(1)} %pad_maximum_fusion.2), channel_id=1, replica_groups=mesh['col'=32,'z'=16,'core'=2] {'core'}, dimensions={2}, use_global_device_ids=true | all-gather | bytes 196608 | tf_op jit(solution)/shard_map/all_gather | solution.py:49
  23.1 3.3 %copy.39 = bf16[3,3,3,8,256]{3,2,1,0,4:T(4,128)(2,1)S(1)} copy(bf16[3,3,3,8,256]{4,3,2,1,0:T(8,128)(2,1)} %param.4) | data formatting | bytes 221184 | tf_op args[1]
  26.4 1.8 %reshape.8 = bf16[32,2,864]{2,1,0:T(2,128)(2,1)S(1)} reshape(bf16[256,3,3,3,8]{4,3,2,1,0:T(4,128)(2,1)S(1)} %bitcast.37) | data formatting | bytes 221184
  28.2 36.6 %all_to_all.23 = bf16[32,2,864]{2,1,0:T(2,128)(2,1)S(1)} all-to-all(bf16[32,2,864]{2,1,0:T(2,128)(2,1)S(1)} %reshape.8), channel_id=1, replica_groups=mesh['col'=32,'z'=16,'core'=2] {'z','core'}, dimensions={0} | all-to-all | bytes 221184 | tf_op jit(solution)/shard_map/all_to_all | solution.py:50
  64.8 1.6 reshape.9
  66.5 2.1 %copy.53 = bf16[3,3,3,8,32,8]{3,4,5,2,1,0:T(8,128)(2,1)} copy(bf16[3,3,3,8,32,8]{3,2,1,0,5,4:T(4,128)(2,1)S(1)} %bitcast.36) | data formatting | bytes 221184 | tf_op jit(solution)/shard_map/all_to_all | solution.py:50
  68.5 3.4 %all_to_all.19 = bf16[3,3,3,256,8]{3,4,2,1,0:T(8,128)(2,1)S(1)} reshape(bf16[3,3,3,32,8,8]{4,3,5,2,1,0:T(8,128)(2,1)} %bitcast.38) | data formatting | bytes 221184 | tf_op jit(solution)/shard_map/all_to_all | solution.py:50
  72.0 35.5 %all-gather.2.cloned.1.call-done = bf16[2,4,64,8,256]{4,0,3,2,1:T(2,128)(2,1)} async-done(((bf16[2,4,4,8,256]{4,0,3,2,1:T(2,128)(2,1)}), bf16[2,4,64,8,256]{4,0,3,2,1:T(2,128)(2,1)}) %all-gather.2.cloned.1.call-update) | async-done | bytes 2097168 | tf_op jit(solution)/shard_map/all_gather | solution.py:49
  107.5 13.9 %fusion = bf16[2,2,64,8,8]{4,0,3,2,1:T(2,128)(2,1)S(1)} fusion(bf16[2,4,64,8,256]{4,0,3,2,1:T(2,128)(2,1)} %all-gather.2.cloned.1.call-done, bf16[3,3,3,256,8]{3,4,2,1,0:T(8,128)(2,1)S(1)} %all_to_all.19), kind=kOutput, calls=%fused_computation.2 | convolution fusion | flops 205488128 | bytes 2240512 | tf_op jit(solution)/shard_map/conv_general_dilated | solution.py:27
  121.6 2.1 %collective-permute-start.2 = (bf16[2,1,64,8,8]{4,0,3,2,1:T(2,128)(2,1)S(1)}, bf16[2,1,64,8,8]{4,0,3,2,1:T(2,128)(2,1)S(1)}, u32[]{:S(2)}, u32[]{:S(2)}) collective-permute-start(bf16[2,1,64,8,8]{4,0,3,2,1:T(2,128)(2,1)S(1)} %slice.14), channel_id=1, source_target_pairs={{0,32},{32,64},{64,96},{96,128},{128,160},{160,192},{192,224},{224... | collective-permute-start | bytes 49160 | tf_op jit(solution)/shard_map/ppermute | solution.py:23
  123.7 9.5 %collective-permute-done.2 = bf16[2,1,64,8,8]{4,0,3,2,1:T(2,128)(2,1)S(1)} collective-permute-done((bf16[2,1,64,8,8]{4,0,3,2,1:T(2,128)(2,1)S(1)}, bf16[2,1,64,8,8]{4,0,3,2,1:T(2,128)(2,1)S(1)}, u32[]{:S(2)}, u32[]{:S(2)}) %collective-permute-start.2) | collective-permute-done | bytes 16416 | tf_op jit(solution)/shard_map/ppermute | solution.py:23
  133.2 1.9 %fusion.1 = f32[256,2,1,32,4]{0,1,4,3,2:T(2,128)S(1)} fusion(bf16[3,3,3,8,256]{4,3,2,1,0:T(8,128)(2,1)S(1)} %copy-done, bf16[2,2,64,8,8]{4,0,3,2,1:T(2,128)(2,1)S(1)} %fusion, bf16[2,1,64,8,8]{4,0,3,2,1:T(2,128)(2,1)S(1)} %collective-permute-done.2), kind=kOutput, calls=%fused_computation.4 | convolution fusion | flops 25780224 | bytes 421888 | tf_op jit(solution)/shard_map/conv_general_dilated | solution.py:27
  135.1 0.4 copy.42
  135.6 1.9 %collective-permute-start.3 = (f32[16,8,2,1,32,4]{4,1,5,3,2,0:T(8,128)S(1)}, f32[16,8,2,1,32,4]{4,1,5,3,2,0:T(8,128)S(1)}, u32[]{:S(2)}, u32[]{:S(2)}) collective-permute-start(f32[16,8,2,1,32,4]{4,1,5,3,2,0:T(8,128)S(1)} %bitcast.40), channel_id=1, source_target_pairs={{0,1},{1,0},{2,3},{3,2},{4,5},{5,4},{6,7},{7,6},{8,9},{9,8},{10,11... | collective-permute-start | bytes 393224 | tf_op jit(solution)/shard_map/ppermute | solution.py:43
  137.6 1.9 %collective-permute-done.3 = f32[16,8,2,1,32,4]{4,1,5,3,2,0:T(8,128)S(1)} collective-permute-done((f32[16,8,2,1,32,4]{4,1,5,3,2,0:T(8,128)S(1)}, f32[16,8,2,1,32,4]{4,1,5,3,2,0:T(8,128)S(1)}, u32[]{:S(2)}, u32[]{:S(2)}) %collective-permute-start.3) | collective-permute-done | bytes 131104 | tf_op jit(solution)/shard_map/ppermute | solution.py:43
  139.5 0.3 reshape.10
  139.8 21.9 %all_to_all.24 = f32[16,1,2048]{2,1,0:T(1,128)S(1)} all-to-all(f32[16,1,2048]{2,1,0:T(1,128)S(1)} %reshape.10), channel_id=1, replica_groups=mesh['col'=32,'z'=16,'core'=2] {'z'}, dimensions={0} | all-to-all | bytes 262144 | tf_op jit(solution)/shard_map/all_to_all | solution.py:44
  161.6 0.5 broadcast.4
  162.2 1.0 reduce.1
  163.3 0.6 fusion.3
  (13 shorter events, 0.8 us)
Async XLA Ops:
  6.5 126.7 %copy-start = (bf16[3,3,3,8,256]{4,3,2,1,0:T(8,128)(2,1)S(1)}, bf16[3,3,3,8,256]{4,3,2,1,0:T(8,128)(2,1)}, u32[]{:S(2)}) copy-start(bf16[3,3,3,8,256]{4,3,2,1,0:T(8,128)(2,1)} %param.5) | copy-start | bytes 331780
  6.5 100.9 %all-gather.2.cloned.1.call-start = ((), (), s32[]{:S(2)}) async-start(), calls=%async_computation.2 | async-start | bytes 2228224 | tf_op jit(solution)/shard_map/all_gather | solution.py:49
  7.4 6.5 %collective-permute-start.1 = (bf16[2,1,2,8,256]{4,0,3,2,1:T(2,128)(2,1)S(1)}, bf16[2,1,2,8,256]{4,0,3,2,1:T(2,128)(2,1)S(1)}, u32[]{:S(2)}, u32[]{:S(2)}) collective-permute-start(bf16[2,1,2,8,256]{4,0,3,2,1:T(2,128)(2,1)S(1)} %get-tuple-element.8), channel_id=1, source_target_pairs={{32,0},{64,32},{96,64},{128,96},{160,128},{192,160},{224,192},{256... | collective-permute-start | bytes 49160 | tf_op jit(solution)/shard_map/ppermute | solution.py:15
  12.0 9.0 %collective-permute-start = (bf16[2,1,2,8,256]{4,0,3,2,1:T(2,128)(2,1)S(1)}, bf16[2,1,2,8,256]{4,0,3,2,1:T(2,128)(2,1)S(1)}, u32[]{:S(2)}, u32[]{:S(2)}) collective-permute-start(bf16[2,1,2,8,256]{4,0,3,2,1:T(2,128)(2,1)S(1)} %get-tuple-element.7), channel_id=1, source_target_pairs={{0,32},{32,64},{64,96},{96,128},{128,160},{160,192},{192,224},{224... | collective-permute-start | bytes 49160 | tf_op jit(solution)/shard_map/ppermute | solution.py:12
  121.6 11.6 %collective-permute-start.2 = (bf16[2,1,64,8,8]{4,0,3,2,1:T(2,128)(2,1)S(1)}, bf16[2,1,64,8,8]{4,0,3,2,1:T(2,128)(2,1)S(1)}, u32[]{:S(2)}, u32[]{:S(2)}) collective-permute-start(bf16[2,1,64,8,8]{4,0,3,2,1:T(2,128)(2,1)S(1)} %slice.14), channel_id=1, source_target_pairs={{0,32},{32,64},{64,96},{96,128},{128,160},{160,192},{192,224},{224... | collective-permute-start | bytes 49160 | tf_op jit(solution)/shard_map/ppermute | solution.py:23
  135.6 3.8 %collective-permute-start.3 = (f32[16,8,2,1,32,4]{4,1,5,3,2,0:T(8,128)S(1)}, f32[16,8,2,1,32,4]{4,1,5,3,2,0:T(8,128)S(1)}, u32[]{:S(2)}, u32[]{:S(2)}) collective-permute-start(f32[16,8,2,1,32,4]{4,1,5,3,2,0:T(8,128)S(1)} %bitcast.40), channel_id=1, source_target_pairs={{0,1},{1,0},{2,3},{3,2},{4,5},{5,4},{6,7},{7,6},{8,9},{9,8},{10,11... | collective-permute-start | bytes 393224 | tf_op jit(solution)/shard_map/ppermute | solution.py:43
Sparse Core Ops, SparseCore 0:
  23.2 84.2 all-gather.1

commit v4 on v3

--- a/solution.py
+++ b/solution.py
@@ -44,9 +44,23 @@
     return lax.all_to_all(half, "z", 0, 0, tiled=True).sum(axis=0)
 
 
+def gathered_rows(block, axis):
+    peers = lax.axis_size(axis)
+    me = lax.axis_index(axis)
+    rows = jnp.transpose(block, (2, 0, 1, 3, 4))[None]
+    for bit in reversed(range(peers.bit_length() - 1)):
+        pairs = [(i, i ^ (1 << bit)) for i in range(peers)]
+        other = lax.ppermute(rows, axis, pairs)
+        low = (me // (1 << bit)) % 2 == 0
+        rows = jnp.where(low, jnp.stack([rows, other], 1), jnp.stack([other, rows], 1))
+        rows = rows.reshape((-1,) + rows.shape[2:])
+    rows = rows.reshape((-1,) + rows.shape[2:])
+    return jnp.transpose(rows, (1, 2, 0, 3, 4))
+
+
 def per_device(inputs, first_filters, second_filters):
     padded = extended(inputs, (("col", 1),), 1)
-    gathered = lax.all_gather(lax.all_gather(padded, "core", axis=2, tiled=True), "z", axis=2, tiled=True)
+    gathered = gathered_rows(padded, ("z", "core"))
     own_first = lax.all_to_all(first_filters, ("z", "core"), split_axis=4, concat_axis=3, tiled=True)
     hidden = jnp.maximum(convolve(gathered, own_first, 1, 1), 0.0).astype(jnp.bfloat16)
     lower_plane = passed_along(hidden[:, -1:], "col", 1)

time: 171 us -> 184 us (1.076)
  starting transfers between devices: 10.5 us -> 59 us
  blocking collectives: 60.5 us -> 17 us
  waiting for transfers between devices: 53.9 us -> 67.6 us
  between operations: 13.5 us -> 0.39 us
  local copies, waits for them, and re-layouts: 14.7 us -> 18.8 us
  other arithmetic: 1.79 us -> 3.94 us
    ppermute x0 -> x5, waiting for transfers between devices: none -> 38.6 us  [gathered_rows(): other = lax.ppermute(rows, axis, pairs)]
    all_to_all x1 -> x0, blocking collectives: 36.6 us -> none  [per_device(): lax.all_to_all(first_filters, ('z', 'core'), split_axis=4, concat_axis=3,...]
    all_gather x1 -> x0, waiting for transfers between devices: 35.5 us -> none  [per_device(): lax.all_gather(lax.all_gather(padded, 'core', axis=2, tiled=True), 'z', a...]
    ppermute x0 -> x5, starting transfers between devices: none -> 32.1 us  [gathered_rows(): other = lax.ppermute(rows, axis, pairs)]
    all_to_all x0 -> x1, waiting for transfers between devices: none -> 16.3 us  [per_device(): lax.all_to_all(first_filters, ('z', 'core'), split_axis=4, concat_axis=3,...]
    all_to_all x0 -> x1, starting transfers between devices: none -> 13.7 us  [per_device(): lax.all_to_all(first_filters, ('z', 'core'), split_axis=4, concat_axis=3,...]
    ppermute x1, waiting for transfers between devices: 7.01 us -> 0.01 us  [extended(): lax.ppermute(lax.slice_in_dim(block, block.shape[dim] - width, None, axis...]
    all_to_all x1, blocking collectives: 21.9 us -> 17 us  [reduce_scattered(): return lax.all_to_all(half, 'z', 0, 0, tiled=True).sum(axis=0)]
  transfers between devices with their start and end apart: 5 -> 10, of which waited for: 4 -> 8; matrix products, arithmetic and copies ran while one was open for 5% -> 7% of each run, Pallas kernels for 0% -> 0%
where the time goes in v4:
time: 184 us; the launch traced here: 183 us
  waiting for transfers between devices  67.6 us (37%)
  starting transfers between devices  59 us (32%)
  local copies, waits for them, and re-layouts  18.8 us (10%)
  blocking collectives  17 us (9%)
  matrix products  15.8 us (9%)
  other arithmetic  3.94 us (2%)
    ppermute x5, waiting for transfers between devices, gathered_rows(): other = lax.ppermute(rows, axis, pairs)  38.6 us
    ppermute x5, starting transfers between devices, gathered_rows(): other = lax.ppermute(rows, axis, pairs)  32.1 us
    all_to_all x1, blocking collectives, reduce_scattered(): return lax.all_to_all(half, 'z', 0, 0, tiled=True).sum(axis=0)  17 us
    all_to_all x1, waiting for transfers between devices, per_device(): lax.all_to_all(first_filters, ('z', 'core'), split_axis=4, concat_axis=3,...  16.3 us
    conv_general_dilated x2, matrix products, convolve(): lax.conv_general_dilated(volume, kernel, (stride, stride, stride), ((0, 0...  15.8 us
    all_to_all x1, starting transfers between devices, per_device(): lax.all_to_all(first_filters, ('z', 'core'), split_axis=4, concat_axis=3,...  13.7 us
    unnamed x11, local copies, waits for them, and re-layouts  11 us
    ppermute x1, waiting for transfers between devices, passed_along(): return lax.ppermute(array, axis, pairs)  10.2 us
  transfers between devices with their start and end apart: 10, of which 8 were waited for; matrix products, arithmetic and copies ran while one was open for 7% of the time, Pallas kernels for 0%

profile of v4, /device:TPU:32, one launch (start us, length us, event | category | flops | bytes accessed | tf_op | source)
XLA Modules:
  0.0 182.5 jit_solution(16720447945325639099)
XLA Ops:
  0.8 3.4 %collective-permute-start = (bf16[2,1,2,8,256]{4,3,1,0,2:T(8,128)(2,1)S(1)}, bf16[2,1,2,8,256]{4,3,1,0,2:T(8,128)(2,1)S(1)}, u32[]{:S(2)}, u32[]{:S(2)}) collective-permute-start(bf16[2,1,2,8,256]{4,3,1,0,2:T(8,128)(2,1)S(1)} %copy.100), channel_id=1, source_target_pairs={{0,32},{32,64},{64,96},{96,128},{128,160},{160,192},{192,224},{224... | collective-permute-start | bytes 49160 | tf_op jit(solution)/shard_map/ppermute | solution.py:12
  4.2 5.8 %collective-permute-start.1 = (bf16[2,1,2,8,256]{4,3,1,0,2:T(8,128)(2,1)S(1)}, bf16[2,1,2,8,256]{4,3,1,0,2:T(8,128)(2,1)S(1)}, u32[]{:S(2)}, u32[]{:S(2)}) collective-permute-start(bf16[2,1,2,8,256]{4,3,1,0,2:T(8,128)(2,1)S(1)} %copy.101), channel_id=1, source_target_pairs={{32,0},{64,32},{96,64},{128,96},{160,128},{192,160},{224,192},{256... | collective-permute-start | bytes 49160 | tf_op jit(solution)/shard_map/ppermute | solution.py:15
  11.4 19.3 %collective-permute-start.2 = (bf16[1,2,2,4,8,256]{5,4,3,2,1,0:T(8,128)(2,1)S(1)}, bf16[1,2,2,4,8,256]{5,4,3,2,1,0:T(8,128)(2,1)S(1)}, u32[]{:S(2)}, u32[]{:S(2)}) collective-permute-start(bf16[1,2,2,4,8,256]{5,4,3,2,1,0:T(8,128)(2,1)S(1)} %bitcast.65), channel_id=1, source_target_pairs={{0,16},{1,17},{2,18},{3,19},{4,20},{5,21},{6,22},{7,23},{8,24},{9,... | collective-permute-start | bytes 196616 | tf_op jit(solution)/shard_map/ppermute | solution.py:53
  30.8 3.4 %collective-permute-done.2 = bf16[1,2,2,4,8,256]{5,4,3,2,1,0:T(8,128)(2,1)S(1)} collective-permute-done((bf16[1,2,2,4,8,256]{5,4,3,2,1,0:T(8,128)(2,1)S(1)}, bf16[1,2,2,4,8,256]{5,4,3,2,1,0:T(8,128)(2,1)S(1)}, u32[]{:S(2)}, u32[]{:S(2)}) %collective-permute-start.2) | collective-permute-done | bytes 65568 | tf_op jit(solution)/shard_map/ppermute | solution.py:53
  34.2 7.0 %collective-permute-start.3 = (bf16[2,2,2,4,8,256]{5,4,3,2,1,0:T(8,128)(2,1)S(1)}, bf16[2,2,2,4,8,256]{5,4,3,2,1,0:T(8,128)(2,1)S(1)}, u32[]{:S(2)}, u32[]{:S(2)}) collective-permute-start(bf16[2,2,2,4,8,256]{5,4,3,2,1,0:T(8,128)(2,1)S(1)} %maximum_select_fusion.5), channel_id=1, source_target_pairs={{0,8},{1,9},{2,10},{3,11},{4,12},{5,13},{6,14},{7,15},{8,0},{9,1},... | collective-permute-start | bytes 393224 | tf_op jit(solution)/shard_map/ppermute | solution.py:53
  41.2 9.9 %collective-permute-done.3 = bf16[2,2,2,4,8,256]{5,4,3,2,1,0:T(8,128)(2,1)S(1)} collective-permute-done((bf16[2,2,2,4,8,256]{5,4,3,2,1,0:T(8,128)(2,1)S(1)}, bf16[2,2,2,4,8,256]{5,4,3,2,1,0:T(8,128)(2,1)S(1)}, u32[]{:S(2)}, u32[]{:S(2)}) %collective-permute-start.3) | collective-permute-done | bytes 131104 | tf_op jit(solution)/shard_map/ppermute | solution.py:53
  51.2 1.9 %collective-permute-start.4 = (bf16[4,2,2,4,8,256]{5,4,3,2,1,0:T(8,128)(2,1)S(1)}, bf16[4,2,2,4,8,256]{5,4,3,2,1,0:T(8,128)(2,1)S(1)}, u32[]{:S(2)}, u32[]{:S(2)}) collective-permute-start(bf16[4,2,2,4,8,256]{5,4,3,2,1,0:T(8,128)(2,1)S(1)} %bitcast.61), channel_id=1, source_target_pairs={{0,4},{1,5},{2,6},{3,7},{4,0},{5,1},{6,2},{7,3},{8,12},{9,13},{10,... | collective-permute-start | bytes 786440 | tf_op jit(solution)/shard_map/ppermute | solution.py:53
  53.1 11.5 %collective-permute-done.4 = bf16[4,2,2,4,8,256]{5,4,3,2,1,0:T(8,128)(2,1)S(1)} collective-permute-done((bf16[4,2,2,4,8,256]{5,4,3,2,1,0:T(8,128)(2,1)S(1)}, bf16[4,2,2,4,8,256]{5,4,3,2,1,0:T(8,128)(2,1)S(1)}, u32[]{:S(2)}, u32[]{:S(2)}) %collective-permute-start.4) | collective-permute-done | bytes 262176 | tf_op jit(solution)/shard_map/ppermute | solution.py:53
  64.7 1.9 %collective-permute-start.5 = (bf16[8,2,2,4,8,256]{5,4,3,2,1,0:T(8,128)(2,1)S(1)}, bf16[8,2,2,4,8,256]{5,4,3,2,1,0:T(8,128)(2,1)S(1)}, u32[]{:S(2)}, u32[]{:S(2)}) collective-permute-start(bf16[8,2,2,4,8,256]{5,4,3,2,1,0:T(8,128)(2,1)S(1)} %bitcast.58), channel_id=1, source_target_pairs={{0,2},{1,3},{2,0},{3,1},{4,6},{5,7},{6,4},{7,5},{8,10},{9,11},{10,... | collective-permute-start | bytes 1572872 | tf_op jit(solution)/shard_map/ppermute | solution.py:53
  66.7 13.8 %collective-permute-done.5 = bf16[8,2,2,4,8,256]{5,4,3,2,1,0:T(8,128)(2,1)S(1)} collective-permute-done((bf16[8,2,2,4,8,256]{5,4,3,2,1,0:T(8,128)(2,1)S(1)}, bf16[8,2,2,4,8,256]{5,4,3,2,1,0:T(8,128)(2,1)S(1)}, u32[]{:S(2)}, u32[]{:S(2)}) %collective-permute-start.5) | collective-permute-done | bytes 524320 | tf_op jit(solution)/shard_map/ppermute | solution.py:53
  80.8 1.9 %collective-permute-start.6 = (bf16[16,2,2,4,8,256]{5,4,3,2,1,0:T(8,128)(2,1)S(1)}, bf16[16,2,2,4,8,256]{5,4,3,2,1,0:T(8,128)(2,1)}, u32[]{:S(2)}, u32[]{:S(2)}) collective-permute-start(bf16[16,2,2,4,8,256]{5,4,3,2,1,0:T(8,128)(2,1)S(1)} %bitcast.55), channel_id=1, source_target_pairs={{0,1},{1,0},{2,3},{3,2},{4,5},{5,4},{6,7},{7,6},{8,9},{9,8},{10,11... | collective-permute-start | bytes 3145736 | tf_op jit(solution)/shard_map/ppermute | solution.py:53
  82.7 3.3 %copy.80 = bf16[3,3,3,8,256]{3,2,1,0,4:T(4,128)(2,1)S(1)} copy(bf16[3,3,3,8,256]{4,3,2,1,0:T(8,128)(2,1)} %param.4) | data formatting | bytes 221184 | tf_op args[1]
  86.0 2.6 %reshape.165 = bf16[32,2,864]{2,1,0:T(2,128)(2,1)} reshape(bf16[256,3,3,3,8]{4,3,2,1,0:T(4,128)(2,1)S(1)} %bitcast.53) | data formatting | bytes 221184
  88.6 13.7 %all-to-all-start = ((bf16[32,2,864]{2,1,0:T(2,128)(2,1)}), bf16[32,2,864]{2,1,0:T(2,128)(2,1)}, u32[]{:S(2)}, u32[]{:S(2)}) async-start(bf16[32,2,864]{2,1,0:T(2,128)(2,1)} %reshape.165), calls=%async_computation | async-start | bytes 229376 | tf_op jit(solution)/shard_map/all_to_all | solution.py:64
  102.3 16.3 %all-to-all-done = bf16[32,2,864]{2,1,0:T(2,128)(2,1)} async-done(((bf16[32,2,864]{2,1,0:T(2,128)(2,1)}), bf16[32,2,864]{2,1,0:T(2,128)(2,1)}, u32[]{:S(2)}, u32[]{:S(2)}) %all-to-all-start) | async-done | bytes 110624 | tf_op jit(solution)/shard_map/all_to_all | solution.py:64
  118.6 3.9 %reshape.166 = bf16[256,3,3,3,8]{4,3,2,1,0:T(4,128)(2,1)S(1)} reshape(bf16[32,2,864]{2,1,0:T(2,128)(2,1)} %all-to-all-done) | data formatting | bytes 221184
  122.5 2.1 %copy.104 = bf16[3,3,3,8,32,8]{3,4,5,2,1,0:T(8,128)(2,1)} copy(bf16[3,3,3,8,32,8]{3,2,1,0,5,4:T(4,128)(2,1)S(1)} %bitcast.52) | data formatting | bytes 221184 | tf_op jit(solution)/shard_map/all_to_all | solution.py:64
  124.6 3.4 %all_to_all.19 = bf16[3,3,3,256,8]{3,4,2,1,0:T(8,128)(2,1)S(1)} reshape(bf16[3,3,3,32,8,8]{4,3,5,2,1,0:T(8,128)(2,1)} %bitcast.54) | data formatting | bytes 221184 | tf_op jit(solution)/shard_map/all_to_all | solution.py:64
  128.1 1.9 %maximum_select_fusion = bf16[16,2,2,2,4,8,256]{6,5,4,3,2,0,1:T(8,128)(2,1)S(1)} fusion(bf16[16,1,2,2,4,8,256]{6,5,4,3,2,0,1:T(8,128)(2,1)} %bitcast.15, bf16[16,1,2,2,4,8,256]{6,5,4,3,2,0,1:T(8,128)(2,1)S(1)} %bitcast.56, pred[]{:T(512)S(6)} %eq.21), kind=kLoop, calls=%fused_computation | loop fusion | flops 3145728 | bytes 4194305 | tf_op jit(solution)/shard_map/jit(_where)/select_n | solution.py:55
  130.2 13.9 %fusion.5 = bf16[2,2,64,8,8]{4,0,3,2,1:T(2,128)(2,1)S(1)} fusion(bf16[3,3,3,256,8]{3,4,2,1,0:T(8,128)(2,1)S(1)} %all_to_all.19, bf16[64,2,4,8,256]{4,3,2,1,0:T(8,128)(2,1)S(1)} %bitcast.60), kind=kOutput, calls=%fused_computation.5 | convolution fusion | flops 205488128 | bytes 2240512 | tf_op jit(solution)/shard_map/conv_general_dilated | solution.py:27
  144.3 2.1 %collective-permute-start.7 = (bf16[2,1,64,8,8]{4,0,3,2,1:T(2,128)(2,1)S(1)}, bf16[2,1,64,8,8]{4,0,3,2,1:T(2,128)(2,1)S(1)}, u32[]{:S(2)}, u32[]{:S(2)}) collective-permute-start(bf16[2,1,64,8,8]{4,0,3,2,1:T(2,128)(2,1)S(1)} %slice.14), channel_id=1, source_target_pairs={{0,32},{32,64},{64,96},{96,128},{128,160},{160,192},{192,224},{224... | collective-permute-start | bytes 49160 | tf_op jit(solution)/shard_map/ppermute | solution.py:23
  146.4 10.2 %collective-permute-done.7 = bf16[2,1,64,8,8]{4,0,3,2,1:T(2,128)(2,1)S(1)} collective-permute-done((bf16[2,1,64,8,8]{4,0,3,2,1:T(2,128)(2,1)S(1)}, bf16[2,1,64,8,8]{4,0,3,2,1:T(2,128)(2,1)S(1)}, u32[]{:S(2)}, u32[]{:S(2)}) %collective-permute-start.7) | collective-permute-done | bytes 16416 | tf_op jit(solution)/shard_map/ppermute | solution.py:23
  156.6 1.9 %fusion.8 = f32[256,2,1,32,4]{0,1,4,3,2:T(2,128)S(1)} fusion(bf16[3,3,3,8,256]{4,3,2,1,0:T(8,128)(2,1)S(1)} %copy-done, bf16[2,2,64,8,8]{4,0,3,2,1:T(2,128)(2,1)S(1)} %fusion.5, bf16[2,1,64,8,8]{4,0,3,2,1:T(2,128)(2,1)S(1)} %collective-permute-done.7), kind=kOutput, calls=%fused_computation.8 | convolution fusion | flops 25780224 | bytes 421888 | tf_op jit(solution)/shard_map/conv_general_dilated | solution.py:27
  163.2 17.0 %all_to_all.23 = f32[16,1,2048]{2,1,0:T(1,128)S(1)} all-to-all(f32[16,1,2048]{2,1,0:T(1,128)S(1)} %reshape.167), channel_id=1, replica_groups=mesh['col'=32,'z'=16,'core'=2] {'z'}, dimensions={0} | all-to-all | bytes 262144 | tf_op jit(solution)/shard_map/all_to_all | solution.py:44
  (32 shorter events, 9.9 us)
Async XLA Ops:
  0.0 156.6 %copy-start = (bf16[3,3,3,8,256]{4,3,2,1,0:T(8,128)(2,1)S(1)}, bf16[3,3,3,8,256]{4,3,2,1,0:T(8,128)(2,1)}, u32[]{:S(2)}) copy-start(bf16[3,3,3,8,256]{4,3,2,1,0:T(8,128)(2,1)} %param.5) | copy-start | bytes 331780
  0.8 9.2 %collective-permute-start = (bf16[2,1,2,8,256]{4,3,1,0,2:T(8,128)(2,1)S(1)}, bf16[2,1,2,8,256]{4,3,1,0,2:T(8,128)(2,1)S(1)}, u32[]{:S(2)}, u32[]{:S(2)}) collective-permute-start(bf16[2,1,2,8,256]{4,3,1,0,2:T(8,128)(2,1)S(1)} %copy.100), channel_id=1, source_target_pairs={{0,32},{32,64},{64,96},{96,128},{128,160},{160,192},{192,224},{224... | collective-permute-start | bytes 49160 | tf_op jit(solution)/shard_map/ppermute | solution.py:12
  4.2 7.2 %collective-permute-start.1 = (bf16[2,1,2,8,256]{4,3,1,0,2:T(8,128)(2,1)S(1)}, bf16[2,1,2,8,256]{4,3,1,0,2:T(8,128)(2,1)S(1)}, u32[]{:S(2)}, u32[]{:S(2)}) collective-permute-start(bf16[2,1,2,8,256]{4,3,1,0,2:T(8,128)(2,1)S(1)} %copy.101), channel_id=1, source_target_pairs={{32,0},{64,32},{96,64},{128,96},{160,128},{192,160},{224,192},{256... | collective-permute-start | bytes 49160 | tf_op jit(solution)/shard_map/ppermute | solution.py:15
  11.4 22.8 %collective-permute-start.2 = (bf16[1,2,2,4,8,256]{5,4,3,2,1,0:T(8,128)(2,1)S(1)}, bf16[1,2,2,4,8,256]{5,4,3,2,1,0:T(8,128)(2,1)S(1)}, u32[]{:S(2)}, u32[]{:S(2)}) collective-permute-start(bf16[1,2,2,4,8,256]{5,4,3,2,1,0:T(8,128)(2,1)S(1)} %bitcast.65), channel_id=1, source_target_pairs={{0,16},{1,17},{2,18},{3,19},{4,20},{5,21},{6,22},{7,23},{8,24},{9,... | collective-permute-start | bytes 196616 | tf_op jit(solution)/shard_map/ppermute | solution.py:53
  34.2 17.0 %collective-permute-start.3 = (bf16[2,2,2,4,8,256]{5,4,3,2,1,0:T(8,128)(2,1)S(1)}, bf16[2,2,2,4,8,256]{5,4,3,2,1,0:T(8,128)(2,1)S(1)}, u32[]{:S(2)}, u32[]{:S(2)}) collective-permute-start(bf16[2,2,2,4,8,256]{5,4,3,2,1,0:T(8,128)(2,1)S(1)} %maximum_select_fusion.5), channel_id=1, source_target_pairs={{0,8},{1,9},{2,10},{3,11},{4,12},{5,13},{6,14},{7,15},{8,0},{9,1},... | collective-permute-start | bytes 393224 | tf_op jit(solution)/shard_map/ppermute | solution.py:53
  51.2 13.4 %collective-permute-start.4 = (bf16[4,2,2,4,8,256]{5,4,3,2,1,0:T(8,128)(2,1)S(1)}, bf16[4,2,2,4,8,256]{5,4,3,2,1,0:T(8,128)(2,1)S(1)}, u32[]{:S(2)}, u32[]{:S(2)}) collective-permute-start(bf16[4,2,2,4,8,256]{5,4,3,2,1,0:T(8,128)(2,1)S(1)} %bitcast.61), channel_id=1, source_target_pairs={{0,4},{1,5},{2,6},{3,7},{4,0},{5,1},{6,2},{7,3},{8,12},{9,13},{10,... | collective-permute-start | bytes 786440 | tf_op jit(solution)/shard_map/ppermute | solution.py:53
  64.7 15.7 %collective-permute-start.5 = (bf16[8,2,2,4,8,256]{5,4,3,2,1,0:T(8,128)(2,1)S(1)}, bf16[8,2,2,4,8,256]{5,4,3,2,1,0:T(8,128)(2,1)S(1)}, u32[]{:S(2)}, u32[]{:S(2)}) collective-permute-start(bf16[8,2,2,4,8,256]{5,4,3,2,1,0:T(8,128)(2,1)S(1)} %bitcast.58), channel_id=1, source_target_pairs={{0,2},{1,3},{2,0},{3,1},{4,6},{5,7},{6,4},{7,5},{8,10},{9,11},{10,... | collective-permute-start | bytes 1572872 | tf_op jit(solution)/shard_map/ppermute | solution.py:53
  80.8 47.3 %collective-permute-start.6 = (bf16[16,2,2,4,8,256]{5,4,3,2,1,0:T(8,128)(2,1)S(1)}, bf16[16,2,2,4,8,256]{5,4,3,2,1,0:T(8,128)(2,1)}, u32[]{:S(2)}, u32[]{:S(2)}) collective-permute-start(bf16[16,2,2,4,8,256]{5,4,3,2,1,0:T(8,128)(2,1)S(1)} %bitcast.55), channel_id=1, source_target_pairs={{0,1},{1,0},{2,3},{3,2},{4,5},{5,4},{6,7},{7,6},{8,9},{9,8},{10,11... | collective-permute-start | bytes 3145736 | tf_op jit(solution)/shard_map/ppermute | solution.py:53
  88.6 30.0 %all-to-all-start = ((bf16[32,2,864]{2,1,0:T(2,128)(2,1)}), bf16[32,2,864]{2,1,0:T(2,128)(2,1)}, u32[]{:S(2)}, u32[]{:S(2)}) async-start(bf16[32,2,864]{2,1,0:T(2,128)(2,1)} %reshape.165), calls=%async_computation | async-start | bytes 229376 | tf_op jit(solution)/shard_map/all_to_all | solution.py:64
  144.3 12.3 %collective-permute-start.7 = (bf16[2,1,64,8,8]{4,0,3,2,1:T(2,128)(2,1)S(1)}, bf16[2,1,64,8,8]{4,0,3,2,1:T(2,128)(2,1)S(1)}, u32[]{:S(2)}, u32[]{:S(2)}) collective-permute-start(bf16[2,1,64,8,8]{4,0,3,2,1:T(2,128)(2,1)S(1)} %slice.14), channel_id=1, source_target_pairs={{0,32},{32,64},{64,96},{96,128},{128,160},{160,192},{192,224},{224... | collective-permute-start | bytes 49160 | tf_op jit(solution)/shard_map/ppermute | solution.py:23
  159.1 3.8 %collective-permute-start.8 = (f32[16,8,2,1,32,4]{4,1,5,3,2,0:T(8,128)S(1)}, f32[16,8,2,1,32,4]{4,1,5,3,2,0:T(8,128)S(1)}, u32[]{:S(2)}, u32[]{:S(2)}) collective-permute-start(f32[16,8,2,1,32,4]{4,1,5,3,2,0:T(8,128)S(1)} %bitcast.64), channel_id=1, source_target_pairs={{0,1},{1,0},{2,3},{3,2},{4,5},{5,4},{6,7},{7,6},{8,9},{9,8},{10,11... | collective-permute-start | bytes 393224 | tf_op jit(solution)/shard_map/ppermute | solution.py:43

commit v5 on v4

--- a/solution.py
+++ b/solution.py
@@ -44,25 +44,33 @@
     return lax.all_to_all(half, "z", 0, 0, tiled=True).sum(axis=0)
 
 
-def gathered_rows(block, axis):
+def gathered(block, kernel, axis):
     peers = lax.axis_size(axis)
     me = lax.axis_index(axis)
     rows = jnp.transpose(block, (2, 0, 1, 3, 4))[None]
+    taps, width, filters = kernel.shape[:3], kernel.shape[3], kernel.shape[4] // peers
+    held = kernel.reshape((-1, width, peers, filters)).transpose(2, 0, 1, 3)[None]
     for bit in reversed(range(peers.bit_length() - 1)):
         pairs = [(i, i ^ (1 << bit)) for i in range(peers)]
-        other = lax.ppermute(rows, axis, pairs)
-        low = (me // (1 << bit)) % 2 == 0
+        mine = (me // (1 << bit)) % 2
+        low = mine == 0
+        split = held.reshape(held.shape[:1] + (2, -1) + held.shape[2:])
+        keep = lax.dynamic_index_in_dim(split, mine, axis=1, keepdims=False)
+        give = lax.dynamic_index_in_dim(split, 1 - mine, axis=1, keepdims=False)
+        other, got = lax.ppermute((rows, give), axis, pairs)
         rows = jnp.where(low, jnp.stack([rows, other], 1), jnp.stack([other, rows], 1))
         rows = rows.reshape((-1,) + rows.shape[2:])
+        held = jnp.where(low, jnp.stack([keep, got], 1), jnp.stack([got, keep], 1))
+        held = held.reshape((-1,) + held.shape[2:])
     rows = rows.reshape((-1,) + rows.shape[2:])
-    return jnp.transpose(rows, (1, 2, 0, 3, 4))
+    own = held.reshape((peers,) + held.shape[2:]).transpose(1, 0, 2, 3)
+    return jnp.transpose(rows, (1, 2, 0, 3, 4)), own.reshape(taps + (peers * width, filters))
 
 
 def per_device(inputs, first_filters, second_filters):
     padded = extended(inputs, (("col", 1),), 1)
-    gathered = gathered_rows(padded, ("z", "core"))
-    own_first = lax.all_to_all(first_filters, ("z", "core"), split_axis=4, concat_axis=3, tiled=True)
-    hidden = jnp.maximum(convolve(gathered, own_first, 1, 1), 0.0).astype(jnp.bfloat16)
+    slab, own_first = gathered(padded, first_filters, ("z", "core"))
+    hidden = jnp.maximum(convolve(slab, own_first, 1, 1), 0.0).astype(jnp.bfloat16)
     lower_plane = passed_along(hidden[:, -1:], "col", 1)
     stacked = jnp.concatenate([lower_plane, hidden], axis=1)
     partial = convolve(stacked, second_filters, 2, 1, out_spec="CNDHW")

time: 184 us -> 230 us (1.25)
  starting transfers between devices: 59 us -> 98.3 us
  blocking collectives: 17 us -> 23.5 us
    ppermute x5 -> x10, starting transfers between devices: 32.1 us -> 85.1 us  [gathered(): other, got = lax.ppermute((rows, give), axis, pairs)]
    all_to_all x1 -> x0, waiting for transfers between devices: 16.3 us -> none  [per_device(): lax.all_to_all(first_filters, ('z', 'core'), split_axis=4, concat_axis=3,...]
    ppermute x5 -> x10, waiting for transfers between devices: 38.6 us -> 53.8 us  [gathered(): other, got = lax.ppermute((rows, give), axis, pairs)]
    all_to_all x1 -> x0, starting transfers between devices: 13.7 us -> none  [per_device(): lax.all_to_all(first_filters, ('z', 'core'), split_axis=4, concat_axis=3,...]
    unnamed x11, local copies, waits for them, and re-layouts: 11 us -> 3.54 us
    all_to_all x1, blocking collectives: 17 us -> 23.5 us  [reduce_scattered(): return lax.all_to_all(half, 'z', 0, 0, tiled=True).sum(axis=0)]
    all_to_all x2 -> x0, local copies, waits for them, and re-layouts: 5.51 us -> none  [per_device(): lax.all_to_all(first_filters, ('z', 'core'), split_axis=4, concat_axis=3,...]
    reshape x0 -> x2, local copies, waits for them, and re-layouts: none -> 5.02 us  [the longest x1 2.93 us: gathered(): own.reshape(taps + (peers * width, filters))]
  transfers between devices with their start and end apart: 10 -> 14, of which waited for: 8 -> 11; matrix products, arithmetic and copies ran while one was open for 7% -> 7% of each run, Pallas kernels for 0% -> 0%
where the time goes in v5:
time: 230 us; the launch traced here: 229 us
  starting transfers between devices  98.3 us (43%)
  waiting for transfers between devices  67.8 us (29%)
  blocking collectives  23.5 us (10%)
  local copies, waits for them, and re-layouts  17.1 us (7%)
  matrix products  15.8 us (7%)
  other arithmetic  6.13 us (3%)
    ppermute x10, starting transfers between devices, gathered(): other, got = lax.ppermute((rows, give), axis, pairs)  85.1 us
    ppermute x10, waiting for transfers between devices, gathered(): other, got = lax.ppermute((rows, give), axis, pairs)  53.8 us
    all_to_all x1, blocking collectives, reduce_scattered(): return lax.all_to_all(half, 'z', 0, 0, tiled=True).sum(axis=0)  23.5 us
    conv_general_dilated x2, matrix products, convolve(): lax.conv_general_dilated(volume, kernel, (stride, stride, stride), ((0, 0...  15.8 us
    ppermute x1, waiting for transfers between devices, passed_along(): return lax.ppermute(array, axis, pairs)  11.4 us
    ppermute x1, starting transfers between devices, extended(): lax.ppermute(lax.slice_in_dim(block, 0, width, axis=dim), axis, backward)  5.76 us
  transfers between devices with their start and end apart: 14, of which 11 were waited for; matrix products, arithmetic and copies ran while one was open for 7% of the time, Pallas kernels for 0%

profile of v5, /device:TPU:32, one launch (start us, length us, event | category | flops | bytes accessed | tf_op | source)
XLA Modules:
  0.0 229.2 jit_solution(10714624805937224500)
XLA Ops:
  0.8 3.4 %collective-permute-start = (bf16[2,1,2,8,256]{4,3,1,0,2:T(8,128)(2,1)S(1)}, bf16[2,1,2,8,256]{4,3,1,0,2:T(8,128)(2,1)S(1)}, u32[]{:S(2)}, u32[]{:S(2)}) collective-permute-start(bf16[2,1,2,8,256]{4,3,1,0,2:T(8,128)(2,1)S(1)} %copy.104), channel_id=1, source_target_pairs={{0,32},{32,64},{64,96},{96,128},{128,160},{160,192},{192,224},{224... | collective-permute-start | bytes 49160 | tf_op jit(solution)/shard_map/ppermute | solution.py:12
  4.2 5.8 %collective-permute-start.1 = (bf16[2,1,2,8,256]{4,3,1,0,2:T(8,128)(2,1)S(1)}, bf16[2,1,2,8,256]{4,3,1,0,2:T(8,128)(2,1)S(1)}, u32[]{:S(2)}, u32[]{:S(2)}) collective-permute-start(bf16[2,1,2,8,256]{4,3,1,0,2:T(8,128)(2,1)S(1)} %copy.105), channel_id=1, source_target_pairs={{32,0},{64,32},{96,64},{128,96},{160,128},{192,160},{224,192},{256... | collective-permute-start | bytes 49160 | tf_op jit(solution)/shard_map/ppermute | solution.py:15
  11.4 19.3 %collective-permute-start.2 = (bf16[1,2,2,4,8,256]{5,4,3,2,1,0:T(8,128)(2,1)S(1)}, bf16[1,2,2,4,8,256]{5,4,3,2,1,0:T(8,128)(2,1)S(1)}, u32[]{:S(2)}, u32[]{:S(2)}) collective-permute-start(bf16[1,2,2,4,8,256]{5,4,3,2,1,0:T(8,128)(2,1)S(1)} %bitcast.86), channel_id=1, source_target_pairs={{0,16},{1,17},{2,18},{3,19},{4,20},{5,21},{6,22},{7,23},{8,24},{9,... | collective-permute-start | bytes 196616 | tf_op jit(solution)/shard_map/ppermute | solution.py:60
  30.8 3.4 %collective-permute-done.2 = bf16[1,2,2,4,8,256]{5,4,3,2,1,0:T(8,128)(2,1)S(1)} collective-permute-done((bf16[1,2,2,4,8,256]{5,4,3,2,1,0:T(8,128)(2,1)S(1)}, bf16[1,2,2,4,8,256]{5,4,3,2,1,0:T(8,128)(2,1)S(1)}, u32[]{:S(2)}, u32[]{:S(2)}) %collective-permute-start.2) | collective-permute-done | bytes 65568 | tf_op jit(solution)/shard_map/ppermute | solution.py:60
  34.2 7.0 %collective-permute-start.3 = (bf16[2,2,2,4,8,256]{5,4,3,2,1,0:T(8,128)(2,1)S(1)}, bf16[2,2,2,4,8,256]{5,4,3,2,1,0:T(8,128)(2,1)S(1)}, u32[]{:S(2)}, u32[]{:S(2)}) collective-permute-start(bf16[2,2,2,4,8,256]{5,4,3,2,1,0:T(8,128)(2,1)S(1)} %maximum_select_fusion.10), channel_id=1, source_target_pairs={{0,8},{1,9},{2,10},{3,11},{4,12},{5,13},{6,14},{7,15},{8,0},{9,1},... | collective-permute-start | bytes 393224 | tf_op jit(solution)/shard_map/ppermute | solution.py:60
  41.2 9.9 %collective-permute-done.3 = bf16[2,2,2,4,8,256]{5,4,3,2,1,0:T(8,128)(2,1)S(1)} collective-permute-done((bf16[2,2,2,4,8,256]{5,4,3,2,1,0:T(8,128)(2,1)S(1)}, bf16[2,2,2,4,8,256]{5,4,3,2,1,0:T(8,128)(2,1)S(1)}, u32[]{:S(2)}, u32[]{:S(2)}) %collective-permute-start.3) | collective-permute-done | bytes 131104 | tf_op jit(solution)/shard_map/ppermute | solution.py:60
  53.1 11.5 %collective-permute-done.4 = bf16[4,2,2,4,8,256]{5,4,3,2,1,0:T(8,128)(2,1)S(1)} collective-permute-done((bf16[4,2,2,4,8,256]{5,4,3,2,1,0:T(8,128)(2,1)S(1)}, bf16[4,2,2,4,8,256]{5,4,3,2,1,0:T(8,128)(2,1)S(1)}, u32[]{:S(2)}, u32[]{:S(2)}) %collective-permute-start.4) | collective-permute-done | bytes 262176 | tf_op jit(solution)/shard_map/ppermute | solution.py:60
  66.7 2.1 reshape.239
  70.0 2.3 %copy.94 = bf16[1,1,16,27,8,8]{3,5,4,2,1,0:T(8,128)(2,1)S(1)} copy(bf16[1,1,16,27,8,8]{5,2,1,4,3,0:T(8,128)(2,1)} %get-tuple-element.6) | data formatting | bytes 110592
  72.4 13.5 %collective-permute-start.7 = (bf16[1,16,27,8,8]{2,4,3,1,0:T(8,128)(2,1)S(1)}, bf16[1,16,27,8,8]{2,4,3,1,0:T(8,128)(2,1)S(1)}, u32[]{:S(2)}, u32[]{:S(2)}) collective-permute-start(bf16[1,16,27,8,8]{2,4,3,1,0:T(8,128)(2,1)S(1)} %bitcast.90), channel_id=1, source_target_pairs={{0,16},{1,17},{2,18},{3,19},{4,20},{5,21},{6,22},{7,23},{8,24},{9,... | collective-permute-start | bytes 165896 | tf_op jit(solution)/shard_map/ppermute | solution.py:60
  87.2 11.1 %collective-permute-done.7 = bf16[1,16,27,8,8]{2,4,3,1,0:T(8,128)(2,1)S(1)} collective-permute-done((bf16[1,16,27,8,8]{2,4,3,1,0:T(8,128)(2,1)S(1)}, bf16[1,16,27,8,8]{2,4,3,1,0:T(8,128)(2,1)S(1)}, u32[]{:S(2)}, u32[]{:S(2)}) %collective-permute-start.7) | collective-permute-done | bytes 55328 | tf_op jit(solution)/shard_map/ppermute | solution.py:60
  98.6 14.6 %collective-permute-start.8 = (bf16[2,8,27,8,8]{2,4,3,1,0:T(8,128)(2,1)S(1)}, bf16[2,8,27,8,8]{2,4,3,1,0:T(8,128)(2,1)S(1)}, u32[]{:S(2)}, u32[]{:S(2)}) collective-permute-start(bf16[2,8,27,8,8]{2,4,3,1,0:T(8,128)(2,1)S(1)} %get-tuple-element.16), channel_id=1, source_target_pairs={{0,8},{1,9},{2,10},{3,11},{4,12},{5,13},{6,14},{7,15},{8,0},{9,1},... | collective-permute-start | bytes 165896 | tf_op jit(solution)/shard_map/ppermute | solution.py:60
  116.7 2.7 %collective-permute-done.8 = bf16[2,8,27,8,8]{2,4,3,1,0:T(8,128)(2,1)S(1)} collective-permute-done((bf16[2,8,27,8,8]{2,4,3,1,0:T(8,128)(2,1)S(1)}, bf16[2,8,27,8,8]{2,4,3,1,0:T(8,128)(2,1)S(1)}, u32[]{:S(2)}, u32[]{:S(2)}) %collective-permute-start.8) | collective-permute-done | bytes 55328 | tf_op jit(solution)/shard_map/ppermute | solution.py:60
  119.6 14.7 %collective-permute-start.9 = (bf16[4,4,27,8,8]{2,4,3,1,0:T(8,128)(2,1)S(1)}, bf16[4,4,27,8,8]{2,4,3,1,0:T(8,128)(2,1)S(1)}, u32[]{:S(2)}, u32[]{:S(2)}) collective-permute-start(bf16[4,4,27,8,8]{2,4,3,1,0:T(8,128)(2,1)S(1)} %get-tuple-element.14), channel_id=1, source_target_pairs={{0,4},{1,5},{2,6},{3,7},{4,0},{5,1},{6,2},{7,3},{8,12},{9,13},{10,... | collective-permute-start | bytes 165896 | tf_op jit(solution)/shard_map/ppermute | solution.py:60
  134.3 8.4 %collective-permute-done.9 = bf16[4,4,27,8,8]{2,4,3,1,0:T(8,128)(2,1)S(1)} collective-permute-done((bf16[4,4,27,8,8]{2,4,3,1,0:T(8,128)(2,1)S(1)}, bf16[4,4,27,8,8]{2,4,3,1,0:T(8,128)(2,1)S(1)}, u32[]{:S(2)}, u32[]{:S(2)}) %collective-permute-start.9) | collective-permute-done | bytes 55328 | tf_op jit(solution)/shard_map/ppermute | solution.py:60
  143.0 8.1 %collective-permute-start.10 = (bf16[8,2,27,8,8]{2,4,3,1,0:T(8,128)(2,1)S(1)}, bf16[8,2,27,8,8]{2,4,3,1,0:T(8,128)(2,1)S(1)}, u32[]{:S(2)}, u32[]{:S(2)}) collective-permute-start(bf16[8,2,27,8,8]{2,4,3,1,0:T(8,128)(2,1)S(1)} %get-tuple-element.12), channel_id=1, source_target_pairs={{0,2},{1,3},{2,0},{3,1},{4,6},{5,7},{6,4},{7,5},{8,10},{9,11},{10,... | collective-permute-start | bytes 165896 | tf_op jit(solution)/shard_map/ppermute | solution.py:60
  151.1 5.5 %collective-permute-done.10 = bf16[8,2,27,8,8]{2,4,3,1,0:T(8,128)(2,1)S(1)} collective-permute-done((bf16[8,2,27,8,8]{2,4,3,1,0:T(8,128)(2,1)S(1)}, bf16[8,2,27,8,8]{2,4,3,1,0:T(8,128)(2,1)S(1)}, u32[]{:S(2)}, u32[]{:S(2)}) %collective-permute-start.10) | collective-permute-done | bytes 55328 | tf_op jit(solution)/shard_map/ppermute | solution.py:60
  156.8 2.1 collective-permute-start.11
  160.4 3.5 %copy.88 = bf16[32,27,8,8]{2,0,3,1:T(8,128)(2,1)S(1)} copy(bf16[32,27,8,8]{1,3,2,0:T(8,128)(2,1)S(1)} %bitcast.81) | data formatting | bytes 221184 | tf_op jit(solution)/shard_map/jit(_where)/select_n | solution.py:63
  164.0 2.9 %reshape.240 = bf16[3,3,3,256,8]{3,4,2,1,0:T(8,128)(2,1)S(1)} reshape(bf16[27,32,8,8]{2,1,3,0:T(8,128)(2,1)S(1)} %bitcast.70) | data formatting | bytes 221184 | tf_op jit(solution)/shard_map/reshape | solution.py:67
  169.1 13.9 %fusion.5 = bf16[2,2,64,8,8]{4,0,3,2,1:T(2,128)(2,1)S(1)} fusion(bf16[3,3,3,256,8]{3,4,2,1,0:T(8,128)(2,1)S(1)} %reshape.240, bf16[64,2,4,8,256]{4,3,2,1,0:T(8,128)(2,1)S(1)} %bitcast.77), kind=kOutput, calls=%fused_computation.4 | convolution fusion | flops 205488128 | bytes 2240512 | tf_op jit(solution)/shard_map/conv_general_dilated | solution.py:27
  183.2 2.1 collective-permute-start.12
  185.4 11.4 %collective-permute-done.12 = bf16[2,1,64,8,8]{4,0,3,2,1:T(2,128)(2,1)S(1)} collective-permute-done((bf16[2,1,64,8,8]{4,0,3,2,1:T(2,128)(2,1)S(1)}, bf16[2,1,64,8,8]{4,0,3,2,1:T(2,128)(2,1)S(1)}, u32[]{:S(2)}, u32[]{:S(2)}) %collective-permute-start.12) | collective-permute-done | bytes 16416 | tf_op jit(solution)/shard_map/ppermute | solution.py:23
  203.4 23.5 %all_to_all.5 = f32[16,1,2048]{2,1,0:T(1,128)S(1)} all-to-all(f32[16,1,2048]{2,1,0:T(1,128)S(1)} %reshape.242), channel_id=1, replica_groups=mesh['col'=32,'z'=16,'core'=2] {'z'}, dimensions={0} | all-to-all | bytes 262144 | tf_op jit(solution)/shard_map/all_to_all | solution.py:44
  (52 shorter events, 25.7 us)
Async XLA Ops:
  0.0 196.8 %copy-start = (bf16[3,3,3,8,256]{4,3,2,1,0:T(8,128)(2,1)S(1)}, bf16[3,3,3,8,256]{4,3,2,1,0:T(8,128)(2,1)}, u32[]{:S(2)}) copy-start(bf16[3,3,3,8,256]{4,3,2,1,0:T(8,128)(2,1)} %param.5) | copy-start | bytes 331780
  0.0 66.7 %copy-start.1 = (bf16[3,3,3,8,256]{4,3,2,1,0:T(8,128)(2,1)S(1)}, bf16[3,3,3,8,256]{4,3,2,1,0:T(8,128)(2,1)}, u32[]{:S(2)}) copy-start(bf16[3,3,3,8,256]{4,3,2,1,0:T(8,128)(2,1)} %param.4) | copy-start | bytes 331780
  0.8 9.2 %collective-permute-start = (bf16[2,1,2,8,256]{4,3,1,0,2:T(8,128)(2,1)S(1)}, bf16[2,1,2,8,256]{4,3,1,0,2:T(8,128)(2,1)S(1)}, u32[]{:S(2)}, u32[]{:S(2)}) collective-permute-start(bf16[2,1,2,8,256]{4,3,1,0,2:T(8,128)(2,1)S(1)} %copy.104), channel_id=1, source_target_pairs={{0,32},{32,64},{64,96},{96,128},{128,160},{160,192},{192,224},{224... | collective-permute-start | bytes 49160 | tf_op jit(solution)/shard_map/ppermute | solution.py:12
  4.2 7.2 %collective-permute-start.1 = (bf16[2,1,2,8,256]{4,3,1,0,2:T(8,128)(2,1)S(1)}, bf16[2,1,2,8,256]{4,3,1,0,2:T(8,128)(2,1)S(1)}, u32[]{:S(2)}, u32[]{:S(2)}) collective-permute-start(bf16[2,1,2,8,256]{4,3,1,0,2:T(8,128)(2,1)S(1)} %copy.105), channel_id=1, source_target_pairs={{32,0},{64,32},{96,64},{128,96},{160,128},{192,160},{224,192},{256... | collective-permute-start | bytes 49160 | tf_op jit(solution)/shard_map/ppermute | solution.py:15
  11.4 22.8 %collective-permute-start.2 = (bf16[1,2,2,4,8,256]{5,4,3,2,1,0:T(8,128)(2,1)S(1)}, bf16[1,2,2,4,8,256]{5,4,3,2,1,0:T(8,128)(2,1)S(1)}, u32[]{:S(2)}, u32[]{:S(2)}) collective-permute-start(bf16[1,2,2,4,8,256]{5,4,3,2,1,0:T(8,128)(2,1)S(1)} %bitcast.86), channel_id=1, source_target_pairs={{0,16},{1,17},{2,18},{3,19},{4,20},{5,21},{6,22},{7,23},{8,24},{9,... | collective-permute-start | bytes 196616 | tf_op jit(solution)/shard_map/ppermute | solution.py:60
  34.2 17.0 %collective-permute-start.3 = (bf16[2,2,2,4,8,256]{5,4,3,2,1,0:T(8,128)(2,1)S(1)}, bf16[2,2,2,4,8,256]{5,4,3,2,1,0:T(8,128)(2,1)S(1)}, u32[]{:S(2)}, u32[]{:S(2)}) collective-permute-start(bf16[2,2,2,4,8,256]{5,4,3,2,1,0:T(8,128)(2,1)S(1)} %maximum_select_fusion.10), channel_id=1, source_target_pairs={{0,8},{1,9},{2,10},{3,11},{4,12},{5,13},{6,14},{7,15},{8,0},{9,1},... | collective-permute-start | bytes 393224 | tf_op jit(solution)/shard_map/ppermute | solution.py:60
  51.2 13.4 %collective-permute-start.4 = (bf16[4,2,2,4,8,256]{5,4,3,2,1,0:T(8,128)(2,1)S(1)}, bf16[4,2,2,4,8,256]{5,4,3,2,1,0:T(8,128)(2,1)S(1)}, u32[]{:S(2)}, u32[]{:S(2)}) collective-permute-start(bf16[4,2,2,4,8,256]{5,4,3,2,1,0:T(8,128)(2,1)S(1)} %bitcast.82), channel_id=1, source_target_pairs={{0,4},{1,5},{2,6},{3,7},{4,0},{5,1},{6,2},{7,3},{8,12},{9,13},{10,... | collective-permute-start | bytes 786440 | tf_op jit(solution)/shard_map/ppermute | solution.py:60
  64.7 48.4 %collective-permute-start.5 = (bf16[8,2,2,4,8,256]{5,4,3,2,1,0:T(8,128)(2,1)S(1)}, bf16[8,2,2,4,8,256]{5,4,3,2,1,0:T(8,128)(2,1)}, u32[]{:S(2)}, u32[]{:S(2)}) collective-permute-start(bf16[8,2,2,4,8,256]{5,4,3,2,1,0:T(8,128)(2,1)S(1)} %bitcast.75), channel_id=1, source_target_pairs={{0,2},{1,3},{2,0},{3,1},{4,6},{5,7},{6,4},{7,5},{8,10},{9,11},{10,... | collective-permute-start | bytes 1572872 | tf_op jit(solution)/shard_map/ppermute | solution.py:60
  72.4 26.0 %collective-permute-start.7 = (bf16[1,16,27,8,8]{2,4,3,1,0:T(8,128)(2,1)S(1)}, bf16[1,16,27,8,8]{2,4,3,1,0:T(8,128)(2,1)S(1)}, u32[]{:S(2)}, u32[]{:S(2)}) collective-permute-start(bf16[1,16,27,8,8]{2,4,3,1,0:T(8,128)(2,1)S(1)} %bitcast.90), channel_id=1, source_target_pairs={{0,16},{1,17},{2,18},{3,19},{4,20},{5,21},{6,22},{7,23},{8,24},{9,... | collective-permute-start | bytes 165896 | tf_op jit(solution)/shard_map/ppermute | solution.py:60
  98.6 20.8 %collective-permute-start.8 = (bf16[2,8,27,8,8]{2,4,3,1,0:T(8,128)(2,1)S(1)}, bf16[2,8,27,8,8]{2,4,3,1,0:T(8,128)(2,1)S(1)}, u32[]{:S(2)}, u32[]{:S(2)}) collective-permute-start(bf16[2,8,27,8,8]{2,4,3,1,0:T(8,128)(2,1)S(1)} %get-tuple-element.16), channel_id=1, source_target_pairs={{0,8},{1,9},{2,10},{3,11},{4,12},{5,13},{6,14},{7,15},{8,0},{9,1},... | collective-permute-start | bytes 165896 | tf_op jit(solution)/shard_map/ppermute | solution.py:60
  114.7 52.2 %collective-permute-start.6 = (bf16[16,2,2,4,8,256]{5,4,3,2,1,0:T(8,128)(2,1)S(1)}, bf16[16,2,2,4,8,256]{5,4,3,2,1,0:T(8,128)(2,1)}, u32[]{:S(2)}, u32[]{:S(2)}) collective-permute-start(bf16[16,2,2,4,8,256]{5,4,3,2,1,0:T(8,128)(2,1)S(1)} %bitcast.72), channel_id=1, source_target_pairs={{0,1},{1,0},{2,3},{3,2},{4,5},{5,4},{6,7},{7,6},{8,9},{9,8},{10,11... | collective-permute-start | bytes 3145736 | tf_op jit(solution)/shard_map/ppermute | solution.py:60
  119.6 23.1 %collective-permute-start.9 = (bf16[4,4,27,8,8]{2,4,3,1,0:T(8,128)(2,1)S(1)}, bf16[4,4,27,8,8]{2,4,3,1,0:T(8,128)(2,1)S(1)}, u32[]{:S(2)}, u32[]{:S(2)}) collective-permute-start(bf16[4,4,27,8,8]{2,4,3,1,0:T(8,128)(2,1)S(1)} %get-tuple-element.14), channel_id=1, source_target_pairs={{0,4},{1,5},{2,6},{3,7},{4,0},{5,1},{6,2},{7,3},{8,12},{9,13},{10,... | collective-permute-start | bytes 165896 | tf_op jit(solution)/shard_map/ppermute | solution.py:60
  143.0 13.6 %collective-permute-start.10 = (bf16[8,2,27,8,8]{2,4,3,1,0:T(8,128)(2,1)S(1)}, bf16[8,2,27,8,8]{2,4,3,1,0:T(8,128)(2,1)S(1)}, u32[]{:S(2)}, u32[]{:S(2)}) collective-permute-start(bf16[8,2,27,8,8]{2,4,3,1,0:T(8,128)(2,1)S(1)} %get-tuple-element.12), channel_id=1, source_target_pairs={{0,2},{1,3},{2,0},{3,1},{4,6},{5,7},{6,4},{7,5},{8,10},{9,11},{10,... | collective-permute-start | bytes 165896 | tf_op jit(solution)/shard_map/ppermute | solution.py:60
  156.8 3.4 %collective-permute-start.11 = (bf16[16,1,27,8,8]{2,4,3,1,0:T(8,128)(2,1)S(1)}, bf16[16,1,27,8,8]{2,4,3,1,0:T(8,128)(2,1)S(1)}, u32[]{:S(2)}, u32[]{:S(2)}) collective-permute-start(bf16[16,1,27,8,8]{2,4,3,1,0:T(8,128)(2,1)S(1)} %get-tuple-element.10), channel_id=1, source_target_pairs={{0,1},{1,0},{2,3},{3,2},{4,5},{5,4},{6,7},{7,6},{8,9},{9,8},{10,11... | collective-permute-start | bytes 165896 | tf_op jit(solution)/shard_map/ppermute | solution.py:60
  183.2 13.6 %collective-permute-start.12 = (bf16[2,1,64,8,8]{4,0,3,2,1:T(2,128)(2,1)S(1)}, bf16[2,1,64,8,8]{4,0,3,2,1:T(2,128)(2,1)S(1)}, u32[]{:S(2)}, u32[]{:S(2)}) collective-permute-start(bf16[2,1,64,8,8]{4,0,3,2,1:T(2,128)(2,1)S(1)} %slice.14), channel_id=1, source_target_pairs={{0,32},{32,64},{64,96},{96,128},{128,160},{160,192},{192,224},{224... | collective-permute-start | bytes 49160 | tf_op jit(solution)/shard_map/ppermute | solution.py:23
  199.2 3.8 %collective-permute-start.13 = (f32[16,8,2,1,32,4]{4,1,5,3,2,0:T(8,128)S(1)}, f32[16,8,2,1,32,4]{4,1,5,3,2,0:T(8,128)S(1)}, u32[]{:S(2)}, u32[]{:S(2)}) collective-permute-start(f32[16,8,2,1,32,4]{4,1,5,3,2,0:T(8,128)S(1)} %bitcast.85), channel_id=1, source_target_pairs={{0,1},{1,0},{2,3},{3,2},{4,5},{5,4},{6,7},{7,6},{8,9},{9,8},{10,11... | collective-permute-start | bytes 393224 | tf_op jit(solution)/shard_map/ppermute | solution.py:43

commit v6 on v5

--- a/solution.py
+++ b/solution.py
@@ -57,7 +57,11 @@
         split = held.reshape(held.shape[:1] + (2, -1) + held.shape[2:])
         keep = lax.dynamic_index_in_dim(split, mine, axis=1, keepdims=False)
         give = lax.dynamic_index_in_dim(split, 1 - mine, axis=1, keepdims=False)
-        other, got = lax.ppermute((rows, give), axis, pairs)
+        lanes = rows.shape[-1]
+        both = jnp.concatenate([rows.reshape(-1, lanes), give.reshape(-1, lanes)])
+        both = lax.ppermute(both, axis, pairs)
+        other = both[: rows.size // lanes].reshape(rows.shape)
+        got = both[rows.size // lanes :].reshape(give.shape)
         rows = jnp.where(low, jnp.stack([rows, other], 1), jnp.stack([other, rows], 1))
         rows = rows.reshape((-1,) + rows.shape[2:])
         held = jnp.where(low, jnp.stack([keep, got], 1), jnp.stack([got, keep], 1))

time: 230 us -> 190 us (0.83)
  starting transfers between devices: 98.3 us -> 44.6 us
  local copies, waits for them, and re-layouts: 17.1 us -> 36.4 us
  waiting for transfers between devices: 67.8 us -> 61.1 us
  blocking collectives: 23.5 us -> 26.4 us
    ppermute x10 -> x5, starting transfers between devices: 85.1 us -> 31.4 us  [gathered(): both = lax.ppermute(both, axis, pairs)]
    another operation x0 -> x10, local copies, waits for them, and re-layouts: none -> 10.2 us  [gathered(): held = jnp.where(low, jnp.stack([keep, got], 1), jnp.stack([got, keep], 1))]
    reshape x0 -> x5, local copies, waits for them, and re-layouts: none -> 6.14 us  [gathered(): both = jnp.concatenate([rows.reshape(-1, lanes), give.reshape(-1, lanes)])]
    ppermute x10 -> x5, waiting for transfers between devices: 53.8 us -> 47.9 us  [gathered(): both = lax.ppermute(both, axis, pairs)]
    transpose x0 -> x1, local copies, waits for them, and re-layouts: none -> 3.75 us  [gathered(): own = held.reshape((peers,) + held.shape[2:]).transpose(1, 0, 2, 3)]
    dynamic_slice x0 -> x4, local copies, waits for them, and re-layouts: none -> 3.59 us  [gathered(): give = lax.dynamic_index_in_dim(split, 1 - mine, axis=1, keepdims=False)]
    select_n x1 -> x0, local copies, waits for them, and re-layouts: 3.53 us -> none  [gathered(): held = jnp.where(low, jnp.stack([keep, got], 1), jnp.stack([got, keep], 1))]
    select_n x6, other arithmetic: 3.56 us -> 0.65 us  [gathered(): jnp.where(low, jnp.stack([rows, other], 1), jnp.stack([other, rows], 1))]
  transfers between devices with their start and end apart: 14 -> 9, of which waited for: 11 -> 7; matrix products, arithmetic and copies ran while one was open for 7% -> 3% of each run, Pallas kernels for 0% -> 0%
where the time goes in v6:
time: 190 us
  waiting for transfers between devices  61.1 us (32%)
  starting transfers between devices  44.6 us (23%)
  local copies, waits for them, and re-layouts  36.4 us (19%)
  blocking collectives  26.4 us (14%)
  matrix products  15.8 us (8%)
  other arithmetic  4.64 us (2%)
    ppermute x5, waiting for transfers between devices, gathered(): both = lax.ppermute(both, axis, pairs)  47.9 us
    ppermute x5, starting transfers between devices, gathered(): both = lax.ppermute(both, axis, pairs)  31.4 us
    all_to_all x1, blocking collectives, reduce_scattered(): return lax.all_to_all(half, 'z', 0, 0, tiled=True).sum(axis=0)  26.4 us
    conv_general_dilated x2, matrix products, convolve(): lax.conv_general_dilated(volume, kernel, (stride, stride, stride), ((0, 0...  15.8 us
    ppermute x1, waiting for transfers between devices, passed_along(): return lax.ppermute(array, axis, pairs)  11.4 us
    another operation x10, local copies, waits for them, and re-layouts, gathered(): held = jnp.where(low, jnp.stack([keep, got], 1), jnp.stack([got, keep], 1))  10.2 us
    reshape x5, local copies, waits for them, and re-layouts, gathered(): both = jnp.concatenate([rows.reshape(-1, lanes), give.reshape(-1, lanes)])  6.14 us
    ppermute x1, starting transfers between devices, extended(): lax.ppermute(lax.slice_in_dim(block, 0, width, axis=dim), axis, backward)  5.76 us
  transfers between devices with their start and end apart: 9, of which 7 were waited for; matrix products, arithmetic and copies ran while one was open for 3% of the time, Pallas kernels for 0%

profile of v6, /device:TPU:32, one launch (start us, length us, event | category | flops | bytes accessed | tf_op | source)
XLA Modules:
  0.0 189.7 jit_solution(18076629604939612807)
XLA Ops:
  0.8 3.4 %collective-permute-start = (bf16[2,1,2,8,256]{4,3,1,0,2:T(8,128)(2,1)S(1)}, bf16[2,1,2,8,256]{4,3,1,0,2:T(8,128)(2,1)S(1)}, u32[]{:S(2)}, u32[]{:S(2)}) collective-permute-start(bf16[2,1,2,8,256]{4,3,1,0,2:T(8,128)(2,1)S(1)} %copy.159), channel_id=1, source_target_pairs={{0,32},{32,64},{64,96},{96,128},{128,160},{160,192},{192,224},{224... | collective-permute-start | bytes 49160 | tf_op jit(solution)/shard_map/ppermute | solution.py:12
  4.2 5.8 %collective-permute-start.1 = (bf16[2,1,2,8,256]{4,3,1,0,2:T(8,128)(2,1)S(1)}, bf16[2,1,2,8,256]{4,3,1,0,2:T(8,128)(2,1)S(1)}, u32[]{:S(2)}, u32[]{:S(2)}) collective-permute-start(bf16[2,1,2,8,256]{4,3,1,0,2:T(8,128)(2,1)S(1)} %copy.160), channel_id=1, source_target_pairs={{32,0},{64,32},{96,64},{128,96},{160,128},{192,160},{224,192},{256... | collective-permute-start | bytes 49160 | tf_op jit(solution)/shard_map/ppermute | solution.py:15
  10.0 3.0 %reshape.251 = bf16[27,8,32,8]{3,2,1,0:T(8,128)(2,1)S(1)} reshape(bf16[3,3,3,8,256]{4,3,2,1,0:T(8,128)(2,1)} %param.4) | data formatting | bytes 221184 | tf_op jit(solution)/shard_map/reshape | solution.py:52
  14.9 19.4 %collective-permute-start.2 = (bf16[236,256]{1,0:T(8,128)(2,1)S(1)}, bf16[236,256]{1,0:T(8,128)(2,1)S(1)}, u32[]{:S(2)}, u32[]{:S(2)}) collective-permute-start(bf16[236,256]{1,0:T(8,128)(2,1)S(1)} %pad_maximum_fusion.6), channel_id=1, source_target_pairs={{0,16},{1,17},{2,18},{3,19},{4,20},{5,21},{6,22},{7,23},{8,24},{9,... | collective-permute-start | bytes 362504 | tf_op jit(solution)/shard_map/ppermute | solution.py:62
  35.6 7.5 %collective-permute-done.2 = bf16[236,256]{1,0:T(8,128)(2,1)S(1)} collective-permute-done((bf16[236,256]{1,0:T(8,128)(2,1)S(1)}, bf16[236,256]{1,0:T(8,128)(2,1)S(1)}, u32[]{:S(2)}, u32[]{:S(2)}) %collective-permute-start.2) | collective-permute-done | bytes 120864 | tf_op jit(solution)/shard_map/ppermute | solution.py:62
  47.5 5.5 %collective-permute-start.3 = (bf16[364,256]{1,0:T(8,128)(2,1)S(1)}, bf16[364,256]{1,0:T(8,128)(2,1)S(1)}, u32[]{:S(2)}, u32[]{:S(2)}) collective-permute-start(bf16[364,256]{1,0:T(8,128)(2,1)S(1)} %pad_maximum_fusion.5), channel_id=1, source_target_pairs={{0,8},{1,9},{2,10},{3,11},{4,12},{5,13},{6,14},{7,15},{8,0},{9,1},... | collective-permute-start | bytes 559112 | tf_op jit(solution)/shard_map/ppermute | solution.py:62
  53.0 14.0 %collective-permute-done.3 = bf16[364,256]{1,0:T(8,128)(2,1)S(1)} collective-permute-done((bf16[364,256]{1,0:T(8,128)(2,1)S(1)}, bf16[364,256]{1,0:T(8,128)(2,1)S(1)}, u32[]{:S(2)}, u32[]{:S(2)}) %collective-permute-start.3) | collective-permute-done | bytes 186400 | tf_op jit(solution)/shard_map/ppermute | solution.py:62
  71.4 2.7 %collective-permute-start.4 = (bf16[620,256]{1,0:T(8,128)(2,1)S(1)}, bf16[620,256]{1,0:T(8,128)(2,1)S(1)}, u32[]{:S(2)}, u32[]{:S(2)}) collective-permute-start(bf16[620,256]{1,0:T(8,128)(2,1)S(1)} %pad_maximum_fusion.4), channel_id=1, source_target_pairs={{0,4},{1,5},{2,6},{3,7},{4,0},{5,1},{6,2},{7,3},{8,12},{9,13},{10,... | collective-permute-start | bytes 952328 | tf_op jit(solution)/shard_map/ppermute | solution.py:62
  74.1 10.9 %collective-permute-done.4 = bf16[620,256]{1,0:T(8,128)(2,1)S(1)} collective-permute-done((bf16[620,256]{1,0:T(8,128)(2,1)S(1)}, bf16[620,256]{1,0:T(8,128)(2,1)S(1)}, u32[]{:S(2)}, u32[]{:S(2)}) %collective-permute-start.4) | collective-permute-done | bytes 317472 | tf_op jit(solution)/shard_map/ppermute | solution.py:62
  89.5 1.9 %collective-permute-start.5 = (bf16[1132,256]{1,0:T(8,128)(2,1)S(1)}, bf16[1132,256]{1,0:T(8,128)(2,1)S(1)}, u32[]{:S(2)}, u32[]{:S(2)}) collective-permute-start(bf16[1132,256]{1,0:T(8,128)(2,1)S(1)} %pad_maximum_fusion.3), channel_id=1, source_target_pairs={{0,2},{1,3},{2,0},{3,1},{4,6},{5,7},{6,4},{7,5},{8,10},{9,11},{10,... | collective-permute-start | bytes 1738760 | tf_op jit(solution)/shard_map/ppermute | solution.py:62
  91.5 12.7 %collective-permute-done.5 = bf16[1132,256]{1,0:T(8,128)(2,1)S(1)} collective-permute-done((bf16[1132,256]{1,0:T(8,128)(2,1)S(1)}, bf16[1132,256]{1,0:T(8,128)(2,1)S(1)}, u32[]{:S(2)}, u32[]{:S(2)}) %collective-permute-start.5) | collective-permute-done | bytes 579616 | tf_op jit(solution)/shard_map/ppermute | solution.py:62
  109.6 1.9 %collective-permute-start.6 = (bf16[2156,256]{1,0:T(8,128)(2,1)S(1)}, bf16[2156,256]{1,0:T(8,128)(2,1)S(1)}, u32[]{:S(2)}, u32[]{:S(2)}) collective-permute-start(bf16[2156,256]{1,0:T(8,128)(2,1)S(1)} %pad_maximum_fusion), channel_id=1, source_target_pairs={{0,1},{1,0},{2,3},{3,2},{4,5},{5,4},{6,7},{7,6},{8,9},{9,8},{10,11... | collective-permute-start | bytes 3311624 | tf_op jit(solution)/shard_map/ppermute | solution.py:62
  111.5 2.7 %collective-permute-done.6 = bf16[2156,256]{1,0:T(8,128)(2,1)S(1)} collective-permute-done((bf16[2156,256]{1,0:T(8,128)(2,1)S(1)}, bf16[2156,256]{1,0:T(8,128)(2,1)S(1)}, u32[]{:S(2)}, u32[]{:S(2)}) %collective-permute-start.6) | collective-permute-done | bytes 1103904 | tf_op jit(solution)/shard_map/ppermute | solution.py:62
  115.3 1.6 copy.141
  116.8 1.4 maximum_select_fusion.7
  118.3 3.7 %copy.143 = bf16[27,32,8,8]{2,1,3,0:T(8,128)(2,1)S(1)} copy(bf16[27,32,8,8]{0,3,2,1:T(8,128)(2,1)S(1)} %bitcast.92) | data formatting | bytes 221184 | tf_op jit(solution)/shard_map/transpose | solution.py:70
  122.0 2.9 %reshape.257 = bf16[3,3,3,256,8]{3,4,2,1,0:T(8,128)(2,1)S(1)} reshape(bf16[27,32,8,8]{2,1,3,0:T(8,128)(2,1)S(1)} %copy.143) | data formatting | bytes 221184 | tf_op jit(solution)/shard_map/reshape | solution.py:71
  126.7 13.9 %fusion.5 = bf16[2,2,64,8,8]{4,0,3,2,1:T(2,128)(2,1)S(1)} fusion(bf16[3,3,3,256,8]{3,4,2,1,0:T(8,128)(2,1)S(1)} %reshape.257, bf16[64,2,4,8,256]{4,3,2,1,0:T(8,128)(2,1)S(1)} %bitcast.88), kind=kOutput, calls=%fused_computation.4 | convolution fusion | flops 205488128 | bytes 2240512 | tf_op jit(solution)/shard_map/conv_general_dilated | solution.py:27
  140.8 2.2 %collective-permute-start.7 = (bf16[2,1,64,8,8]{4,0,3,2,1:T(2,128)(2,1)S(1)}, bf16[2,1,64,8,8]{4,0,3,2,1:T(2,128)(2,1)S(1)}, u32[]{:S(2)}, u32[]{:S(2)}) collective-permute-start(bf16[2,1,64,8,8]{4,0,3,2,1:T(2,128)(2,1)S(1)} %slice.64), channel_id=1, source_target_pairs={{0,32},{32,64},{64,96},{96,128},{128,160},{160,192},{192,224},{224... | collective-permute-start | bytes 49160 | tf_op jit(solution)/shard_map/ppermute | solution.py:23
  143.0 11.4 %collective-permute-done.7 = bf16[2,1,64,8,8]{4,0,3,2,1:T(2,128)(2,1)S(1)} collective-permute-done((bf16[2,1,64,8,8]{4,0,3,2,1:T(2,128)(2,1)S(1)}, bf16[2,1,64,8,8]{4,0,3,2,1:T(2,128)(2,1)S(1)}, u32[]{:S(2)}, u32[]{:S(2)}) %collective-permute-start.7) | collective-permute-done | bytes 16416 | tf_op jit(solution)/shard_map/ppermute | solution.py:23
  154.4 1.9 %fusion.8 = f32[256,2,1,32,4]{0,1,4,3,2:T(2,128)S(1)} fusion(bf16[3,3,3,8,256]{4,3,2,1,0:T(8,128)(2,1)S(1)} %copy-done, bf16[2,2,64,8,8]{4,0,3,2,1:T(2,128)(2,1)S(1)} %fusion.5, bf16[2,1,64,8,8]{4,0,3,2,1:T(2,128)(2,1)S(1)} %collective-permute-done.7), kind=kOutput, calls=%fused_computation.8 | convolution fusion | flops 25780224 | bytes 421888 | tf_op jit(solution)/shard_map/conv_general_dilated | solution.py:27
  156.8 1.9 %collective-permute-start.8 = (f32[16,8,2,1,32,4]{4,1,5,3,2,0:T(8,128)S(1)}, f32[16,8,2,1,32,4]{4,1,5,3,2,0:T(8,128)S(1)}, u32[]{:S(2)}, u32[]{:S(2)}) collective-permute-start(f32[16,8,2,1,32,4]{4,1,5,3,2,0:T(8,128)S(1)} %bitcast.102), channel_id=1, source_target_pairs={{0,1},{1,0},{2,3},{3,2},{4,5},{5,4},{6,7},{7,6},{8,9},{9,8},{10,11... | collective-permute-start | bytes 393224 | tf_op jit(solution)/shard_map/ppermute | solution.py:43
  158.7 1.9 collective-permute-done.8
  160.9 26.4 %all_to_all.5 = f32[16,1,2048]{2,1,0:T(1,128)S(1)} all-to-all(f32[16,1,2048]{2,1,0:T(1,128)S(1)} %reshape.259), channel_id=1, replica_groups=mesh['col'=32,'z'=16,'core'=2] {'z'}, dimensions={0} | all-to-all | bytes 262144 | tf_op jit(solution)/shard_map/all_to_all | solution.py:44
  (79 shorter events, 28.3 us)
Async XLA Ops:
  0.0 154.4 %copy-start = (bf16[3,3,3,8,256]{4,3,2,1,0:T(8,128)(2,1)S(1)}, bf16[3,3,3,8,256]{4,3,2,1,0:T(8,128)(2,1)}, u32[]{:S(2)}) copy-start(bf16[3,3,3,8,256]{4,3,2,1,0:T(8,128)(2,1)} %param.5) | copy-start | bytes 331780
  0.8 14.1 %collective-permute-start = (bf16[2,1,2,8,256]{4,3,1,0,2:T(8,128)(2,1)S(1)}, bf16[2,1,2,8,256]{4,3,1,0,2:T(8,128)(2,1)S(1)}, u32[]{:S(2)}, u32[]{:S(2)}) collective-permute-start(bf16[2,1,2,8,256]{4,3,1,0,2:T(8,128)(2,1)S(1)} %copy.159), channel_id=1, source_target_pairs={{0,32},{32,64},{64,96},{96,128},{128,160},{160,192},{192,224},{224... | collective-permute-start | bytes 49160 | tf_op jit(solution)/shard_map/ppermute | solution.py:12
  4.2 10.7 %collective-permute-start.1 = (bf16[2,1,2,8,256]{4,3,1,0,2:T(8,128)(2,1)S(1)}, bf16[2,1,2,8,256]{4,3,1,0,2:T(8,128)(2,1)S(1)}, u32[]{:S(2)}, u32[]{:S(2)}) collective-permute-start(bf16[2,1,2,8,256]{4,3,1,0,2:T(8,128)(2,1)S(1)} %copy.160), channel_id=1, source_target_pairs={{32,0},{64,32},{96,64},{128,96},{160,128},{192,160},{224,192},{256... | collective-permute-start | bytes 49160 | tf_op jit(solution)/shard_map/ppermute | solution.py:15
  13.4 1.5 copy-start.2
  14.9 28.2 %collective-permute-start.2 = (bf16[236,256]{1,0:T(8,128)(2,1)S(1)}, bf16[236,256]{1,0:T(8,128)(2,1)S(1)}, u32[]{:S(2)}, u32[]{:S(2)}) collective-permute-start(bf16[236,256]{1,0:T(8,128)(2,1)S(1)} %pad_maximum_fusion.6), channel_id=1, source_target_pairs={{0,16},{1,17},{2,18},{3,19},{4,20},{5,21},{6,22},{7,23},{8,24},{9,... | collective-permute-start | bytes 362504 | tf_op jit(solution)/shard_map/ppermute | solution.py:62
  47.5 19.6 %collective-permute-start.3 = (bf16[364,256]{1,0:T(8,128)(2,1)S(1)}, bf16[364,256]{1,0:T(8,128)(2,1)S(1)}, u32[]{:S(2)}, u32[]{:S(2)}) collective-permute-start(bf16[364,256]{1,0:T(8,128)(2,1)S(1)} %pad_maximum_fusion.5), channel_id=1, source_target_pairs={{0,8},{1,9},{2,10},{3,11},{4,12},{5,13},{6,14},{7,15},{8,0},{9,1},... | collective-permute-start | bytes 559112 | tf_op jit(solution)/shard_map/ppermute | solution.py:62
  71.4 13.6 %collective-permute-start.4 = (bf16[620,256]{1,0:T(8,128)(2,1)S(1)}, bf16[620,256]{1,0:T(8,128)(2,1)S(1)}, u32[]{:S(2)}, u32[]{:S(2)}) collective-permute-start(bf16[620,256]{1,0:T(8,128)(2,1)S(1)} %pad_maximum_fusion.4), channel_id=1, source_target_pairs={{0,4},{1,5},{2,6},{3,7},{4,0},{5,1},{6,2},{7,3},{8,12},{9,13},{10,... | collective-permute-start | bytes 952328 | tf_op jit(solution)/shard_map/ppermute | solution.py:62
  89.5 14.7 %collective-permute-start.5 = (bf16[1132,256]{1,0:T(8,128)(2,1)S(1)}, bf16[1132,256]{1,0:T(8,128)(2,1)S(1)}, u32[]{:S(2)}, u32[]{:S(2)}) collective-permute-start(bf16[1132,256]{1,0:T(8,128)(2,1)S(1)} %pad_maximum_fusion.3), channel_id=1, source_target_pairs={{0,2},{1,3},{2,0},{3,1},{4,6},{5,7},{6,4},{7,5},{8,10},{9,11},{10,... | collective-permute-start | bytes 1738760 | tf_op jit(solution)/shard_map/ppermute | solution.py:62
  109.6 4.6 %collective-permute-start.6 = (bf16[2156,256]{1,0:T(8,128)(2,1)S(1)}, bf16[2156,256]{1,0:T(8,128)(2,1)S(1)}, u32[]{:S(2)}, u32[]{:S(2)}) collective-permute-start(bf16[2156,256]{1,0:T(8,128)(2,1)S(1)} %pad_maximum_fusion), channel_id=1, source_target_pairs={{0,1},{1,0},{2,3},{3,2},{4,5},{5,4},{6,7},{7,6},{8,9},{9,8},{10,11... | collective-permute-start | bytes 3311624 | tf_op jit(solution)/shard_map/ppermute | solution.py:62
  114.2 4.0 %copy-start.1 = (bf16[2156,256]{1,0:T(8,128)(2,1)}, bf16[2156,256]{1,0:T(8,128)(2,1)S(1)}, u32[]{:S(2)}) copy-start(bf16[2156,256]{1,0:T(8,128)(2,1)S(1)} %collective-permute-done.6) | copy-start | bytes 3311620
  124.9 1.2 slice-start
  140.8 13.6 %collective-permute-start.7 = (bf16[2,1,64,8,8]{4,0,3,2,1:T(2,128)(2,1)S(1)}, bf16[2,1,64,8,8]{4,0,3,2,1:T(2,128)(2,1)S(1)}, u32[]{:S(2)}, u32[]{:S(2)}) collective-permute-start(bf16[2,1,64,8,8]{4,0,3,2,1:T(2,128)(2,1)S(1)} %slice.64), channel_id=1, source_target_pairs={{0,32},{32,64},{64,96},{96,128},{128,160},{160,192},{192,224},{224... | collective-permute-start | bytes 49160 | tf_op jit(solution)/shard_map/ppermute | solution.py:23
  156.8 3.8 %collective-permute-start.8 = (f32[16,8,2,1,32,4]{4,1,5,3,2,0:T(8,128)S(1)}, f32[16,8,2,1,32,4]{4,1,5,3,2,0:T(8,128)S(1)}, u32[]{:S(2)}, u32[]{:S(2)}) collective-permute-start(f32[16,8,2,1,32,4]{4,1,5,3,2,0:T(8,128)S(1)} %bitcast.102), channel_id=1, source_target_pairs={{0,1},{1,0},{2,3},{3,2},{4,5},{5,4},{6,7},{7,6},{8,9},{9,8},{10,11... | collective-permute-start | bytes 393224 | tf_op jit(solution)/shard_map/ppermute | solution.py:43

commit v7 on v3

--- a/solution.py
+++ b/solution.py
@@ -45,8 +45,10 @@
 
 
 def per_device(inputs, first_filters, second_filters):
-    padded = extended(inputs, (("col", 1),), 1)
-    gathered = lax.all_gather(lax.all_gather(padded, "core", axis=2, tiled=True), "z", axis=2, tiled=True)
+    own = lax.all_gather(inputs, ("z", "core"), axis=2, tiled=True)
+    lower = passed_along(own[:, -1:], "col", 1)
+    upper = passed_along(own[:, :1], "col", -1)
+    gathered = jnp.concatenate([lower, own, upper], axis=1)
     own_first = lax.all_to_all(first_filters, ("z", "core"), split_axis=4, concat_axis=3, tiled=True)
     hidden = jnp.maximum(convolve(gathered, own_first, 1, 1), 0.0).astype(jnp.bfloat16)
     lower_plane = passed_along(hidden[:, -1:], "col", 1)

time: 171 us -> 197 us (1.15)
  waiting for transfers between devices: 53.9 us -> 95.5 us
  blocking collectives: 60.5 us -> 41.6 us
  local copies, waits for them, and re-layouts: 14.7 us -> 16.7 us
    all_gather x1, waiting for transfers between devices: 35.5 us -> 83.9 us  [per_device(): own = lax.all_gather(inputs, ('z', 'core'), axis=2, tiled=True)]
    all_to_all x1, blocking collectives: 36.6 us -> 24.6 us  [per_device(): lax.all_to_all(first_filters, ('z', 'core'), split_axis=4, concat_axis=3,...]
    ppermute x1 -> x3, starting transfers between devices: 2.1 us -> 9.39 us  [passed_along(): return lax.ppermute(array, axis, pairs)]
    ppermute x2 -> x0, waiting for transfers between devices: 7.02 us -> none  [the longest x1 7.01 us: extended(): lax.ppermute(lax.slice_in_dim(block, block.shape[dim] - width, None, axis...]
    ppermute x2 -> x0, starting transfers between devices: 6.47 us -> none  [the longest x1 4.55 us: extended(): lax.ppermute(lax.slice_in_dim(block, 0, width, axis=dim), axis, backward)]
    all_to_all x1, blocking collectives: 21.9 us -> 17 us  [reduce_scattered(): return lax.all_to_all(half, 'z', 0, 0, tiled=True).sum(axis=0)]
    slice x1, local copies, waits for them, and re-layouts: 0.03 us -> 2.9 us  [per_device(): lower = passed_along(own[:, -1:], 'col', 1)]
    all_gather x1 -> x0, blocking collectives: 2.03 us -> none  [per_device(): lax.all_gather(padded, 'core', axis=2, tiled=True)]
  transfers between devices with their start and end apart: 5 -> 5, of which waited for: 4 -> 3; matrix products, arithmetic and copies ran while one was open for 5% -> 4% of each run, Pallas kernels for 0% -> 0%
where the time goes in v7:
time: 197 us
  waiting for transfers between devices  95.5 us (48%)
  blocking collectives  41.6 us (21%)
  local copies, waits for them, and re-layouts  16.7 us (8%)
  matrix products  16.2 us (8%)
  between operations  13.6 us (7%)
  starting transfers between devices  11.3 us (6%)
    all_gather x1, waiting for transfers between devices, per_device(): own = lax.all_gather(inputs, ('z', 'core'), axis=2, tiled=True)  83.9 us
    all_to_all x1, blocking collectives, per_device(): lax.all_to_all(first_filters, ('z', 'core'), split_axis=4, concat_axis=3,...  24.6 us
    all_to_all x1, blocking collectives, reduce_scattered(): return lax.all_to_all(half, 'z', 0, 0, tiled=True).sum(axis=0)  17 us
    conv_general_dilated x2, matrix products, convolve(): lax.conv_general_dilated(volume, kernel, (stride, stride, stride), ((0, 0...  16.2 us
    ppermute x3, waiting for transfers between devices, passed_along(): return lax.ppermute(array, axis, pairs)  9.72 us
    ppermute x3, starting transfers between devices, passed_along(): return lax.ppermute(array, axis, pairs)  9.39 us
    unnamed x12, local copies, waits for them, and re-layouts  7.08 us
    all_to_all x2, local copies, waits for them, and re-layouts, per_device(): lax.all_to_all(first_filters, ('z', 'core'), split_axis=4, concat_axis=3,...  5.52 us
  transfers between devices with their start and end apart: 5, of which 3 were waited for; matrix products, arithmetic and copies ran while one was open for 4% of the time, Pallas kernels for 0%

profile of v7, /device:TPU:32, one launch (start us, length us, event | category | flops | bytes accessed | tf_op | source)
XLA Modules:
  0.0 196.6 jit_solution(18150066987594967534)
XLA Ops:
  6.5 1.5 copy.28
  8.0 83.9 %all-gather.2.cloned.1.call-done = bf16[2,2,64,8,256]{4,0,3,2,1:T(2,128)(2,1)} async-done(((bf16[2,2,2,8,256]{4,0,3,2,1:T(2,128)(2,1)}), bf16[2,2,64,8,256]{4,0,3,2,1:T(2,128)(2,1)}) %all-gather.2.cloned.1.call-update) | async-done | bytes 1048592 | tf_op jit(solution)/shard_map/all_gather | solution.py:48
  91.9 2.9 %fusion.8 = (bf16[2,1,64,8,256]{4,0,3,2,1:T(2,128)(2,1)}, bf16[2,1,64,8,256]{4,0,3,2,1:T(2,128)(2,1)}) fusion(bf16[2,2,64,8,256]{4,0,3,2,1:T(2,128)(2,1)} %all-gather.2.cloned.1.call-done), kind=kLoop, calls=%fused_computation.16 | loop fusion | bytes 2097152 | tf_op jit(solution)/shard_map/slice | solution.py:49
  94.8 4.6 %collective-permute-start.1 = (bf16[2,1,64,8,256]{4,0,3,2,1:T(2,128)(2,1)}, bf16[2,1,64,8,256]{4,0,3,2,1:T(2,128)(2,1)}, u32[]{:S(2)}, u32[]{:S(2)}) collective-permute-start(bf16[2,1,64,8,256]{4,0,3,2,1:T(2,128)(2,1)} %get-tuple-element.8), channel_id=1, source_target_pairs={{32,0},{64,32},{96,64},{128,96},{160,128},{192,160},{224,192},{256... | collective-permute-start | bytes 1572872 | tf_op jit(solution)/shard_map/ppermute | solution.py:23
  99.4 1.9 collective-permute-start
  101.4 1.8 copy.29
  103.2 1.8 reshape.8
  105.0 24.6 %all_to_all.23 = bf16[32,2,864]{2,1,0:T(2,128)(2,1)S(1)} all-to-all(bf16[32,2,864]{2,1,0:T(2,128)(2,1)S(1)} %reshape.8), channel_id=1, replica_groups=mesh['col'=32,'z'=16,'core'=2] {'z','core'}, dimensions={0} | all-to-all | bytes 221184 | tf_op jit(solution)/shard_map/all_to_all | solution.py:52
  129.6 1.6 reshape.9
  131.2 2.1 %copy.43 = bf16[3,3,3,8,32,8]{3,4,5,2,1,0:T(8,128)(2,1)} copy(bf16[3,3,3,8,32,8]{3,2,1,0,5,4:T(4,128)(2,1)S(1)} %bitcast.35) | data formatting | bytes 221184 | tf_op jit(solution)/shard_map/all_to_all | solution.py:52
  133.3 3.4 %all_to_all.19 = bf16[3,3,3,256,8]{3,4,2,1,0:T(8,128)(2,1)S(1)} reshape(bf16[3,3,3,32,8,8]{4,3,5,2,1,0:T(8,128)(2,1)} %bitcast.37) | data formatting | bytes 221184 | tf_op jit(solution)/shard_map/all_to_all | solution.py:52
  136.8 14.3 %fusion.2 = bf16[2,2,64,8,8]{4,0,3,2,1:T(2,128)(2,1)S(1)} fusion(bf16[3,3,3,256,8]{3,4,2,1,0:T(8,128)(2,1)S(1)} %all_to_all.19, bf16[2,1,64,8,256]{4,0,3,2,1:T(2,128)(2,1)} %collective-permute-done.1, bf16[2,2,64,8,256]{4,0,3,2,1:T(2,128)(2,1)S(1)} %copy-done.1, bf16[2,1,64,8,256]{4,0,3,2,1:T(2,128)(2,1)} %collective-permute-done), kind=kOutput, calls=%fused_computation.4 | convolution fusion | flops 211779584 | bytes 2240512 | tf_op jit(solution)/shard_map/conv_general_dilated | solution.py:27
  151.1 0.2 slice.14
  151.3 2.9 %collective-permute-start.2 = (bf16[2,1,64,8,8]{4,0,3,2,1:T(2,128)(2,1)S(1)}, bf16[2,1,64,8,8]{4,0,3,2,1:T(2,128)(2,1)S(1)}, u32[]{:S(2)}, u32[]{:S(2)}) collective-permute-start(bf16[2,1,64,8,8]{4,0,3,2,1:T(2,128)(2,1)S(1)} %slice.14), channel_id=1, source_target_pairs={{0,32},{32,64},{64,96},{96,128},{128,160},{160,192},{192,224},{224... | collective-permute-start | bytes 49160 | tf_op jit(solution)/shard_map/ppermute | solution.py:23
  154.2 9.7 %collective-permute-done.2 = bf16[2,1,64,8,8]{4,0,3,2,1:T(2,128)(2,1)S(1)} collective-permute-done((bf16[2,1,64,8,8]{4,0,3,2,1:T(2,128)(2,1)S(1)}, bf16[2,1,64,8,8]{4,0,3,2,1:T(2,128)(2,1)S(1)}, u32[]{:S(2)}, u32[]{:S(2)}) %collective-permute-start.2) | collective-permute-done | bytes 16416 | tf_op jit(solution)/shard_map/ppermute | solution.py:23
  163.9 1.9 fusion.3
  165.8 0.4 copy.32
  166.3 1.9 collective-permute-start.3
  168.3 1.9 collective-permute-done.3
  170.2 0.3 reshape.10
  170.5 17.0 %all_to_all.24 = f32[16,1,2048]{2,1,0:T(1,128)S(1)} all-to-all(f32[16,1,2048]{2,1,0:T(1,128)S(1)} %reshape.10), channel_id=1, replica_groups=mesh['col'=32,'z'=16,'core'=2] {'z'}, dimensions={0} | all-to-all | bytes 262144 | tf_op jit(solution)/shard_map/all_to_all | solution.py:44
  187.5 0.5 broadcast.4
  188.0 1.0 reduce.1
  189.2 0.6 fusion.5
  (15 shorter events, 0.5 us)
Async XLA Ops:
  6.5 157.4 %copy-start = (bf16[3,3,3,8,256]{4,3,2,1,0:T(8,128)(2,1)S(1)}, bf16[3,3,3,8,256]{4,3,2,1,0:T(8,128)(2,1)}, u32[]{:S(2)}) copy-start(bf16[3,3,3,8,256]{4,3,2,1,0:T(8,128)(2,1)} %param.5) | copy-start | bytes 331780
  6.5 94.8 %copy-start.2 = (bf16[3,3,3,8,256]{4,3,2,1,0:T(8,128)(2,1)S(1)}, bf16[3,3,3,8,256]{4,3,2,1,0:T(8,128)(2,1)}, u32[]{:S(2)}) copy-start(bf16[3,3,3,8,256]{4,3,2,1,0:T(8,128)(2,1)} %param.4) | copy-start | bytes 331780
  6.5 85.4 %all-gather.2.cloned.1.call-start = ((), (), s32[]{:S(2)}) async-start(), calls=%async_computation.2 | async-start | bytes 1081344 | tf_op jit(solution)/shard_map/all_gather | solution.py:48
  94.8 41.9 %collective-permute-start.1 = (bf16[2,1,64,8,256]{4,0,3,2,1:T(2,128)(2,1)}, bf16[2,1,64,8,256]{4,0,3,2,1:T(2,128)(2,1)}, u32[]{:S(2)}, u32[]{:S(2)}) collective-permute-start(bf16[2,1,64,8,256]{4,0,3,2,1:T(2,128)(2,1)} %get-tuple-element.8), channel_id=1, source_target_pairs={{32,0},{64,32},{96,64},{128,96},{160,128},{192,160},{224,192},{256... | collective-permute-start | bytes 1572872 | tf_op jit(solution)/shard_map/ppermute | solution.py:23
  99.4 37.3 %collective-permute-start = (bf16[2,1,64,8,256]{4,0,3,2,1:T(2,128)(2,1)}, bf16[2,1,64,8,256]{4,0,3,2,1:T(2,128)(2,1)}, u32[]{:S(2)}, u32[]{:S(2)}) collective-permute-start(bf16[2,1,64,8,256]{4,0,3,2,1:T(2,128)(2,1)} %get-tuple-element.7), channel_id=1, source_target_pairs={{0,32},{32,64},{64,96},{96,128},{128,160},{160,192},{192,224},{224... | collective-permute-start | bytes 1572872 | tf_op jit(solution)/shard_map/ppermute | solution.py:23
  131.2 5.6 %copy-start.1 = (bf16[2,2,64,8,256]{4,0,3,2,1:T(2,128)(2,1)S(1)}, bf16[2,2,64,8,256]{4,0,3,2,1:T(2,128)(2,1)}, u32[]{:S(2)}) copy-start(bf16[2,2,64,8,256]{4,0,3,2,1:T(2,128)(2,1)} %all-gather.2.cloned.1.call-done) | copy-start | bytes 3145732
  151.3 12.6 %collective-permute-start.2 = (bf16[2,1,64,8,8]{4,0,3,2,1:T(2,128)(2,1)S(1)}, bf16[2,1,64,8,8]{4,0,3,2,1:T(2,128)(2,1)S(1)}, u32[]{:S(2)}, u32[]{:S(2)}) collective-permute-start(bf16[2,1,64,8,8]{4,0,3,2,1:T(2,128)(2,1)S(1)} %slice.14), channel_id=1, source_target_pairs={{0,32},{32,64},{64,96},{96,128},{128,160},{160,192},{192,224},{224... | collective-permute-start | bytes 49160 | tf_op jit(solution)/shard_map/ppermute | solution.py:23
  166.3 3.8 %collective-permute-start.3 = (f32[16,8,2,1,32,4]{4,1,5,3,2,0:T(8,128)S(1)}, f32[16,8,2,1,32,4]{4,1,5,3,2,0:T(8,128)S(1)}, u32[]{:S(2)}, u32[]{:S(2)}) collective-permute-start(f32[16,8,2,1,32,4]{4,1,5,3,2,0:T(8,128)S(1)} %bitcast.39), channel_id=1, source_target_pairs={{0,1},{1,0},{2,3},{3,2},{4,5},{5,4},{6,7},{7,6},{8,9},{9,8},{10,11... | collective-permute-start | bytes 393224 | tf_op jit(solution)/shard_map/ppermute | solution.py:43
Sparse Core Ops, SparseCore 0:
  10.1 81.8 all-gather.1

commit v8 on v3

--- a/solution.py
+++ b/solution.py
@@ -34,6 +34,25 @@
     )
 
 
+def convolve_by_taps(volume, kernel):
+    samples, depth, rows, cols, width = volume.shape
+    taps = kernel.shape[:3]
+    filters = kernel.shape[-1]
+    flat = jnp.transpose(kernel, (3, 0, 1, 2, 4)).reshape(width, -1)
+    products = jnp.dot(volume.reshape(-1, width), flat, preferred_element_type=jnp.float32)
+    products = products.reshape((samples, depth, rows, cols, -1))
+    products = jnp.pad(products, ((0, 0), (0, 0), (1, 1), (1, 1), (0, 0)))
+    out = depth - taps[0] + 1
+    total = None
+    for a in range(taps[0]):
+        for b in range(taps[1]):
+            for c in range(taps[2]):
+                t = (a * taps[1] + b) * taps[2] + c
+                term = products[:, a : a + out, b : b + rows, c : c + cols, t * filters : (t + 1) * filters]
+                total = term if total is None else total + term
+    return total
+
+
 def reduce_scattered(partial):
     chips = lax.axis_size("z")
     mine = lax.axis_index("core")
@@ -48,7 +67,7 @@
     padded = extended(inputs, (("col", 1),), 1)
     gathered = lax.all_gather(lax.all_gather(padded, "core", axis=2, tiled=True), "z", axis=2, tiled=True)
     own_first = lax.all_to_all(first_filters, ("z", "core"), split_axis=4, concat_axis=3, tiled=True)
-    hidden = jnp.maximum(convolve(gathered, own_first, 1, 1), 0.0).astype(jnp.bfloat16)
+    hidden = jnp.maximum(convolve_by_taps(gathered, own_first), 0.0).astype(jnp.bfloat16)
     lower_plane = passed_along(hidden[:, -1:], "col", 1)
     stacked = jnp.concatenate([lower_plane, hidden], axis=1)
     partial = convolve(stacked, second_filters, 2, 1, out_spec="CNDHW")

time: 171 us -> 168 us (0.982)
  matrix products: 15.9 us -> 4.86 us
  other arithmetic: 1.79 us -> 9.48 us
    conv_general_dilated x2 -> x1, matrix products: 15.9 us -> 2.54 us  [convolve(): lax.conv_general_dilated(volume, kernel, (stride, stride, stride), ((0, 0...]
    convert_element_type x0 -> x1, other arithmetic: none -> 6.87 us  [per_device(): jnp.maximum(convolve_by_taps(gathered, own_first), 0.0).astype(jnp.bfloat16)]
    dot_general x0 -> x1, matrix products: none -> 2.32 us  [convolve_by_taps(): jnp.dot(volume.reshape(-1, width), flat, preferred_element_type=jnp.float32)]
    unnamed x8 -> x7, local copies, waits for them, and re-layouts: 7.99 us -> 7.16 us
where the time goes in v8:
time: 168 us; the launch traced here: 167 us
  blocking collectives  60.5 us (36%)
  waiting for transfers between devices  54.1 us (32%)
  local copies, waits for them, and re-layouts  14.4 us (9%)
  between operations  13.5 us (8%)
  starting transfers between devices  10.3 us (6%)
  other arithmetic  9.48 us (6%)
  matrix products  4.86 us (3%)
    all_to_all x1, blocking collectives, per_device(): lax.all_to_all(first_filters, ('z', 'core'), split_axis=4, concat_axis=3,...  36.6 us
    all_gather x1, waiting for transfers between devices, per_device(): lax.all_gather(lax.all_gather(padded, 'core', axis=2, tiled=True), 'z', a...  35.5 us
    all_to_all x1, blocking collectives, reduce_scattered(): return lax.all_to_all(half, 'z', 0, 0, tiled=True).sum(axis=0)  21.9 us
    ppermute x1, waiting for transfers between devices, passed_along(): return lax.ppermute(array, axis, pairs)  9.65 us
    unnamed x7, local copies, waits for them, and re-layouts  7.16 us
    ppermute x1, waiting for transfers between devices, extended(): lax.ppermute(lax.slice_in_dim(block, block.shape[dim] - width, None, axis...  7.01 us
    convert_element_type x1, other arithmetic, per_device(): jnp.maximum(convolve_by_taps(gathered, own_first), 0.0).astype(jnp.bfloat16)  6.87 us
    all_to_all x2, local copies, waits for them, and re-layouts, per_device(): lax.all_to_all(first_filters, ('z', 'core'), split_axis=4, concat_axis=3,...  5.49 us
  transfers between devices with their start and end apart: 5, of which 4 were waited for; matrix products, arithmetic and copies ran while one was open for 5% of the time, Pallas kernels for 0%

profile of v8, /device:TPU:32, one launch (start us, length us, event | category | flops | bytes accessed | tf_op | source)
XLA Modules:
  0.0 167.2 jit_solution(17039461736704424083)
XLA Ops:
  6.5 0.8 fusion.30
  7.3 4.5 %collective-permute-start.1 = (bf16[2,1,2,8,256]{4,3,2,1,0:T(8,128)(2,1)S(1)}, bf16[2,1,2,8,256]{4,3,2,1,0:T(8,128)(2,1)S(1)}, u32[]{:S(2)}, u32[]{:S(2)}) collective-permute-start(bf16[2,1,2,8,256]{4,3,2,1,0:T(8,128)(2,1)S(1)} %get-tuple-element.8), channel_id=1, source_target_pairs={{32,0},{64,32},{96,64},{128,96},{160,128},{192,160},{224,192},{256... | collective-permute-start | bytes 49160 | tf_op jit(solution)/shard_map/ppermute | solution.py:15
  11.9 1.9 %collective-permute-start = (bf16[2,1,2,8,256]{4,3,2,1,0:T(8,128)(2,1)S(1)}, bf16[2,1,2,8,256]{4,3,2,1,0:T(8,128)(2,1)S(1)}, u32[]{:S(2)}, u32[]{:S(2)}) collective-permute-start(bf16[2,1,2,8,256]{4,3,2,1,0:T(8,128)(2,1)S(1)} %get-tuple-element.7), channel_id=1, source_target_pairs={{0,32},{32,64},{64,96},{96,128},{128,160},{160,192},{192,224},{224... | collective-permute-start | bytes 49160 | tf_op jit(solution)/shard_map/ppermute | solution.py:12
  13.8 7.0 %collective-permute-done = bf16[2,1,2,8,256]{4,3,2,1,0:T(8,128)(2,1)S(1)} collective-permute-done((bf16[2,1,2,8,256]{4,3,2,1,0:T(8,128)(2,1)S(1)}, bf16[2,1,2,8,256]{4,3,2,1,0:T(8,128)(2,1)S(1)}, u32[]{:S(2)}, u32[]{:S(2)}) %collective-permute-start) | collective-permute-done | bytes 16416 | tf_op jit(solution)/shard_map/ppermute | solution.py:12
  20.8 0.8 pad_maximum_fusion.1
  21.6 2.0 %all_gather.6 = bf16[2,4,4,8,256]{4,3,2,1,0:T(8,128)(2,1)} all-gather(bf16[2,4,2,8,256]{4,3,2,1,0:T(8,128)(2,1)S(1)} %pad_maximum_fusion.1), channel_id=1, replica_groups=mesh['col'=32,'z'=16,'core'=2] {'core'}, dimensions={2}, use_global_device_ids=true | all-gather | bytes 196608 | tf_op jit(solution)/shard_map/all_gather | solution.py:68
  23.6 3.3 %copy.26 = bf16[3,3,3,8,256]{3,2,1,0,4:T(4,128)(2,1)S(1)} copy(bf16[3,3,3,8,256]{4,3,2,1,0:T(8,128)(2,1)} %param.4) | data formatting | bytes 221184 | tf_op args[1]
  27.0 1.8 %reshape.17 = bf16[32,2,864]{2,1,0:T(2,128)(2,1)S(1)} reshape(bf16[256,3,3,3,8]{4,3,2,1,0:T(4,128)(2,1)S(1)} %bitcast.44) | data formatting | bytes 221184
  28.8 36.6 %all_to_all.23 = bf16[32,2,864]{2,1,0:T(2,128)(2,1)S(1)} all-to-all(bf16[32,2,864]{2,1,0:T(2,128)(2,1)S(1)} %reshape.17), channel_id=1, replica_groups=mesh['col'=32,'z'=16,'core'=2] {'z','core'}, dimensions={0} | all-to-all | bytes 221184 | tf_op jit(solution)/shard_map/all_to_all | solution.py:69
  65.4 1.6 reshape.18
  67.0 2.1 %copy.44 = bf16[3,3,3,8,32,8]{3,4,5,2,1,0:T(8,128)(2,1)} copy(bf16[3,3,3,8,32,8]{3,2,1,0,5,4:T(4,128)(2,1)S(1)} %bitcast.43) | data formatting | bytes 221184 | tf_op jit(solution)/shard_map/all_to_all | solution.py:69
  69.1 3.4 %all_to_all.19 = bf16[3,3,3,256,8]{3,4,2,1,0:T(8,128)(2,1)S(1)} reshape(bf16[3,3,3,32,8,8]{4,3,5,2,1,0:T(8,128)(2,1)} %bitcast.45) | data formatting | bytes 221184 | tf_op jit(solution)/shard_map/all_to_all | solution.py:69
  72.5 35.5 %all-gather.2.cloned.1.call-done = bf16[2,4,64,8,256]{4,3,2,1,0:T(8,128)(2,1)} async-done(((bf16[2,4,4,8,256]{4,3,2,1,0:T(8,128)(2,1)}), bf16[2,4,64,8,256]{4,3,2,1,0:T(8,128)(2,1)}) %all-gather.2.cloned.1.call-update) | async-done | bytes 2097168 | tf_op jit(solution)/shard_map/all_gather | solution.py:68
  108.0 2.3 %fusion.32 = f32[2,4,64,8,216]{4,3,2,1,0:T(8,128)S(1)} fusion(bf16[2,4,64,8,256]{4,3,2,1,0:T(8,128)(2,1)} %all-gather.2.cloned.1.call-done, bf16[256,216,1,1,1]{0,1,4,3,2:T(8,128)(2,1)S(1)} %bitcast.48), kind=kOutput, calls=%fused_computation.66 | convolution fusion | flops 452984832 | bytes 5746688 | tf_op jit(solution)/shard_map/dot_general | solution.py:42
  110.3 6.9 %maximum_convert_fusion = bf16[2,2,64,8,8]{4,3,2,1,0:T(8,128)(2,1)S(1)} fusion(f32[2,4,64,8,216]{4,3,2,1,0:T(8,128)S(1)} %fusion.32), kind=kLoop, calls=%fused_computation.51 | loop fusion | flops 458752 | bytes 7372800 | tf_op jit(solution)/shard_map/convert_element_type | solution.py:70
  117.3 1.9 %collective-permute-start.2 = (bf16[2,1,64,8,8]{4,3,2,1,0:T(8,128)(2,1)S(1)}, bf16[2,1,64,8,8]{4,3,2,1,0:T(8,128)(2,1)S(1)}, u32[]{:S(2)}, u32[]{:S(2)}) collective-permute-start(bf16[2,1,64,8,8]{4,3,2,1,0:T(8,128)(2,1)S(1)} %slice.126), channel_id=1, source_target_pairs={{0,32},{32,64},{64,96},{96,128},{128,160},{160,192},{192,224},{224... | collective-permute-start | bytes 49160 | tf_op jit(solution)/shard_map/ppermute | solution.py:23
  119.2 9.7 %collective-permute-done.2 = bf16[2,1,64,8,8]{4,3,2,1,0:T(8,128)(2,1)S(1)} collective-permute-done((bf16[2,1,64,8,8]{4,3,2,1,0:T(8,128)(2,1)S(1)}, bf16[2,1,64,8,8]{4,3,2,1,0:T(8,128)(2,1)S(1)}, u32[]{:S(2)}, u32[]{:S(2)}) %collective-permute-start.2) | collective-permute-done | bytes 16416 | tf_op jit(solution)/shard_map/ppermute | solution.py:23
  129.0 2.5 %fusion.26 = f32[256,2,1,32,4]{0,1,4,3,2:T(2,128)S(1)} fusion(bf16[3,3,3,8,256]{4,3,2,1,0:T(8,128)(2,1)S(1)} %copy-done, bf16[2,3,64,8,8]{4,3,2,1,0:T(8,128)(2,1)S(1)} %pad_maximum_fusion), kind=kOutput, calls=%fused_computation.53 | convolution fusion | flops 25681920 | bytes 421888 | tf_op jit(solution)/shard_map/conv_general_dilated | solution.py:27
  132.1 1.9 %collective-permute-start.3 = (f32[16,8,2,1,32,4]{4,1,5,3,2,0:T(8,128)S(1)}, f32[16,8,2,1,32,4]{4,1,5,3,2,0:T(8,128)S(1)}, u32[]{:S(2)}, u32[]{:S(2)}) collective-permute-start(f32[16,8,2,1,32,4]{4,1,5,3,2,0:T(8,128)S(1)} %bitcast.47), channel_id=1, source_target_pairs={{0,1},{1,0},{2,3},{3,2},{4,5},{5,4},{6,7},{7,6},{8,9},{9,8},{10,11... | collective-permute-start | bytes 393224 | tf_op jit(solution)/shard_map/ppermute | solution.py:62
  134.0 1.9 %collective-permute-done.3 = f32[16,8,2,1,32,4]{4,1,5,3,2,0:T(8,128)S(1)} collective-permute-done((f32[16,8,2,1,32,4]{4,1,5,3,2,0:T(8,128)S(1)}, f32[16,8,2,1,32,4]{4,1,5,3,2,0:T(8,128)S(1)}, u32[]{:S(2)}, u32[]{:S(2)}) %collective-permute-start.3) | collective-permute-done | bytes 131104 | tf_op jit(solution)/shard_map/ppermute | solution.py:62
  136.2 21.9 %all_to_all.24 = f32[16,1,2048]{2,1,0:T(1,128)S(1)} all-to-all(f32[16,1,2048]{2,1,0:T(1,128)S(1)} %reshape.19), channel_id=1, replica_groups=mesh['col'=32,'z'=16,'core'=2] {'z'}, dimensions={0} | all-to-all | bytes 262144 | tf_op jit(solution)/shard_map/all_to_all | solution.py:63
  158.1 0.5 broadcast.6
  158.6 1.0 reduce.1
  159.8 0.6 fusion.29
  (14 shorter events, 1.2 us)
Async XLA Ops:
  6.5 122.5 %copy-start = (bf16[3,3,3,8,256]{4,3,2,1,0:T(8,128)(2,1)S(1)}, bf16[3,3,3,8,256]{4,3,2,1,0:T(8,128)(2,1)}, u32[]{:S(2)}) copy-start(bf16[3,3,3,8,256]{4,3,2,1,0:T(8,128)(2,1)} %param.5) | copy-start | bytes 331780
  6.5 101.5 %all-gather.2.cloned.1.call-start = ((), (), s32[]{:S(2)}) async-start(), calls=%async_computation.2 | async-start | bytes 2228224 | tf_op jit(solution)/shard_map/all_gather | solution.py:68
  7.3 6.5 %collective-permute-start.1 = (bf16[2,1,2,8,256]{4,3,2,1,0:T(8,128)(2,1)S(1)}, bf16[2,1,2,8,256]{4,3,2,1,0:T(8,128)(2,1)S(1)}, u32[]{:S(2)}, u32[]{:S(2)}) collective-permute-start(bf16[2,1,2,8,256]{4,3,2,1,0:T(8,128)(2,1)S(1)} %get-tuple-element.8), channel_id=1, source_target_pairs={{32,0},{64,32},{96,64},{128,96},{160,128},{192,160},{224,192},{256... | collective-permute-start | bytes 49160 | tf_op jit(solution)/shard_map/ppermute | solution.py:15
  11.9 9.0 %collective-permute-start = (bf16[2,1,2,8,256]{4,3,2,1,0:T(8,128)(2,1)S(1)}, bf16[2,1,2,8,256]{4,3,2,1,0:T(8,128)(2,1)S(1)}, u32[]{:S(2)}, u32[]{:S(2)}) collective-permute-start(bf16[2,1,2,8,256]{4,3,2,1,0:T(8,128)(2,1)S(1)} %get-tuple-element.7), channel_id=1, source_target_pairs={{0,32},{32,64},{64,96},{96,128},{128,160},{160,192},{192,224},{224... | collective-permute-start | bytes 49160 | tf_op jit(solution)/shard_map/ppermute | solution.py:12
  117.3 11.6 %collective-permute-start.2 = (bf16[2,1,64,8,8]{4,3,2,1,0:T(8,128)(2,1)S(1)}, bf16[2,1,64,8,8]{4,3,2,1,0:T(8,128)(2,1)S(1)}, u32[]{:S(2)}, u32[]{:S(2)}) collective-permute-start(bf16[2,1,64,8,8]{4,3,2,1,0:T(8,128)(2,1)S(1)} %slice.126), channel_id=1, source_target_pairs={{0,32},{32,64},{64,96},{96,128},{128,160},{160,192},{192,224},{224... | collective-permute-start | bytes 49160 | tf_op jit(solution)/shard_map/ppermute | solution.py:23
  132.1 3.8 %collective-permute-start.3 = (f32[16,8,2,1,32,4]{4,1,5,3,2,0:T(8,128)S(1)}, f32[16,8,2,1,32,4]{4,1,5,3,2,0:T(8,128)S(1)}, u32[]{:S(2)}, u32[]{:S(2)}) collective-permute-start(f32[16,8,2,1,32,4]{4,1,5,3,2,0:T(8,128)S(1)} %bitcast.47), channel_id=1, source_target_pairs={{0,1},{1,0},{2,3},{3,2},{4,5},{5,4},{6,7},{7,6},{8,9},{9,8},{10,11... | collective-permute-start | bytes 393224 | tf_op jit(solution)/shard_map/ppermute | solution.py:62
Sparse Core Ops, SparseCore 0:
  23.8 84.2 all-gather.1

commit v9 on v8

--- a/solution.py
+++ b/solution.py
@@ -40,15 +40,20 @@
     filters = kernel.shape[-1]
     flat = jnp.transpose(kernel, (3, 0, 1, 2, 4)).reshape(width, -1)
     products = jnp.dot(volume.reshape(-1, width), flat, preferred_element_type=jnp.float32)
-    products = products.reshape((samples, depth, rows, cols, -1))
+    return products.reshape((samples, depth, rows, cols, -1))
+
+
+def tap_sum(products, kernel, plane, rows, cols):
     products = jnp.pad(products, ((0, 0), (0, 0), (1, 1), (1, 1), (0, 0)))
-    out = depth - taps[0] + 1
+    taps = kernel.shape[:3]
+    filters = kernel.shape[-1]
+    out = 1
     total = None
     for a in range(taps[0]):
         for b in range(taps[1]):
             for c in range(taps[2]):
                 t = (a * taps[1] + b) * taps[2] + c
-                term = products[:, a : a + out, b : b + rows, c : c + cols, t * filters : (t + 1) * filters]
+                term = products[:, plane + a : plane + a + out, b : b + rows, c : c + cols, t * filters : (t + 1) * filters]
                 total = term if total is None else total + term
     return total
 
@@ -67,9 +72,13 @@
     padded = extended(inputs, (("col", 1),), 1)
     gathered = lax.all_gather(lax.all_gather(padded, "core", axis=2, tiled=True), "z", axis=2, tiled=True)
     own_first = lax.all_to_all(first_filters, ("z", "core"), split_axis=4, concat_axis=3, tiled=True)
-    hidden = jnp.maximum(convolve_by_taps(gathered, own_first), 0.0).astype(jnp.bfloat16)
-    lower_plane = passed_along(hidden[:, -1:], "col", 1)
-    stacked = jnp.concatenate([lower_plane, hidden], axis=1)
+    products = convolve_by_taps(gathered, own_first)
+    rows, cols = gathered.shape[2], gathered.shape[3]
+    last = jnp.maximum(tap_sum(products, own_first, 1, rows, cols), 0.0).astype(jnp.bfloat16)
+    lower_plane = passed_along(last, "col", 1)
+    products, _ = lax.optimization_barrier((products, last))
+    first = jnp.maximum(tap_sum(products, own_first, 0, rows, cols), 0.0).astype(jnp.bfloat16)
+    stacked = jnp.concatenate([lower_plane, first, last], axis=1)
     partial = convolve(stacked, second_filters, 2, 1, out_spec="CNDHW")
     totals = reduce_scattered(partial)
     return jnp.maximum(jnp.transpose(totals, (1, 2, 3, 4, 0)), 0.0).astype(jnp.bfloat16)

time: 168 us -> 164 us (0.976)
  blocking collectives: 60.5 us -> 24.6 us
  starting transfers between devices: 10.3 us -> 33.6 us
  waiting for transfers between devices: 54.1 us -> 61.8 us
    all_to_all x1 -> x0, blocking collectives: 36.6 us -> none  [per_device(): lax.all_to_all(first_filters, ('z', 'core'), split_axis=4, concat_axis=3,...]
    all_to_all x0 -> x1, starting transfers between devices: none -> 19.1 us  [per_device(): lax.all_to_all(first_filters, ('z', 'core'), split_axis=4, concat_axis=3,...]
    all_to_all x0 -> x1, waiting for transfers between devices: none -> 17 us  [per_device(): lax.all_to_all(first_filters, ('z', 'core'), split_axis=4, concat_axis=3,...]
    ppermute x1, waiting for transfers between devices: 7.01 us -> 0.01 us  [extended(): lax.ppermute(lax.slice_in_dim(block, block.shape[dim] - width, None, axis...]
    ppermute x1, waiting for transfers between devices: 9.65 us -> 4.78 us  [passed_along(): return lax.ppermute(array, axis, pairs)]
    convert_element_type x1 -> x2, other arithmetic: 6.87 us -> 6.81 us  [the longest x1 3.4 us: per_device(): jnp.maximum(tap_sum(products, own_first, 1, rows, cols), 0.0)]
  transfers between devices with their start and end apart: 5 -> 6, of which waited for: 4 -> 5; matrix products, arithmetic and copies ran while one was open for 5% -> 8% of each run, Pallas kernels for 0% -> 0%
where the time goes in v9:
time: 164 us; the launch traced here: 163 us
  waiting for transfers between devices  61.8 us (38%)
  starting transfers between devices  33.6 us (20%)
  blocking collectives  24.6 us (15%)
  local copies, waits for them, and re-layouts  15.2 us (9%)
  between operations  13.5 us (8%)
  other arithmetic  9.46 us (6%)
  matrix products  4.86 us (3%)
    all_gather x1, waiting for transfers between devices, per_device(): lax.all_gather(lax.all_gather(padded, 'core', axis=2, tiled=True), 'z', a...  36.7 us
    all_to_all x1, blocking collectives, reduce_scattered(): return lax.all_to_all(half, 'z', 0, 0, tiled=True).sum(axis=0)  22.6 us
    all_to_all x1, starting transfers between devices, per_device(): lax.all_to_all(first_filters, ('z', 'core'), split_axis=4, concat_axis=3,...  19.1 us
    all_to_all x1, waiting for transfers between devices, per_device(): lax.all_to_all(first_filters, ('z', 'core'), split_axis=4, concat_axis=3,...  17 us
    unnamed x7, local copies, waits for them, and re-layouts  7.91 us
    ppermute x1, starting transfers between devices, extended(): lax.ppermute(lax.slice_in_dim(block, 0, width, axis=dim), axis, backward)  5.76 us
    all_to_all x2, local copies, waits for them, and re-layouts, per_device(): lax.all_to_all(first_filters, ('z', 'core'), split_axis=4, concat_axis=3,...  5.49 us
    ppermute x1, waiting for transfers between devices, passed_along(): return lax.ppermute(array, axis, pairs)  4.78 us
  transfers between devices with their start and end apart: 6, of which 5 were waited for; matrix products, arithmetic and copies ran while one was open for 8% of the time, Pallas kernels for 0%

profile of v9, /device:TPU:32, one launch (start us, length us, event | category | flops | bytes accessed | tf_op | source)
XLA Modules:
  0.0 163.0 jit_solution(10708828275333186117)
XLA Ops:
  6.5 0.8 fusion.56
  7.3 3.4 %collective-permute-start = (bf16[2,1,2,8,256]{4,3,2,1,0:T(8,128)(2,1)S(1)}, bf16[2,1,2,8,256]{4,3,2,1,0:T(8,128)(2,1)S(1)}, u32[]{:S(2)}, u32[]{:S(2)}) collective-permute-start(bf16[2,1,2,8,256]{4,3,2,1,0:T(8,128)(2,1)S(1)} %get-tuple-element.9), channel_id=1, source_target_pairs={{0,32},{32,64},{64,96},{96,128},{128,160},{160,192},{192,224},{224... | collective-permute-start | bytes 49160 | tf_op jit(solution)/shard_map/ppermute | solution.py:12
  10.7 5.8 %collective-permute-start.1 = (bf16[2,1,2,8,256]{4,3,2,1,0:T(8,128)(2,1)S(1)}, bf16[2,1,2,8,256]{4,3,2,1,0:T(8,128)(2,1)S(1)}, u32[]{:S(2)}, u32[]{:S(2)}) collective-permute-start(bf16[2,1,2,8,256]{4,3,2,1,0:T(8,128)(2,1)S(1)} %get-tuple-element.10), channel_id=1, source_target_pairs={{32,0},{64,32},{96,64},{128,96},{160,128},{192,160},{224,192},{256... | collective-permute-start | bytes 49160 | tf_op jit(solution)/shard_map/ppermute | solution.py:15
  16.5 1.4 collective-permute-done.1
  17.9 0.8 pad_maximum_fusion.1
  18.7 2.0 %all_gather.6 = bf16[2,4,4,8,256]{4,3,2,1,0:T(8,128)(2,1)} all-gather(bf16[2,4,2,8,256]{4,3,2,1,0:T(8,128)(2,1)S(1)} %pad_maximum_fusion.1), channel_id=1, replica_groups=mesh['col'=32,'z'=16,'core'=2] {'core'}, dimensions={2}, use_global_device_ids=true | all-gather | bytes 196608 | tf_op jit(solution)/shard_map/all_gather | solution.py:73
  20.7 3.3 %copy.28 = bf16[3,3,3,8,256]{3,2,1,0,4:T(4,128)(2,1)S(1)} copy(bf16[3,3,3,8,256]{4,3,2,1,0:T(8,128)(2,1)} %param.4) | data formatting | bytes 221184 | tf_op args[1]
  24.1 2.5 %reshape.17 = bf16[32,2,864]{2,1,0:T(2,128)(2,1)} reshape(bf16[256,3,3,3,8]{4,3,2,1,0:T(4,128)(2,1)S(1)} %bitcast.44) | data formatting | bytes 221184
  26.6 19.1 %all-to-all-start = ((bf16[32,2,864]{2,1,0:T(2,128)(2,1)}), bf16[32,2,864]{2,1,0:T(2,128)(2,1)S(1)}, u32[]{:S(2)}, u32[]{:S(2)}) async-start(bf16[32,2,864]{2,1,0:T(2,128)(2,1)} %reshape.17), calls=%async_computation | async-start | bytes 229376 | tf_op jit(solution)/shard_map/all_to_all | solution.py:74
  45.8 17.0 %all-to-all-done = bf16[32,2,864]{2,1,0:T(2,128)(2,1)S(1)} async-done(((bf16[32,2,864]{2,1,0:T(2,128)(2,1)}), bf16[32,2,864]{2,1,0:T(2,128)(2,1)S(1)}, u32[]{:S(2)}, u32[]{:S(2)}) %all-to-all-start) | async-done | bytes 110624 | tf_op jit(solution)/shard_map/all_to_all | solution.py:74
  62.7 1.6 reshape.18
  64.4 2.0 %copy.46 = bf16[3,3,3,8,32,8]{3,4,5,2,1,0:T(8,128)(2,1)} copy(bf16[3,3,3,8,32,8]{3,2,1,0,5,4:T(4,128)(2,1)S(1)} %bitcast.43) | data formatting | bytes 221184 | tf_op jit(solution)/shard_map/all_to_all | solution.py:74
  66.4 3.4 %all_to_all.19 = bf16[3,3,3,256,8]{3,4,2,1,0:T(8,128)(2,1)S(1)} reshape(bf16[3,3,3,32,8,8]{4,3,5,2,1,0:T(8,128)(2,1)} %bitcast.45) | data formatting | bytes 221184 | tf_op jit(solution)/shard_map/all_to_all | solution.py:74
  69.9 36.7 %all-gather.2.cloned.1.call-done = bf16[2,4,64,8,256]{4,3,2,1,0:T(8,128)(2,1)} async-done(((bf16[2,4,4,8,256]{4,3,2,1,0:T(8,128)(2,1)}), bf16[2,4,64,8,256]{4,3,2,1,0:T(8,128)(2,1)}) %all-gather.2.cloned.1.call-update) | async-done | bytes 2097168 | tf_op jit(solution)/shard_map/all_gather | solution.py:73
  106.6 2.3 %fusion.58 = f32[2,4,64,8,216]{4,3,2,1,0:T(8,128)S(1)} fusion(bf16[2,4,64,8,256]{4,3,2,1,0:T(8,128)(2,1)} %all-gather.2.cloned.1.call-done, bf16[256,216,1,1,1]{0,1,4,3,2:T(8,128)(2,1)S(1)} %bitcast.48), kind=kOutput, calls=%fused_computation.117 | convolution fusion | flops 452984832 | bytes 5746688 | tf_op jit(solution)/shard_map/dot_general | solution.py:42
  108.9 3.4 %maximum_convert_fusion.1 = bf16[2,1,64,8,8]{4,3,2,1,0:T(8,128)(2,1)S(1)} fusion(f32[2,4,64,8,216]{4,3,2,1,0:T(8,128)S(1)} %fusion.58), kind=kLoop, calls=%fused_computation.108 | loop fusion | flops 229376 | bytes 5783552 | tf_op jit(solution)/shard_map/convert_element_type | solution.py:77
  112.3 3.4 %collective-permute-start.2 = (bf16[2,1,64,8,8]{4,3,2,1,0:T(8,128)(2,1)S(1)}, bf16[2,1,64,8,8]{4,3,2,1,0:T(8,128)(2,1)S(1)}, u32[]{:S(2)}, u32[]{:S(2)}) collective-permute-start(bf16[2,1,64,8,8]{4,3,2,1,0:T(8,128)(2,1)S(1)} %maximum_convert_fusion.1), channel_id=1, source_target_pairs={{0,32},{32,64},{64,96},{96,128},{128,160},{160,192},{192,224},{224... | collective-permute-start | bytes 49160 | tf_op jit(solution)/shard_map/ppermute | solution.py:23
  115.7 3.4 %maximum_convert_fusion = bf16[2,1,64,8,8]{4,3,2,1,0:T(8,128)(2,1)S(1)} fusion(f32[2,4,64,8,216]{4,3,2,1,0:T(8,128)S(1)} %fusion.58), kind=kLoop, calls=%fused_computation.107 | loop fusion | flops 229376 | bytes 5783552 | tf_op jit(solution)/shard_map/convert_element_type | solution.py:80
  119.1 4.8 %collective-permute-done.2 = bf16[2,1,64,8,8]{4,3,2,1,0:T(8,128)(2,1)S(1)} collective-permute-done((bf16[2,1,64,8,8]{4,3,2,1,0:T(8,128)(2,1)S(1)}, bf16[2,1,64,8,8]{4,3,2,1,0:T(8,128)(2,1)S(1)}, u32[]{:S(2)}, u32[]{:S(2)}) %collective-permute-start.2) | collective-permute-done | bytes 16416 | tf_op jit(solution)/shard_map/ppermute | solution.py:23
  124.1 2.5 %fusion = f32[256,2,1,32,4]{0,1,4,3,2:T(2,128)S(1)} fusion(bf16[3,3,3,8,256]{4,3,2,1,0:T(8,128)(2,1)S(1)} %copy-done, bf16[2,3,64,8,8]{4,3,2,1,0:T(8,128)(2,1)S(1)} %pad_maximum_fusion), kind=kOutput, calls=%fused_computation.50 | convolution fusion | flops 25681920 | bytes 421888 | tf_op jit(solution)/shard_map/conv_general_dilated | solution.py:27
  127.2 1.9 %collective-permute-start.3 = (f32[16,8,2,1,32,4]{4,1,5,3,2,0:T(8,128)S(1)}, f32[16,8,2,1,32,4]{4,1,5,3,2,0:T(8,128)S(1)}, u32[]{:S(2)}, u32[]{:S(2)}) collective-permute-start(f32[16,8,2,1,32,4]{4,1,5,3,2,0:T(8,128)S(1)} %bitcast.47), channel_id=1, source_target_pairs={{0,1},{1,0},{2,3},{3,2},{4,5},{5,4},{6,7},{7,6},{8,9},{9,8},{10,11... | collective-permute-start | bytes 393224 | tf_op jit(solution)/shard_map/ppermute | solution.py:67
  129.1 1.9 %collective-permute-done.3 = f32[16,8,2,1,32,4]{4,1,5,3,2,0:T(8,128)S(1)} collective-permute-done((f32[16,8,2,1,32,4]{4,1,5,3,2,0:T(8,128)S(1)}, f32[16,8,2,1,32,4]{4,1,5,3,2,0:T(8,128)S(1)}, u32[]{:S(2)}, u32[]{:S(2)}) %collective-permute-start.3) | collective-permute-done | bytes 131104 | tf_op jit(solution)/shard_map/ppermute | solution.py:67
  131.3 22.6 %all_to_all.23 = f32[16,1,2048]{2,1,0:T(1,128)S(1)} all-to-all(f32[16,1,2048]{2,1,0:T(1,128)S(1)} %reshape.19), channel_id=1, replica_groups=mesh['col'=32,'z'=16,'core'=2] {'z'}, dimensions={0} | all-to-all | bytes 262144 | tf_op jit(solution)/shard_map/all_to_all | solution.py:68
  154.4 1.0 reduce.1
  (15 shorter events, 2.4 us)
Async XLA Ops:
  6.5 117.6 %copy-start = (bf16[3,3,3,8,256]{4,3,2,1,0:T(8,128)(2,1)S(1)}, bf16[3,3,3,8,256]{4,3,2,1,0:T(8,128)(2,1)}, u32[]{:S(2)}) copy-start(bf16[3,3,3,8,256]{4,3,2,1,0:T(8,128)(2,1)} %param.5) | copy-start | bytes 331780
  6.5 100.0 %all-gather.2.cloned.1.call-start = ((), (), s32[]{:S(2)}) async-start(), calls=%async_computation.2 | async-start | bytes 2228224 | tf_op jit(solution)/shard_map/all_gather | solution.py:73
  7.3 9.2 %collective-permute-start = (bf16[2,1,2,8,256]{4,3,2,1,0:T(8,128)(2,1)S(1)}, bf16[2,1,2,8,256]{4,3,2,1,0:T(8,128)(2,1)S(1)}, u32[]{:S(2)}, u32[]{:S(2)}) collective-permute-start(bf16[2,1,2,8,256]{4,3,2,1,0:T(8,128)(2,1)S(1)} %get-tuple-element.9), channel_id=1, source_target_pairs={{0,32},{32,64},{64,96},{96,128},{128,160},{160,192},{192,224},{224... | collective-permute-start | bytes 49160 | tf_op jit(solution)/shard_map/ppermute | solution.py:12
  10.7 7.2 %collective-permute-start.1 = (bf16[2,1,2,8,256]{4,3,2,1,0:T(8,128)(2,1)S(1)}, bf16[2,1,2,8,256]{4,3,2,1,0:T(8,128)(2,1)S(1)}, u32[]{:S(2)}, u32[]{:S(2)}) collective-permute-start(bf16[2,1,2,8,256]{4,3,2,1,0:T(8,128)(2,1)S(1)} %get-tuple-element.10), channel_id=1, source_target_pairs={{32,0},{64,32},{96,64},{128,96},{160,128},{192,160},{224,192},{256... | collective-permute-start | bytes 49160 | tf_op jit(solution)/shard_map/ppermute | solution.py:15
  26.6 36.1 %all-to-all-start = ((bf16[32,2,864]{2,1,0:T(2,128)(2,1)}), bf16[32,2,864]{2,1,0:T(2,128)(2,1)S(1)}, u32[]{:S(2)}, u32[]{:S(2)}) async-start(bf16[32,2,864]{2,1,0:T(2,128)(2,1)} %reshape.17), calls=%async_computation | async-start | bytes 229376 | tf_op jit(solution)/shard_map/all_to_all | solution.py:74
  112.3 11.6 %collective-permute-start.2 = (bf16[2,1,64,8,8]{4,3,2,1,0:T(8,128)(2,1)S(1)}, bf16[2,1,64,8,8]{4,3,2,1,0:T(8,128)(2,1)S(1)}, u32[]{:S(2)}, u32[]{:S(2)}) collective-permute-start(bf16[2,1,64,8,8]{4,3,2,1,0:T(8,128)(2,1)S(1)} %maximum_convert_fusion.1), channel_id=1, source_target_pairs={{0,32},{32,64},{64,96},{96,128},{128,160},{160,192},{192,224},{224... | collective-permute-start | bytes 49160 | tf_op jit(solution)/shard_map/ppermute | solution.py:23
  127.2 3.8 %collective-permute-start.3 = (f32[16,8,2,1,32,4]{4,1,5,3,2,0:T(8,128)S(1)}, f32[16,8,2,1,32,4]{4,1,5,3,2,0:T(8,128)S(1)}, u32[]{:S(2)}, u32[]{:S(2)}) collective-permute-start(f32[16,8,2,1,32,4]{4,1,5,3,2,0:T(8,128)S(1)} %bitcast.47), channel_id=1, source_target_pairs={{0,1},{1,0},{2,3},{3,2},{4,5},{5,4},{6,7},{7,6},{8,9},{9,8},{10,11... | collective-permute-start | bytes 393224 | tf_op jit(solution)/shard_map/ppermute | solution.py:67
Sparse Core Ops, SparseCore 0:
  20.8 85.6 all-gather.1

commit v10 on v9

--- a/solution.py
+++ b/solution.py
@@ -78,8 +78,9 @@
     lower_plane = passed_along(last, "col", 1)
     products, _ = lax.optimization_barrier((products, last))
     first = jnp.maximum(tap_sum(products, own_first, 0, rows, cols), 0.0).astype(jnp.bfloat16)
-    stacked = jnp.concatenate([lower_plane, first, last], axis=1)
-    partial = convolve(stacked, second_filters, 2, 1, out_spec="CNDHW")
+    own = jnp.concatenate([first, last], axis=1)
+    partial = convolve(own, second_filters[1:], 2, 1, out_spec="CNDHW")
+    partial = partial + convolve(lower_plane, second_filters[:1], 2, 1, out_spec="CNDHW")
     totals = reduce_scattered(partial)
     return jnp.maximum(jnp.transpose(totals, (1, 2, 3, 4, 0)), 0.0).astype(jnp.bfloat16)
 

time: 164 us -> 162 us (0.988)
  waiting for transfers between devices: 61.8 us -> 59.8 us
    ppermute x1, waiting for transfers between devices: 4.78 us -> 2.79 us  [passed_along(): return lax.ppermute(array, axis, pairs)]
  transfers between devices with their start and end apart: 6 -> 6, of which waited for: 5 -> 5; matrix products, arithmetic and copies ran while one was open for 8% -> 9% of each run, Pallas kernels for 0% -> 0%
where the time goes in v10:
time: 162 us; the launch traced here: 161 us
  waiting for transfers between devices  59.8 us (37%)
  starting transfers between devices  33.7 us (21%)
  blocking collectives  24.6 us (15%)
  local copies, waits for them, and re-layouts  15.1 us (9%)
  between operations  13.6 us (8%)
  other arithmetic  9.37 us (6%)
  matrix products  4.8 us (3%)
    all_gather x1, waiting for transfers between devices, per_device(): lax.all_gather(lax.all_gather(padded, 'core', axis=2, tiled=True), 'z', a...  36.7 us
    all_to_all x1, blocking collectives, reduce_scattered(): return lax.all_to_all(half, 'z', 0, 0, tiled=True).sum(axis=0)  22.5 us
    all_to_all x1, starting transfers between devices, per_device(): lax.all_to_all(first_filters, ('z', 'core'), split_axis=4, concat_axis=3,...  19.2 us
    all_to_all x1, waiting for transfers between devices, per_device(): lax.all_to_all(first_filters, ('z', 'core'), split_axis=4, concat_axis=3,...  17 us
    unnamed x7, local copies, waits for them, and re-layouts  7.87 us
    ppermute x1, starting transfers between devices, extended(): lax.ppermute(lax.slice_in_dim(block, 0, width, axis=dim), axis, backward)  5.76 us
    all_to_all x2, local copies, waits for them, and re-layouts, per_device(): lax.all_to_all(first_filters, ('z', 'core'), split_axis=4, concat_axis=3,...  5.49 us
    ppermute x1, starting transfers between devices, passed_along(): return lax.ppermute(array, axis, pairs)  3.48 us
  transfers between devices with their start and end apart: 6, of which 5 were waited for; matrix products, arithmetic and copies ran while one was open for 9% of the time, Pallas kernels for 0%

profile of v10, /device:TPU:32, one launch (start us, length us, event | category | flops | bytes accessed | tf_op | source)
XLA Modules:
  0.0 160.8 jit_solution(16283604068379993224)
XLA Ops:
  6.5 0.7 fusion.59
  7.3 3.4 %collective-permute-start = (bf16[2,1,2,8,256]{4,3,2,1,0:T(8,128)(2,1)S(1)}, bf16[2,1,2,8,256]{4,3,2,1,0:T(8,128)(2,1)S(1)}, u32[]{:S(2)}, u32[]{:S(2)}) collective-permute-start(bf16[2,1,2,8,256]{4,3,2,1,0:T(8,128)(2,1)S(1)} %get-tuple-element.9), channel_id=1, source_target_pairs={{0,32},{32,64},{64,96},{96,128},{128,160},{160,192},{192,224},{224... | collective-permute-start | bytes 49160 | tf_op jit(solution)/shard_map/ppermute | solution.py:12
  10.7 5.8 %collective-permute-start.1 = (bf16[2,1,2,8,256]{4,3,2,1,0:T(8,128)(2,1)S(1)}, bf16[2,1,2,8,256]{4,3,2,1,0:T(8,128)(2,1)S(1)}, u32[]{:S(2)}, u32[]{:S(2)}) collective-permute-start(bf16[2,1,2,8,256]{4,3,2,1,0:T(8,128)(2,1)S(1)} %get-tuple-element.10), channel_id=1, source_target_pairs={{32,0},{64,32},{96,64},{128,96},{160,128},{192,160},{224,192},{256... | collective-permute-start | bytes 49160 | tf_op jit(solution)/shard_map/ppermute | solution.py:15
  16.5 1.4 collective-permute-done.1
  17.9 0.8 pad_maximum_fusion.1
  18.6 2.0 %all_gather.6 = bf16[2,4,4,8,256]{4,3,2,1,0:T(8,128)(2,1)} all-gather(bf16[2,4,2,8,256]{4,3,2,1,0:T(8,128)(2,1)S(1)} %pad_maximum_fusion.1), channel_id=1, replica_groups=mesh['col'=32,'z'=16,'core'=2] {'core'}, dimensions={2}, use_global_device_ids=true | all-gather | bytes 196608 | tf_op jit(solution)/shard_map/all_gather | solution.py:73
  20.7 3.3 %copy.30 = bf16[3,3,3,8,256]{3,2,1,0,4:T(4,128)(2,1)S(1)} copy(bf16[3,3,3,8,256]{4,3,2,1,0:T(8,128)(2,1)} %param.4) | data formatting | bytes 221184 | tf_op args[1]
  24.0 2.5 %reshape.17 = bf16[32,2,864]{2,1,0:T(2,128)(2,1)} reshape(bf16[256,3,3,3,8]{4,3,2,1,0:T(4,128)(2,1)S(1)} %bitcast.43) | data formatting | bytes 221184
  26.5 19.2 %all-to-all-start = ((bf16[32,2,864]{2,1,0:T(2,128)(2,1)}), bf16[32,2,864]{2,1,0:T(2,128)(2,1)S(1)}, u32[]{:S(2)}, u32[]{:S(2)}) async-start(bf16[32,2,864]{2,1,0:T(2,128)(2,1)} %reshape.17), calls=%async_computation | async-start | bytes 229376 | tf_op jit(solution)/shard_map/all_to_all | solution.py:74
  45.7 17.0 %all-to-all-done = bf16[32,2,864]{2,1,0:T(2,128)(2,1)S(1)} async-done(((bf16[32,2,864]{2,1,0:T(2,128)(2,1)}), bf16[32,2,864]{2,1,0:T(2,128)(2,1)S(1)}, u32[]{:S(2)}, u32[]{:S(2)}) %all-to-all-start) | async-done | bytes 110624 | tf_op jit(solution)/shard_map/all_to_all | solution.py:74
  62.7 1.6 reshape.18
  64.3 2.0 %copy.51 = bf16[3,3,3,8,32,8]{3,4,5,2,1,0:T(8,128)(2,1)} copy(bf16[3,3,3,8,32,8]{3,2,1,0,5,4:T(4,128)(2,1)S(1)} %bitcast.42) | data formatting | bytes 221184 | tf_op jit(solution)/shard_map/all_to_all | solution.py:74
  66.3 3.4 %all_to_all.19 = bf16[3,3,3,256,8]{3,4,2,1,0:T(8,128)(2,1)S(1)} reshape(bf16[3,3,3,32,8,8]{4,3,5,2,1,0:T(8,128)(2,1)} %bitcast.44) | data formatting | bytes 221184 | tf_op jit(solution)/shard_map/all_to_all | solution.py:74
  69.8 36.7 %all-gather.2.cloned.1.call-done = bf16[2,4,64,8,256]{4,3,2,1,0:T(8,128)(2,1)} async-done(((bf16[2,4,4,8,256]{4,3,2,1,0:T(8,128)(2,1)}), bf16[2,4,64,8,256]{4,3,2,1,0:T(8,128)(2,1)}) %all-gather.2.cloned.1.call-update) | async-done | bytes 2097168 | tf_op jit(solution)/shard_map/all_gather | solution.py:73
  106.5 2.3 %fusion.61 = f32[2,4,64,8,216]{4,3,2,1,0:T(8,128)S(1)} fusion(bf16[2,4,64,8,256]{4,3,2,1,0:T(8,128)(2,1)} %all-gather.2.cloned.1.call-done, bf16[256,216,1,1,1]{0,1,4,3,2:T(8,128)(2,1)S(1)} %bitcast.47), kind=kOutput, calls=%fused_computation.121 | convolution fusion | flops 452984832 | bytes 5746688 | tf_op jit(solution)/shard_map/dot_general | solution.py:42
  108.8 3.4 %maximum_convert_fusion.1 = bf16[2,1,64,8,8]{4,3,2,1,0:T(8,128)(2,1)S(1)} fusion(f32[2,4,64,8,216]{4,3,2,1,0:T(8,128)S(1)} %fusion.61), kind=kLoop, calls=%fused_computation.107 | loop fusion | flops 229376 | bytes 5783552 | tf_op jit(solution)/shard_map/convert_element_type | solution.py:77
  112.2 3.5 %collective-permute-start.2 = (bf16[2,1,64,8,8]{4,3,2,1,0:T(8,128)(2,1)S(1)}, bf16[2,1,64,8,8]{4,3,2,1,0:T(8,128)(2,1)S(1)}, u32[]{:S(2)}, u32[]{:S(2)}) collective-permute-start(bf16[2,1,64,8,8]{4,3,2,1,0:T(8,128)(2,1)S(1)} %maximum_convert_fusion.1), channel_id=1, source_target_pairs={{0,32},{32,64},{64,96},{96,128},{128,160},{160,192},{192,224},{224... | collective-permute-start | bytes 49160 | tf_op jit(solution)/shard_map/ppermute | solution.py:23
  115.7 3.4 %maximum_convert_fusion = bf16[2,1,64,8,8]{4,3,2,1,0:T(8,128)(2,1)S(1)} fusion(f32[2,4,64,8,216]{4,3,2,1,0:T(8,128)S(1)} %fusion.61), kind=kLoop, calls=%fused_computation.106 | loop fusion | flops 229376 | bytes 5783552 | tf_op jit(solution)/shard_map/convert_element_type | solution.py:80
  119.2 1.9 %fusion.53 = f32[256,2,1,32,4]{0,1,4,3,2:T(2,128)S(1)} fusion(bf16[2,2,64,8,8]{4,3,2,1,0:T(8,128)(2,1)S(1)} %pad_maximum_fusion, bf16[3,3,3,8,256]{4,3,2,1,0:T(8,128)(2,1)S(1)} %copy-done), kind=kOutput, calls=%fused_computation.108 | convolution fusion | flops 17121280 | bytes 860160 | tf_op jit(solution)/shard_map/conv_general_dilated | solution.py:27
  121.1 2.8 %collective-permute-done.2 = bf16[2,1,64,8,8]{4,3,2,1,0:T(8,128)(2,1)S(1)} collective-permute-done((bf16[2,1,64,8,8]{4,3,2,1,0:T(8,128)(2,1)S(1)}, bf16[2,1,64,8,8]{4,3,2,1,0:T(8,128)(2,1)S(1)}, u32[]{:S(2)}, u32[]{:S(2)}) %collective-permute-start.2) | collective-permute-done | bytes 16416 | tf_op jit(solution)/shard_map/ppermute | solution.py:23
  125.0 1.9 %collective-permute-start.3 = (f32[16,8,2,1,32,4]{4,1,5,3,2,0:T(8,128)S(1)}, f32[16,8,2,1,32,4]{4,1,5,3,2,0:T(8,128)S(1)}, u32[]{:S(2)}, u32[]{:S(2)}) collective-permute-start(f32[16,8,2,1,32,4]{4,1,5,3,2,0:T(8,128)S(1)} %bitcast.46), channel_id=1, source_target_pairs={{0,1},{1,0},{2,3},{3,2},{4,5},{5,4},{6,7},{7,6},{8,9},{9,8},{10,11... | collective-permute-start | bytes 393224 | tf_op jit(solution)/shard_map/ppermute | solution.py:67
  126.9 1.9 %collective-permute-done.3 = f32[16,8,2,1,32,4]{4,1,5,3,2,0:T(8,128)S(1)} collective-permute-done((f32[16,8,2,1,32,4]{4,1,5,3,2,0:T(8,128)S(1)}, f32[16,8,2,1,32,4]{4,1,5,3,2,0:T(8,128)S(1)}, u32[]{:S(2)}, u32[]{:S(2)}) %collective-permute-start.3) | collective-permute-done | bytes 131104 | tf_op jit(solution)/shard_map/ppermute | solution.py:67
  129.2 22.5 %all_to_all.23 = f32[16,1,2048]{2,1,0:T(1,128)S(1)} all-to-all(f32[16,1,2048]{2,1,0:T(1,128)S(1)} %reshape.19), channel_id=1, replica_groups=mesh['col'=32,'z'=16,'core'=2] {'z'}, dimensions={0} | all-to-all | bytes 262144 | tf_op jit(solution)/shard_map/all_to_all | solution.py:68
  152.2 0.9 reduce.1
  (16 shorter events, 2.8 us)
Async XLA Ops:
  6.5 99.9 %all-gather.2.cloned.1.call-start = ((), (), s32[]{:S(2)}) async-start(), calls=%async_computation.2 | async-start | bytes 2228224 | tf_op jit(solution)/shard_map/all_gather | solution.py:73
  7.3 9.2 %collective-permute-start = (bf16[2,1,2,8,256]{4,3,2,1,0:T(8,128)(2,1)S(1)}, bf16[2,1,2,8,256]{4,3,2,1,0:T(8,128)(2,1)S(1)}, u32[]{:S(2)}, u32[]{:S(2)}) collective-permute-start(bf16[2,1,2,8,256]{4,3,2,1,0:T(8,128)(2,1)S(1)} %get-tuple-element.9), channel_id=1, source_target_pairs={{0,32},{32,64},{64,96},{96,128},{128,160},{160,192},{192,224},{224... | collective-permute-start | bytes 49160 | tf_op jit(solution)/shard_map/ppermute | solution.py:12
  10.7 7.2 %collective-permute-start.1 = (bf16[2,1,2,8,256]{4,3,2,1,0:T(8,128)(2,1)S(1)}, bf16[2,1,2,8,256]{4,3,2,1,0:T(8,128)(2,1)S(1)}, u32[]{:S(2)}, u32[]{:S(2)}) collective-permute-start(bf16[2,1,2,8,256]{4,3,2,1,0:T(8,128)(2,1)S(1)} %get-tuple-element.10), channel_id=1, source_target_pairs={{32,0},{64,32},{96,64},{128,96},{160,128},{192,160},{224,192},{256... | collective-permute-start | bytes 49160 | tf_op jit(solution)/shard_map/ppermute | solution.py:15
  26.5 36.1 %all-to-all-start = ((bf16[32,2,864]{2,1,0:T(2,128)(2,1)}), bf16[32,2,864]{2,1,0:T(2,128)(2,1)S(1)}, u32[]{:S(2)}, u32[]{:S(2)}) async-start(bf16[32,2,864]{2,1,0:T(2,128)(2,1)} %reshape.17), calls=%async_computation | async-start | bytes 229376 | tf_op jit(solution)/shard_map/all_to_all | solution.py:74
  112.2 7.0 %copy-start = (bf16[3,3,3,8,256]{4,3,2,1,0:T(8,128)(2,1)S(1)}, bf16[3,3,3,8,256]{4,3,2,1,0:T(8,128)(2,1)}, u32[]{:S(2)}) copy-start(bf16[3,3,3,8,256]{4,3,2,1,0:T(8,128)(2,1)} %param.5) | copy-start | bytes 331780
  112.2 11.7 %collective-permute-start.2 = (bf16[2,1,64,8,8]{4,3,2,1,0:T(8,128)(2,1)S(1)}, bf16[2,1,64,8,8]{4,3,2,1,0:T(8,128)(2,1)S(1)}, u32[]{:S(2)}, u32[]{:S(2)}) collective-permute-start(bf16[2,1,64,8,8]{4,3,2,1,0:T(8,128)(2,1)S(1)} %maximum_convert_fusion.1), channel_id=1, source_target_pairs={{0,32},{32,64},{64,96},{96,128},{128,160},{160,192},{192,224},{224... | collective-permute-start | bytes 49160 | tf_op jit(solution)/shard_map/ppermute | solution.py:23
  125.0 3.8 %collective-permute-start.3 = (f32[16,8,2,1,32,4]{4,1,5,3,2,0:T(8,128)S(1)}, f32[16,8,2,1,32,4]{4,1,5,3,2,0:T(8,128)S(1)}, u32[]{:S(2)}, u32[]{:S(2)}) collective-permute-start(f32[16,8,2,1,32,4]{4,1,5,3,2,0:T(8,128)S(1)} %bitcast.46), channel_id=1, source_target_pairs={{0,1},{1,0},{2,3},{3,2},{4,5},{5,4},{6,7},{7,6},{8,9},{9,8},{10,11... | collective-permute-start | bytes 393224 | tf_op jit(solution)/shard_map/ppermute | solution.py:67
Sparse Core Ops, SparseCore 0:
  20.8 85.6 all-gather.1

commit v11 on v10

--- a/solution.py
+++ b/solution.py
@@ -59,13 +59,9 @@
 
 
 def reduce_scattered(partial):
-    chips = lax.axis_size("z")
-    mine = lax.axis_index("core")
-    blocks = partial.reshape((chips, 2, partial.shape[0] // (2 * chips)) + partial.shape[1:])
-    keep = lax.dynamic_index_in_dim(blocks, mine, axis=1, keepdims=False)
-    give = lax.dynamic_index_in_dim(blocks, 1 - mine, axis=1, keepdims=False)
-    half = keep + lax.ppermute(give, "core", [(0, 1), (1, 0)])
-    return lax.all_to_all(half, "z", 0, 0, tiled=True).sum(axis=0)
+    peers = lax.axis_size(("z", "core"))
+    blocks = partial.reshape((peers, partial.shape[0] // peers) + partial.shape[1:])
+    return lax.all_to_all(blocks, ("z", "core"), 0, 0, tiled=True).sum(axis=0)
 
 
 def per_device(inputs, first_filters, second_filters):

time: 162 us -> 166 us (1.025)
  blocking collectives: 24.6 us -> 68.6 us
  starting transfers between devices: 33.7 us -> 12.1 us
  waiting for transfers between devices: 59.8 us -> 42.1 us
    all_to_all x1 -> x2, blocking collectives: 22.5 us -> 66.5 us  [the longest x1 35.8 us: per_device(): lax.all_to_all(first_filters, ('z', 'core'), split_axis=4, concat_axis=3,...]
    all_to_all x1 -> x0, starting transfers between devices: 19.2 us -> none  [per_device(): lax.all_to_all(first_filters, ('z', 'core'), split_axis=4, concat_axis=3,...]
    all_to_all x1 -> x0, waiting for transfers between devices: 17 us -> none  [per_device(): lax.all_to_all(first_filters, ('z', 'core'), split_axis=4, concat_axis=3,...]
    ppermute x1 -> x0, starting transfers between devices: 1.92 us -> none  [reduce_scattered(): half = keep + lax.ppermute(give, 'core', [(0, 1), (1, 0)])]
    ppermute x1 -> x0, waiting for transfers between devices: 1.88 us -> none  [reduce_scattered(): half = keep + lax.ppermute(give, 'core', [(0, 1), (1, 0)])]
    unnamed x7 -> x8, local copies, waits for them, and re-layouts: 7.87 us -> 7.62 us
  transfers between devices with their start and end apart: 6 -> 4, of which waited for: 5 -> 3; matrix products, arithmetic and copies ran while one was open for 9% -> 9% of each run, Pallas kernels for 0% -> 0%
where the time goes in v11:
time: 166 us; the launch traced here: 165 us
  blocking collectives  68.6 us (41%)
  waiting for transfers between devices  42.1 us (25%)
  local copies, waits for them, and re-layouts  14.7 us (9%)
  between operations  13.5 us (8%)
  starting transfers between devices  12.1 us (7%)
  other arithmetic  9.64 us (6%)
  matrix products  4.8 us (3%)
    all_gather x1, waiting for transfers between devices, per_device(): lax.all_gather(lax.all_gather(padded, 'core', axis=2, tiled=True), 'z', a...  37.3 us
    all_to_all x1, blocking collectives, per_device(): lax.all_to_all(first_filters, ('z', 'core'), split_axis=4, concat_axis=3,...  35.8 us
    all_to_all x1, blocking collectives, reduce_scattered(): return lax.all_to_all(blocks, ('z', 'core'), 0, 0, tiled=True).sum(axis=0)  30.7 us
    unnamed x8, local copies, waits for them, and re-layouts  7.62 us
    ppermute x1, starting transfers between devices, extended(): lax.ppermute(lax.slice_in_dim(block, 0, width, axis=dim), axis, backward)  5.76 us
    all_to_all x2, local copies, waits for them, and re-layouts, per_device(): lax.all_to_all(first_filters, ('z', 'core'), split_axis=4, concat_axis=3,...  5.52 us
    convert_element_type x1, other arithmetic, per_device(): jnp.maximum(tap_sum(products, own_first, 1, rows, cols), 0.0)  3.4 us
    convert_element_type x1, other arithmetic, per_device(): jnp.maximum(tap_sum(products, own_first, 0, rows, cols), 0.0)  3.4 us
  transfers between devices with their start and end apart: 4, of which 3 were waited for; matrix products, arithmetic and copies ran while one was open for 9% of the time, Pallas kernels for 0%

profile of v11, /device:TPU:32, one launch (start us, length us, event | category | flops | bytes accessed | tf_op | source)
XLA Modules:
  0.0 165.4 jit_solution(5280977403342014579)
XLA Ops:
  6.5 0.7 fusion.58
  7.3 3.4 %collective-permute-start = (bf16[2,1,2,8,256]{4,3,2,1,0:T(8,128)(2,1)S(1)}, bf16[2,1,2,8,256]{4,3,2,1,0:T(8,128)(2,1)S(1)}, u32[]{:S(2)}, u32[]{:S(2)}) collective-permute-start(bf16[2,1,2,8,256]{4,3,2,1,0:T(8,128)(2,1)S(1)} %get-tuple-element.7), channel_id=1, source_target_pairs={{0,32},{32,64},{64,96},{96,128},{128,160},{160,192},{192,224},{224... | collective-permute-start | bytes 49160 | tf_op jit(solution)/shard_map/ppermute | solution.py:12
  10.7 5.8 %collective-permute-start.1 = (bf16[2,1,2,8,256]{4,3,2,1,0:T(8,128)(2,1)S(1)}, bf16[2,1,2,8,256]{4,3,2,1,0:T(8,128)(2,1)S(1)}, u32[]{:S(2)}, u32[]{:S(2)}) collective-permute-start(bf16[2,1,2,8,256]{4,3,2,1,0:T(8,128)(2,1)S(1)} %get-tuple-element.8), channel_id=1, source_target_pairs={{32,0},{64,32},{96,64},{128,96},{160,128},{192,160},{224,192},{256... | collective-permute-start | bytes 49160 | tf_op jit(solution)/shard_map/ppermute | solution.py:15
  16.5 1.4 collective-permute-done.1
  17.9 0.8 pad_maximum_fusion.1
  18.6 2.0 %all_gather.6 = bf16[2,4,4,8,256]{4,3,2,1,0:T(8,128)(2,1)} all-gather(bf16[2,4,2,8,256]{4,3,2,1,0:T(8,128)(2,1)S(1)} %pad_maximum_fusion.1), channel_id=1, replica_groups=mesh['col'=32,'z'=16,'core'=2] {'core'}, dimensions={2}, use_global_device_ids=true | all-gather | bytes 196608 | tf_op jit(solution)/shard_map/all_gather | solution.py:69
  20.7 3.3 %copy.20 = bf16[3,3,3,8,256]{3,2,1,0,4:T(4,128)(2,1)S(1)} copy(bf16[3,3,3,8,256]{4,3,2,1,0:T(8,128)(2,1)} %param.4) | data formatting | bytes 221184 | tf_op args[1]
  24.0 1.7 %reshape.17 = bf16[32,2,864]{2,1,0:T(2,128)(2,1)S(1)} reshape(bf16[256,3,3,3,8]{4,3,2,1,0:T(4,128)(2,1)S(1)} %bitcast.32) | data formatting | bytes 221184
  25.8 35.8 %all_to_all.23 = bf16[32,2,864]{2,1,0:T(2,128)(2,1)S(1)} all-to-all(bf16[32,2,864]{2,1,0:T(2,128)(2,1)S(1)} %reshape.17), channel_id=1, replica_groups=mesh['col'=32,'z'=16,'core'=2] {'z','core'}, dimensions={0} | all-to-all | bytes 221184 | tf_op jit(solution)/shard_map/all_to_all | solution.py:70
  61.6 1.6 reshape.18
  63.2 2.1 %copy.36 = bf16[3,3,3,8,32,8]{3,4,5,2,1,0:T(8,128)(2,1)} copy(bf16[3,3,3,8,32,8]{3,2,1,0,5,4:T(4,128)(2,1)S(1)} %bitcast.31) | data formatting | bytes 221184 | tf_op jit(solution)/shard_map/all_to_all | solution.py:70
  65.3 3.5 %all_to_all.19 = bf16[3,3,3,256,8]{3,4,2,1,0:T(8,128)(2,1)S(1)} reshape(bf16[3,3,3,32,8,8]{4,3,5,2,1,0:T(8,128)(2,1)} %bitcast.33) | data formatting | bytes 221184 | tf_op jit(solution)/shard_map/all_to_all | solution.py:70
  68.7 37.3 %all-gather.2.cloned.1.call-done = bf16[2,4,64,8,256]{4,3,2,1,0:T(8,128)(2,1)} async-done(((bf16[2,4,4,8,256]{4,3,2,1,0:T(8,128)(2,1)}), bf16[2,4,64,8,256]{4,3,2,1,0:T(8,128)(2,1)}) %all-gather.2.cloned.1.call-update) | async-done | bytes 2097168 | tf_op jit(solution)/shard_map/all_gather | solution.py:69
  106.0 2.3 %fusion.59 = f32[2,4,64,8,216]{4,3,2,1,0:T(8,128)S(1)} fusion(bf16[2,4,64,8,256]{4,3,2,1,0:T(8,128)(2,1)} %all-gather.2.cloned.1.call-done, bf16[256,216,1,1,1]{0,1,4,3,2:T(8,128)(2,1)S(1)} %bitcast.34), kind=kOutput, calls=%fused_computation.116 | convolution fusion | flops 452984832 | bytes 5746688 | tf_op jit(solution)/shard_map/dot_general | solution.py:42
  108.4 3.4 %maximum_convert_fusion.1 = bf16[2,1,64,8,8]{4,3,2,1,0:T(8,128)(2,1)S(1)} fusion(f32[2,4,64,8,216]{4,3,2,1,0:T(8,128)S(1)} %fusion.59), kind=kLoop, calls=%fused_computation.104 | loop fusion | flops 229376 | bytes 5783552 | tf_op jit(solution)/shard_map/convert_element_type | solution.py:73
  111.8 2.9 %collective-permute-start.2 = (bf16[2,1,64,8,8]{4,3,2,1,0:T(8,128)(2,1)S(1)}, bf16[2,1,64,8,8]{4,3,2,1,0:T(8,128)(2,1)S(1)}, u32[]{:S(2)}, u32[]{:S(2)}) collective-permute-start(bf16[2,1,64,8,8]{4,3,2,1,0:T(8,128)(2,1)S(1)} %maximum_convert_fusion.1), channel_id=1, source_target_pairs={{0,32},{32,64},{64,96},{96,128},{128,160},{160,192},{192,224},{224... | collective-permute-start | bytes 49160 | tf_op jit(solution)/shard_map/ppermute | solution.py:23
  114.7 3.4 %maximum_convert_fusion = bf16[2,1,64,8,8]{4,3,2,1,0:T(8,128)(2,1)S(1)} fusion(f32[2,4,64,8,216]{4,3,2,1,0:T(8,128)S(1)} %fusion.59), kind=kLoop, calls=%fused_computation.103 | loop fusion | flops 229376 | bytes 5783552 | tf_op jit(solution)/shard_map/convert_element_type | solution.py:76
  118.2 1.9 %fusion.52 = f32[256,2,1,32,4]{0,1,4,3,2:T(2,128)S(1)} fusion(bf16[2,2,64,8,8]{4,3,2,1,0:T(8,128)(2,1)S(1)} %pad_maximum_fusion, bf16[3,3,3,8,256]{4,3,2,1,0:T(8,128)(2,1)S(1)} %copy-done), kind=kOutput, calls=%fused_computation.105 | convolution fusion | flops 17121280 | bytes 860160 | tf_op jit(solution)/shard_map/conv_general_dilated | solution.py:27
  120.1 3.4 %collective-permute-done.2 = bf16[2,1,64,8,8]{4,3,2,1,0:T(8,128)(2,1)S(1)} collective-permute-done((bf16[2,1,64,8,8]{4,3,2,1,0:T(8,128)(2,1)S(1)}, bf16[2,1,64,8,8]{4,3,2,1,0:T(8,128)(2,1)S(1)}, u32[]{:S(2)}, u32[]{:S(2)}) %collective-permute-start.2) | collective-permute-done | bytes 16416 | tf_op jit(solution)/shard_map/ppermute | solution.py:23
  123.5 0.6 convolution_add_fusion
  125.0 30.7 %all_to_all.24 = f32[32,1,2048]{2,1,0:T(1,128)S(1)} all-to-all(f32[32,1,2048]{2,1,0:T(1,128)S(1)} %reshape.19), channel_id=1, replica_groups=mesh['col'=32,'z'=16,'core'=2] {'z','core'}, dimensions={0} | all-to-all | bytes 524288 | tf_op jit(solution)/shard_map/all_to_all | solution.py:64
  155.8 0.5 broadcast.14
  156.3 1.3 reduce.1
  158.0 0.6 fusion.57
  (11 shorter events, 1.5 us)
Async XLA Ops:
  6.5 99.5 %all-gather.2.cloned.1.call-start = ((), (), s32[]{:S(2)}) async-start(), calls=%async_computation.2 | async-start | bytes 2228224 | tf_op jit(solution)/shard_map/all_gather | solution.py:69
  7.3 9.2 %collective-permute-start = (bf16[2,1,2,8,256]{4,3,2,1,0:T(8,128)(2,1)S(1)}, bf16[2,1,2,8,256]{4,3,2,1,0:T(8,128)(2,1)S(1)}, u32[]{:S(2)}, u32[]{:S(2)}) collective-permute-start(bf16[2,1,2,8,256]{4,3,2,1,0:T(8,128)(2,1)S(1)} %get-tuple-element.7), channel_id=1, source_target_pairs={{0,32},{32,64},{64,96},{96,128},{128,160},{160,192},{192,224},{224... | collective-permute-start | bytes 49160 | tf_op jit(solution)/shard_map/ppermute | solution.py:12
  10.7 7.2 %collective-permute-start.1 = (bf16[2,1,2,8,256]{4,3,2,1,0:T(8,128)(2,1)S(1)}, bf16[2,1,2,8,256]{4,3,2,1,0:T(8,128)(2,1)S(1)}, u32[]{:S(2)}, u32[]{:S(2)}) collective-permute-start(bf16[2,1,2,8,256]{4,3,2,1,0:T(8,128)(2,1)S(1)} %get-tuple-element.8), channel_id=1, source_target_pairs={{32,0},{64,32},{96,64},{128,96},{160,128},{192,160},{224,192},{256... | collective-permute-start | bytes 49160 | tf_op jit(solution)/shard_map/ppermute | solution.py:15
  111.8 6.5 %copy-start = (bf16[3,3,3,8,256]{4,3,2,1,0:T(8,128)(2,1)S(1)}, bf16[3,3,3,8,256]{4,3,2,1,0:T(8,128)(2,1)}, u32[]{:S(2)}) copy-start(bf16[3,3,3,8,256]{4,3,2,1,0:T(8,128)(2,1)} %param.5) | copy-start | bytes 331780
  111.8 11.7 %collective-permute-start.2 = (bf16[2,1,64,8,8]{4,3,2,1,0:T(8,128)(2,1)S(1)}, bf16[2,1,64,8,8]{4,3,2,1,0:T(8,128)(2,1)S(1)}, u32[]{:S(2)}, u32[]{:S(2)}) collective-permute-start(bf16[2,1,64,8,8]{4,3,2,1,0:T(8,128)(2,1)S(1)} %maximum_convert_fusion.1), channel_id=1, source_target_pairs={{0,32},{32,64},{64,96},{96,128},{128,160},{160,192},{192,224},{224... | collective-permute-start | bytes 49160 | tf_op jit(solution)/shard_map/ppermute | solution.py:23
Sparse Core Ops, SparseCore 0:
  20.8 85.1 all-gather.1

commit v12 on v10

--- a/solution.py
+++ b/solution.py
@@ -70,7 +70,7 @@
 
 def per_device(inputs, first_filters, second_filters):
     padded = extended(inputs, (("col", 1),), 1)
-    gathered = lax.all_gather(lax.all_gather(padded, "core", axis=2, tiled=True), "z", axis=2, tiled=True)
+    gathered = lax.all_gather(padded, ("z", "core"), axis=2, tiled=True)
     own_first = lax.all_to_all(first_filters, ("z", "core"), split_axis=4, concat_axis=3, tiled=True)
     products = convolve_by_taps(gathered, own_first)
     rows, cols = gathered.shape[2], gathered.shape[3]

time: 162 us -> 160 us (0.988)
  blocking collectives: 24.6 us -> 22.3 us
    all_gather x1 -> x0, blocking collectives: 2.03 us -> none  [per_device(): lax.all_gather(padded, 'core', axis=2, tiled=True)]
    all_gather x1, waiting for transfers between devices: 36.7 us -> 34.8 us  [per_device(): gathered = lax.all_gather(padded, ('z', 'core'), axis=2, tiled=True)]
    ppermute x1, waiting for transfers between devices: 2.79 us -> 4.63 us  [passed_along(): return lax.ppermute(array, axis, pairs)]
where the time goes in v12:
time: 160 us; the launch traced here: 159 us
  waiting for transfers between devices  59.7 us (37%)
  starting transfers between devices  33.9 us (21%)
  blocking collectives  22.3 us (14%)
  local copies, waits for them, and re-layouts  15.1 us (9%)
  between operations  13.6 us (8%)
  other arithmetic  9.98 us (6%)
  matrix products  4.79 us (3%)
    all_gather x1, waiting for transfers between devices, per_device(): gathered = lax.all_gather(padded, ('z', 'core'), axis=2, tiled=True)  34.8 us
    all_to_all x1, blocking collectives, reduce_scattered(): return lax.all_to_all(half, 'z', 0, 0, tiled=True).sum(axis=0)  22.3 us
    all_to_all x1, starting transfers between devices, per_device(): lax.all_to_all(first_filters, ('z', 'core'), split_axis=4, concat_axis=3,...  19.2 us
    all_to_all x1, waiting for transfers between devices, per_device(): lax.all_to_all(first_filters, ('z', 'core'), split_axis=4, concat_axis=3,...  17 us
    unnamed x7, local copies, waits for them, and re-layouts  7.87 us
    ppermute x1, starting transfers between devices, extended(): lax.ppermute(lax.slice_in_dim(block, 0, width, axis=dim), axis, backward)  5.76 us
    all_to_all x2, local copies, waits for them, and re-layouts, per_device(): lax.all_to_all(first_filters, ('z', 'core'), split_axis=4, concat_axis=3,...  5.48 us
    ppermute x1, waiting for transfers between devices, passed_along(): return lax.ppermute(array, axis, pairs)  4.63 us
  transfers between devices with their start and end apart: 6, of which 5 were waited for; matrix products, arithmetic and copies ran while one was open for 9% of the time, Pallas kernels for 0%

profile of v12, /device:TPU:32, one launch (start us, length us, event | category | flops | bytes accessed | tf_op | source)
XLA Modules:
  0.0 159.3 jit_solution(5902331594184103425)
XLA Ops:
  6.5 0.7 fusion.59
  7.3 3.4 %collective-permute-start = (bf16[2,1,2,8,256]{4,3,2,1,0:T(8,128)(2,1)S(1)}, bf16[2,1,2,8,256]{4,3,2,1,0:T(8,128)(2,1)S(1)}, u32[]{:S(2)}, u32[]{:S(2)}) collective-permute-start(bf16[2,1,2,8,256]{4,3,2,1,0:T(8,128)(2,1)S(1)} %get-tuple-element.9), channel_id=1, source_target_pairs={{0,32},{32,64},{64,96},{96,128},{128,160},{160,192},{192,224},{224... | collective-permute-start | bytes 49160 | tf_op jit(solution)/shard_map/ppermute | solution.py:12
  10.7 5.8 %collective-permute-start.1 = (bf16[2,1,2,8,256]{4,3,2,1,0:T(8,128)(2,1)S(1)}, bf16[2,1,2,8,256]{4,3,2,1,0:T(8,128)(2,1)S(1)}, u32[]{:S(2)}, u32[]{:S(2)}) collective-permute-start(bf16[2,1,2,8,256]{4,3,2,1,0:T(8,128)(2,1)S(1)} %get-tuple-element.10), channel_id=1, source_target_pairs={{32,0},{64,32},{96,64},{128,96},{160,128},{192,160},{224,192},{256... | collective-permute-start | bytes 49160 | tf_op jit(solution)/shard_map/ppermute | solution.py:15
  16.5 1.4 collective-permute-done.1
  17.9 1.4 pad_maximum_fusion.1
  19.3 3.3 %copy.30 = bf16[3,3,3,8,256]{3,2,1,0,4:T(4,128)(2,1)S(1)} copy(bf16[3,3,3,8,256]{4,3,2,1,0:T(8,128)(2,1)} %param.4) | data formatting | bytes 221184 | tf_op args[1]
  22.6 2.5 %reshape.17 = bf16[32,2,864]{2,1,0:T(2,128)(2,1)} reshape(bf16[256,3,3,3,8]{4,3,2,1,0:T(4,128)(2,1)S(1)} %bitcast.43) | data formatting | bytes 221184
  25.1 19.2 %all-to-all-start = ((bf16[32,2,864]{2,1,0:T(2,128)(2,1)}), bf16[32,2,864]{2,1,0:T(2,128)(2,1)S(1)}, u32[]{:S(2)}, u32[]{:S(2)}) async-start(bf16[32,2,864]{2,1,0:T(2,128)(2,1)} %reshape.17), calls=%async_computation | async-start | bytes 229376 | tf_op jit(solution)/shard_map/all_to_all | solution.py:74
  44.3 17.0 %all-to-all-done = bf16[32,2,864]{2,1,0:T(2,128)(2,1)S(1)} async-done(((bf16[32,2,864]{2,1,0:T(2,128)(2,1)}), bf16[32,2,864]{2,1,0:T(2,128)(2,1)S(1)}, u32[]{:S(2)}, u32[]{:S(2)}) %all-to-all-start) | async-done | bytes 110624 | tf_op jit(solution)/shard_map/all_to_all | solution.py:74
  61.3 1.6 %reshape.18 = bf16[256,3,3,3,8]{4,3,2,1,0:T(4,128)(2,1)S(1)} reshape(bf16[32,2,864]{2,1,0:T(2,128)(2,1)S(1)} %all-to-all-done) | data formatting | bytes 221184
  62.9 2.0 %copy.51 = bf16[3,3,3,8,32,8]{3,4,5,2,1,0:T(8,128)(2,1)} copy(bf16[3,3,3,8,32,8]{3,2,1,0,5,4:T(4,128)(2,1)S(1)} %bitcast.42) | data formatting | bytes 221184 | tf_op jit(solution)/shard_map/all_to_all | solution.py:74
  65.0 3.4 %all_to_all.19 = bf16[3,3,3,256,8]{3,4,2,1,0:T(8,128)(2,1)S(1)} reshape(bf16[3,3,3,32,8,8]{4,3,5,2,1,0:T(8,128)(2,1)} %bitcast.44) | data formatting | bytes 221184 | tf_op jit(solution)/shard_map/all_to_all | solution.py:74
  68.4 34.8 %all-gather.2.cloned.1.call-done = bf16[2,4,64,8,256]{4,3,2,1,0:T(8,128)(2,1)} async-done(((bf16[2,4,2,8,256]{4,3,2,1,0:T(8,128)(2,1)}), bf16[2,4,64,8,256]{4,3,2,1,0:T(8,128)(2,1)}) %all-gather.2.cloned.1.call-update) | async-done | bytes 2097168 | tf_op jit(solution)/shard_map/all_gather | solution.py:73
  103.2 2.3 %fusion.61 = f32[2,4,64,8,216]{4,3,2,1,0:T(8,128)S(1)} fusion(bf16[2,4,64,8,256]{4,3,2,1,0:T(8,128)(2,1)} %all-gather.2.cloned.1.call-done, bf16[256,216,1,1,1]{0,1,4,3,2:T(8,128)(2,1)S(1)} %bitcast.47), kind=kOutput, calls=%fused_computation.121 | convolution fusion | flops 452984832 | bytes 5746688 | tf_op jit(solution)/shard_map/dot_general | solution.py:42
  105.5 3.4 %maximum_convert_fusion.1 = bf16[2,1,64,8,8]{4,3,2,1,0:T(8,128)(2,1)S(1)} fusion(f32[2,4,64,8,216]{4,3,2,1,0:T(8,128)S(1)} %fusion.61), kind=kLoop, calls=%fused_computation.107 | loop fusion | flops 229376 | bytes 5783552 | tf_op jit(solution)/shard_map/convert_element_type | solution.py:77
  108.9 3.7 %collective-permute-start.2 = (bf16[2,1,64,8,8]{4,3,2,1,0:T(8,128)(2,1)S(1)}, bf16[2,1,64,8,8]{4,3,2,1,0:T(8,128)(2,1)S(1)}, u32[]{:S(2)}, u32[]{:S(2)}) collective-permute-start(bf16[2,1,64,8,8]{4,3,2,1,0:T(8,128)(2,1)S(1)} %maximum_convert_fusion.1), channel_id=1, source_target_pairs={{0,32},{32,64},{64,96},{96,128},{128,160},{160,192},{192,224},{224... | collective-permute-start | bytes 49160 | tf_op jit(solution)/shard_map/ppermute | solution.py:23
  112.6 3.4 %maximum_convert_fusion = bf16[2,1,64,8,8]{4,3,2,1,0:T(8,128)(2,1)S(1)} fusion(f32[2,4,64,8,216]{4,3,2,1,0:T(8,128)S(1)} %fusion.61), kind=kLoop, calls=%fused_computation.106 | loop fusion | flops 229376 | bytes 5783552 | tf_op jit(solution)/shard_map/convert_element_type | solution.py:80
  116.2 1.9 %fusion.53 = f32[256,2,1,32,4]{0,1,4,3,2:T(2,128)S(1)} fusion(bf16[2,2,64,8,8]{4,3,2,1,0:T(8,128)(2,1)S(1)} %pad_maximum_fusion, bf16[3,3,3,8,256]{4,3,2,1,0:T(8,128)(2,1)S(1)} %copy-done), kind=kOutput, calls=%fused_computation.108 | convolution fusion | flops 17121280 | bytes 860160 | tf_op jit(solution)/shard_map/conv_general_dilated | solution.py:27
  118.1 4.6 %collective-permute-done.2 = bf16[2,1,64,8,8]{4,3,2,1,0:T(8,128)(2,1)S(1)} collective-permute-done((bf16[2,1,64,8,8]{4,3,2,1,0:T(8,128)(2,1)S(1)}, bf16[2,1,64,8,8]{4,3,2,1,0:T(8,128)(2,1)S(1)}, u32[]{:S(2)}, u32[]{:S(2)}) %collective-permute-start.2) | collective-permute-done | bytes 16416 | tf_op jit(solution)/shard_map/ppermute | solution.py:23
  123.8 1.9 %collective-permute-start.3 = (f32[16,8,2,1,32,4]{4,1,5,3,2,0:T(8,128)S(1)}, f32[16,8,2,1,32,4]{4,1,5,3,2,0:T(8,128)S(1)}, u32[]{:S(2)}, u32[]{:S(2)}) collective-permute-start(f32[16,8,2,1,32,4]{4,1,5,3,2,0:T(8,128)S(1)} %bitcast.46), channel_id=1, source_target_pairs={{0,1},{1,0},{2,3},{3,2},{4,5},{5,4},{6,7},{7,6},{8,9},{9,8},{10,11... | collective-permute-start | bytes 393224 | tf_op jit(solution)/shard_map/ppermute | solution.py:67
  125.7 1.9 %collective-permute-done.3 = f32[16,8,2,1,32,4]{4,1,5,3,2,0:T(8,128)S(1)} collective-permute-done((f32[16,8,2,1,32,4]{4,1,5,3,2,0:T(8,128)S(1)}, f32[16,8,2,1,32,4]{4,1,5,3,2,0:T(8,128)S(1)}, u32[]{:S(2)}, u32[]{:S(2)}) %collective-permute-start.3) | collective-permute-done | bytes 131104 | tf_op jit(solution)/shard_map/ppermute | solution.py:67
  127.9 22.3 %all_to_all.23 = f32[16,1,2048]{2,1,0:T(1,128)S(1)} all-to-all(f32[16,1,2048]{2,1,0:T(1,128)S(1)} %reshape.19), channel_id=1, replica_groups=mesh['col'=32,'z'=16,'core'=2] {'z'}, dimensions={0} | all-to-all | bytes 262144 | tf_op jit(solution)/shard_map/all_to_all | solution.py:68
  150.7 0.9 reduce.1
  151.8 0.6 fusion.58
  (15 shorter events, 2.2 us)
Async XLA Ops:
  6.5 96.6 %all-gather.2.cloned.1.call-start = ((), (), s32[]{:S(2)}) async-start(), calls=%async_computation.2 | async-start | bytes 2162688 | tf_op jit(solution)/shard_map/all_gather | solution.py:73
  7.3 9.2 %collective-permute-start = (bf16[2,1,2,8,256]{4,3,2,1,0:T(8,128)(2,1)S(1)}, bf16[2,1,2,8,256]{4,3,2,1,0:T(8,128)(2,1)S(1)}, u32[]{:S(2)}, u32[]{:S(2)}) collective-permute-start(bf16[2,1,2,8,256]{4,3,2,1,0:T(8,128)(2,1)S(1)} %get-tuple-element.9), channel_id=1, source_target_pairs={{0,32},{32,64},{64,96},{96,128},{128,160},{160,192},{192,224},{224... | collective-permute-start | bytes 49160 | tf_op jit(solution)/shard_map/ppermute | solution.py:12
  10.7 7.2 %collective-permute-start.1 = (bf16[2,1,2,8,256]{4,3,2,1,0:T(8,128)(2,1)S(1)}, bf16[2,1,2,8,256]{4,3,2,1,0:T(8,128)(2,1)S(1)}, u32[]{:S(2)}, u32[]{:S(2)}) collective-permute-start(bf16[2,1,2,8,256]{4,3,2,1,0:T(8,128)(2,1)S(1)} %get-tuple-element.10), channel_id=1, source_target_pairs={{32,0},{64,32},{96,64},{128,96},{160,128},{192,160},{224,192},{256... | collective-permute-start | bytes 49160 | tf_op jit(solution)/shard_map/ppermute | solution.py:15
  25.1 36.2 %all-to-all-start = ((bf16[32,2,864]{2,1,0:T(2,128)(2,1)}), bf16[32,2,864]{2,1,0:T(2,128)(2,1)S(1)}, u32[]{:S(2)}, u32[]{:S(2)}) async-start(bf16[32,2,864]{2,1,0:T(2,128)(2,1)} %reshape.17), calls=%async_computation | async-start | bytes 229376 | tf_op jit(solution)/shard_map/all_to_all | solution.py:74
  108.9 7.2 %copy-start = (bf16[3,3,3,8,256]{4,3,2,1,0:T(8,128)(2,1)S(1)}, bf16[3,3,3,8,256]{4,3,2,1,0:T(8,128)(2,1)}, u32[]{:S(2)}) copy-start(bf16[3,3,3,8,256]{4,3,2,1,0:T(8,128)(2,1)} %param.5) | copy-start | bytes 331780
  108.9 13.8 %collective-permute-start.2 = (bf16[2,1,64,8,8]{4,3,2,1,0:T(8,128)(2,1)S(1)}, bf16[2,1,64,8,8]{4,3,2,1,0:T(8,128)(2,1)S(1)}, u32[]{:S(2)}, u32[]{:S(2)}) collective-permute-start(bf16[2,1,64,8,8]{4,3,2,1,0:T(8,128)(2,1)S(1)} %maximum_convert_fusion.1), channel_id=1, source_target_pairs={{0,32},{32,64},{64,96},{96,128},{128,160},{160,192},{192,224},{224... | collective-permute-start | bytes 49160 | tf_op jit(solution)/shard_map/ppermute | solution.py:23
  123.8 3.8 %collective-permute-start.3 = (f32[16,8,2,1,32,4]{4,1,5,3,2,0:T(8,128)S(1)}, f32[16,8,2,1,32,4]{4,1,5,3,2,0:T(8,128)S(1)}, u32[]{:S(2)}, u32[]{:S(2)}) collective-permute-start(f32[16,8,2,1,32,4]{4,1,5,3,2,0:T(8,128)S(1)} %bitcast.46), channel_id=1, source_target_pairs={{0,1},{1,0},{2,3},{3,2},{4,5},{5,4},{6,7},{7,6},{8,9},{9,8},{10,11... | collective-permute-start | bytes 393224 | tf_op jit(solution)/shard_map/ppermute | solution.py:67
Sparse Core Ops, SparseCore 0:
  19.4 83.7 all-gather.1
